TPU v7x, 512 devices: a whole 4x4x16 slice. The times are simulated.
512 devices in a mesh: seq: 64 (over z_lo, x, core), dp: 8 (over y, z_hi).
Axes of the slice: x: 4, y: 4, z: 16 (z_hi: 2, z_lo: 8; z = z_hi * 8 + z_lo), core: 2. Of those that a mesh axis runs over, the one named last changes fastest.
Arguments:
- queries: bfloat16 [65536, 2048], P(('dp', 'seq')), parts along dimension 0, may hold values from -20 to 20
- keys: bfloat16 [65536, 2048], P(('dp', 'seq')), parts along dimension 0, may hold values from -20 to 20
- values: bfloat16 [65536, 2048], P(('dp', 'seq')), parts along dimension 0, may hold values from -48 to 48
- cotangent: bfloat16 [65536, 2048], P(('dp', 'seq')), parts along dimension 0, may hold values from -24 to 24
- documents: int32 [65536], P(('dp', 'seq')), parts along dimension 0, may hold values from 0 to 7, never falling along the last dimension, each value on 1 to 6144 neighbouring positions
- global_offsets: int32 [1024], P(('dp', 'seq')), parts along dimension 0, may hold values from 0 to 127
Outputs:
- attended: bfloat16 [65536, 2048], P(('dp', 'seq')), parts along dimension 0
- query_grad: bfloat16 [65536, 2048], P(('dp', 'seq')), parts along dimension 0
- key_grad: bfloat16 [65536, 2048], P(('dp', 'seq')), parts along dimension 0
- value_grad: bfloat16 [65536, 2048], P(('dp', 'seq')), parts along dimension 0
There are 8 independent parts, one for each index of `dp`. A program takes and returns all parts, laid end to end along the dimension named above; each array names one. Nothing has to cross between parts.
All inputs are finite; a program needn't handle non-finite values.
Results may differ from a plain program's by a relative error of at most 0.023.
Values may be sent and summed in bfloat16 or wider, within the bound.
No kernel may reach another device: no remote copies, remote signals or barrier semaphores. Data moves between devices by JAX's collectives and lax.ppermute only.
A program may use at most 64 MiB of HBM per device.

v0:
```python
import jax
import jax.numpy as jnp
from jax import lax
from jax.sharding import PartitionSpec as P

HEADS = 16
LEVELS = 2


def from_partner(array, axis, stride):
    return lax.ppermute(array, axis, [(i, i ^ 1 << stride) for i in range(lax.axis_size(axis))])


def local(queries, keys, values, cotangent, documents, global_offsets):
    rows_here, columns = queries.shape
    head_size = columns // HEADS
    temper = head_size ** (-0.5)
    shards = lax.axis_size("seq")
    myself = lax.axis_index("seq")
    log_shards = shards.bit_length() - 1
    level_bits = [step * (log_shards - 2) // (LEVELS - 1) for step in range(LEVELS)]

    def split(array):
        return array.reshape(array.shape[0], HEADS, head_size)

    every_doc = lax.all_gather(documents, "seq", axis=0, tiled=True)
    picked_keys = keys[global_offsets]
    picked_values = values[global_offsets]
    global_keys, global_values = (
        lax.all_gather(picked_keys, "seq", axis=0, tiled=True),
        lax.all_gather(picked_values, "seq", axis=0, tiled=True),
    )
    global_count = global_keys.shape[0]
    per_block = global_offsets.shape[0]
    owners = jnp.arange(global_count, dtype=jnp.int32) // per_block
    distance = owners ^ myself
    nearby = distance == 0
    for level_bit in level_bits:
        nearby = nearby | (distance == 1 << level_bit)
    query_heads = split(queries)
    dout_heads = split(cotangent)
    key_list = [keys]
    value_list = [values]
    mask_list = [documents[:, None] == documents[None, :]]
    for level_bit in level_bits:
        partner_keys, partner_values = from_partner((keys, values), "seq", level_bit)
        partner_docs = lax.dynamic_slice_in_dim(
            every_doc, (myself ^ 1 << level_bit) * rows_here, rows_here
        )
        key_list.append(partner_keys)
        value_list.append(partner_values)
        mask_list.append(documents[:, None] == partner_docs[None, :])
    block_keys = jnp.concatenate(key_list, 0)
    block_values = jnp.concatenate(value_list, 0)
    block_mask = jnp.concatenate(mask_list, 1)
    raw = (
        jnp.einsum(
            "thd,uhd->htu", query_heads, split(block_keys), preferred_element_type=jnp.float32
        )
        * temper
    )
    block_scores = jnp.where(block_mask[None], raw, -jnp.inf)
    global_raw = (
        jnp.einsum(
            "thd,ghd->htg", query_heads, split(global_keys), preferred_element_type=jnp.float32
        )
        * temper
    )
    global_scores = jnp.where(jnp.logical_not(nearby)[None, None, :], global_raw, -jnp.inf)
    highest = jnp.maximum(jnp.max(global_scores, axis=-1), jnp.max(block_scores, axis=-1))
    block_exp = jnp.exp(block_scores - highest[..., None])
    global_exp = jnp.exp(global_scores - highest[..., None])
    totals = jnp.sum(global_exp, axis=-1) + jnp.sum(block_exp, axis=-1)
    probs = block_exp / totals[..., None]
    global_prob = global_exp / totals[..., None]
    probs_b = probs.astype(jnp.bfloat16)
    global_prob_b = global_prob.astype(jnp.bfloat16)
    summed = jnp.einsum(
        "htg,ghd->thd", global_prob_b, split(global_values), preferred_element_type=jnp.float32
    )
    summed = summed + jnp.einsum(
        "htu,uhd->thd", probs_b, split(block_values), preferred_element_type=jnp.float32
    )
    attended = summed.astype(jnp.bfloat16).reshape(rows_here, columns)
    delta = jnp.sum(dout_heads.astype(jnp.float32) * split(attended).astype(jnp.float32), axis=-1).T
    product = jnp.einsum(
        "thd,uhd->htu", dout_heads, split(block_values), preferred_element_type=jnp.float32
    )
    slope = (probs * (product - delta[:, :, None])).astype(jnp.bfloat16)
    query_term = jnp.einsum(
        "htu,uhd->thd", slope, split(block_keys), preferred_element_type=jnp.float32
    )
    key_term = temper * jnp.einsum(
        "htu,thd->uhd", slope, query_heads, preferred_element_type=jnp.float32
    )
    value_term = jnp.einsum("htu,thd->uhd", probs_b, dout_heads, preferred_element_type=jnp.float32)
    query_sum = query_term
    key_sum = key_term[:rows_here]
    value_sum = value_term[:rows_here]
    for level, level_bit in enumerate(level_bits):
        lower = (level + 1) * rows_here
        upper = (level + 2) * rows_here
        back_keys, back_values = from_partner(
            (
                key_term[lower:upper].reshape(rows_here, columns).astype(jnp.bfloat16),
                value_term[lower:upper].reshape(rows_here, columns).astype(jnp.bfloat16),
            ),
            "seq",
            level_bit,
        )
        key_sum = key_sum + split(back_keys).astype(jnp.float32)
        value_sum = value_sum + split(back_values).astype(jnp.float32)
    global_product = jnp.einsum(
        "thd,ghd->htg", dout_heads, split(global_values), preferred_element_type=jnp.float32
    )
    global_slope = (global_prob * (global_product - delta[:, :, None])).astype(jnp.bfloat16)
    query_sum = query_sum + jnp.einsum(
        "htg,ghd->thd", global_slope, split(global_keys), preferred_element_type=jnp.float32
    )
    key_part = temper * jnp.einsum(
        "htg,thd->ghd", global_slope, query_heads, preferred_element_type=jnp.float32
    )
    value_part = jnp.einsum(
        "htg,thd->ghd", global_prob_b, dout_heads, preferred_element_type=jnp.float32
    )
    owned = lax.psum_scatter(
        jnp.concatenate(
            [
                key_part.reshape(per_block * lax.axis_size("seq"), columns),
                value_part.reshape(per_block * lax.axis_size("seq"), columns),
            ],
            1,
        ),
        "seq",
        scatter_dimension=0,
        tiled=True,
    )
    placement = (jnp.arange(rows_here, dtype=jnp.int32)[:, None] == global_offsets[None, :]).astype(
        jnp.float32
    )
    spread_rows = jnp.dot(
        placement, owned, precision=lax.Precision.HIGHEST, preferred_element_type=jnp.float32
    )
    key_grad = (key_sum.reshape(rows_here, columns) + spread_rows[:, :columns]).astype(jnp.bfloat16)
    value_grad = (value_sum.reshape(rows_here, columns) + spread_rows[:, columns:]).astype(
        jnp.bfloat16
    )
    query_grad = (temper * query_sum).reshape(rows_here, columns).astype(jnp.bfloat16)
    return (attended, query_grad, key_grad, value_grad)


def solution(mesh):
    in_specs = (
        P(("dp", "seq"), None),
        P(("dp", "seq"), None),
        P(("dp", "seq"), None),
        P(("dp", "seq"), None),
        P(("dp", "seq")),
        P(("dp", "seq")),
    )
    out_specs = (
        P(("dp", "seq"), None),
        P(("dp", "seq"), None),
        P(("dp", "seq"), None),
        P(("dp", "seq"), None),
    )
    return jax.shard_map(local, mesh=mesh, in_specs=in_specs, out_specs=out_specs, check_vma=False)
```

profile of v0, /device:TPU:24, one launch (start us, length us, event | category | flops | bytes accessed | tf_op | source)
XLA Modules:
  0.0 1264.0 jit_solution(16097213967234120717)
XLA Ops:
  8.6 5.2 collective-permute-start.1
  13.8 1.9 collective-permute-start
  15.7 1.9 collective-permute-start.3
  17.6 2.4 collective-permute-start.2
  20.7 1.7 gather_fusion
  22.4 1.7 gather_fusion.1
  24.1 129.2 %all-gather.2 = bf16[64,2,2048]{2,1,0:T(2,128)(2,1)S(1)} all-gather(bf16[1,2,2048]{2,1,0:T(2,128)(2,1)S(1)} %bitcast.117), channel_id=2, replica_groups=mesh['seq'=64,'dp'=8] {'seq'}, dimensions={0}, use_global_device_ids=true | all-gather | bytes 532480 | tf_op jit(solution)/shard_map/all_gather | solution.py:31
  153.3 113.8 %all-gather.3 = bf16[64,2,2048]{2,1,0:T(2,128)(2,1)S(1)} all-gather(bf16[1,2,2048]{2,1,0:T(2,128)(2,1)S(1)} %bitcast.116), channel_id=3, replica_groups=mesh['seq'=64,'dp'=8] {'seq'}, dimensions={0}, use_global_device_ids=true | all-gather | bytes 532480 | tf_op jit(solution)/shard_map/all_gather | solution.py:30
  267.1 114.1 %all-gather.4 = s32[64,1,128]{2,1,0:T(1,128)S(1)} all-gather(s32[1,1,128]{2,1,0:T(1,128)} %bitcast.118), channel_id=1, replica_groups=mesh['seq'=64,'dp'=8] {'seq'}, dimensions={0}, use_global_device_ids=true | all-gather | bytes 33280 | tf_op jit(solution)/shard_map/all_gather | solution.py:26
  382.1 2.0 copy.84
  394.1 2.5 pad_maximum_fusion.2
  396.7 2.7 copy.82
  399.3 2.0 fusion.23
  402.1 2.1 multiply_reduce_fusion
  404.7 2.6 fusion
  407.2 3.2 fusion.39
  411.9 2.0 copy.108
  415.4 2.6 copy.103
  418.0 3.0 pad_maximum_fusion
  421.1 2.4 fusion.35
  423.5 1.9 collective-permute-start.7
  425.4 2.3 collective-permute-start.6
  427.7 2.3 fusion.40
  431.1 4.7 collective-permute-start.5
  436.8 2.1 collective-permute-start.4
  440.2 2.0 fusion.12
  443.3 4.6 collective-permute-done.7
  447.9 1.7 fusion.16
  449.9 9.5 collective-permute-done.5
  460.9 2.4 fusion.18
  465.2 787.7 %all-reduce.3.cloned.1.call-done = f32[128,4096]{0,1:T(8,128)} async-done(((f32[128,4096]{0,1:T(8,128)}), f32[128,4096]{0,1:T(8,128)}) %all-reduce.3.cloned.1.call-update) | async-done | bytes 2097168
  1252.9 3.1 fusion.4
  (69 shorter events, 25.8 us)
Async XLA Ops:
  7.2 378.9 %copy-start.8 = (bf16[128,2048]{1,0:T(8,128)(2,1)S(1)}, bf16[128,2048]{1,0:T(8,128)(2,1)}, u32[]{:S(2)}) copy-start(bf16[128,2048]{1,0:T(8,128)(2,1)} %param.6) | copy-start | bytes 1572868
  7.2 1245.7 %all-reduce.3.cloned.1.call-start = ((), (), s32[]{:S(2)}) async-start(), calls=%async_computation | async-start | bytes 4194304
  8.6 380.2 %collective-permute-start.1 = (bf16[128,2048]{0,1:T(8,128)(2,1)S(1)}, bf16[128,2048]{0,1:T(8,128)(2,1)S(1)}, u32[]{:S(2)}, u32[]{:S(2)}) collective-permute-start(bf16[128,2048]{0,1:T(8,128)(2,1)S(1)} %copy.77), channel_id=1, source_target_pairs={{0,128},{8,136},{16,144},{24,152},{32,160},{40,168},{48,176},{56,1... | collective-permute-start | bytes 1572872 | tf_op jit(solution)/shard_map/ppermute | solution.py:11
  13.8 375.8 %collective-permute-start = (bf16[128,2048]{0,1:T(8,128)(2,1)S(1)}, bf16[128,2048]{0,1:T(8,128)(2,1)}, u32[]{:S(2)}, u32[]{:S(2)}) collective-permute-start(bf16[128,2048]{0,1:T(8,128)(2,1)S(1)} %copy.77), channel_id=1, source_target_pairs={{0,8},{8,0},{16,24},{24,16},{32,40},{40,32},{48,56},{56,48},{64,72... | collective-permute-start | bytes 1572872 | tf_op jit(solution)/shard_map/ppermute | solution.py:11
  15.7 378.4 %collective-permute-start.3 = (bf16[128,2048]{1,0:T(8,128)(2,1)}, bf16[128,2048]{1,0:T(8,128)(2,1)}, u32[]{:S(2)}, u32[]{:S(2)}) collective-permute-start(bf16[128,2048]{1,0:T(8,128)(2,1)} %param.8), channel_id=1, source_target_pairs={{0,128},{8,136},{16,144},{24,152},{32,160},{40,168},{48,176},{56,1... | collective-permute-start | bytes 1572872 | tf_op jit(solution)/shard_map/ppermute | solution.py:11
  17.6 376.5 %collective-permute-start.2 = (bf16[128,2048]{1,0:T(8,128)(2,1)}, bf16[128,2048]{1,0:T(8,128)(2,1)}, u32[]{:S(2)}, u32[]{:S(2)}) collective-permute-start(bf16[128,2048]{1,0:T(8,128)(2,1)} %param.8), channel_id=1, source_target_pairs={{0,8},{8,0},{16,24},{24,16},{32,40},{40,32},{48,56},{56,48},{64,72... | collective-permute-start | bytes 1572872 | tf_op jit(solution)/shard_map/ppermute | solution.py:11
  388.7 3.1 copy-start.3
  388.7 0.8 copy-start.12
  391.8 1.7 copy-start
  391.8 2.3 copy-start.7
  396.7 4.7 copy-start.9
  399.3 2.4 copy-start.1
  399.3 2.8 copy-start.6
  402.1 2.1 copy-start.4
  402.1 2.1 copy-start.10
  402.1 2.1 copy-start.11
  404.6 9.3 copy-start.5
  421.1 6.6 copy-start.2
  423.5 24.4 %collective-permute-start.7 = (bf16[128,2048]{0,1:T(8,128)(2,1)}, bf16[128,2048]{0,1:T(8,128)(2,1)}, u32[]{:S(2)}, u32[]{:S(2)}) collective-permute-start(bf16[128,2048]{0,1:T(8,128)(2,1)} %bitcast.29), channel_id=1, source_target_pairs={{0,128},{8,136},{16,144},{24,152},{32,160},{40,168},{48,176},{56,1... | collective-permute-start | bytes 1572872 | tf_op jit(solution)/shard_map/ppermute | solution.py:11
  425.4 22.5 %collective-permute-start.6 = (bf16[128,2048]{0,1:T(8,128)(2,1)}, bf16[128,2048]{0,1:T(8,128)(2,1)}, u32[]{:S(2)}, u32[]{:S(2)}) collective-permute-start(bf16[128,2048]{0,1:T(8,128)(2,1)} %bitcast.27), channel_id=1, source_target_pairs={{0,8},{8,0},{16,24},{24,16},{32,40},{40,32},{48,56},{56,48},{64,72... | collective-permute-start | bytes 1572872 | tf_op jit(solution)/shard_map/ppermute | solution.py:11
  431.1 28.3 %collective-permute-start.5 = (bf16[128,2048]{0,1:T(8,128)(2,1)}, bf16[128,2048]{0,1:T(8,128)(2,1)S(1)}, u32[]{:S(2)}, u32[]{:S(2)}) collective-permute-start(bf16[128,2048]{0,1:T(8,128)(2,1)} %bitcast.112), channel_id=1, source_target_pairs={{0,128},{8,136},{16,144},{24,152},{32,160},{40,168},{48,176},{56,1... | collective-permute-start | bytes 1572872 | tf_op jit(solution)/shard_map/ppermute | solution.py:11
  436.8 22.8 %collective-permute-start.4 = (bf16[128,2048]{0,1:T(8,128)(2,1)}, bf16[128,2048]{0,1:T(8,128)(2,1)}, u32[]{:S(2)}, u32[]{:S(2)}) collective-permute-start(bf16[128,2048]{0,1:T(8,128)(2,1)} %bitcast.113), channel_id=1, source_target_pairs={{0,8},{8,0},{16,24},{24,16},{32,40},{40,32},{48,56},{56,48},{64,72... | collective-permute-start | bytes 1572872 | tf_op jit(solution)/shard_map/ppermute | solution.py:11
  463.3 789.6 %copy-start.13 = (s32[2]{0:T(128)S(1)}, s32[2]{0:T(128)}, u32[]{:S(2)}) copy-start(s32[2]{0:T(128)} %param.11) | copy-start | bytes 28
Sparse Core Ops, SparseCore 0:
  421.2 831.6 all-reduce.2
where the time goes:
time: 1270 us; the launch traced here: 1260 us
  waiting for transfers between devices  802 us (63%)
  blocking collectives  357 us (28%)
  local copies, waits for them, and re-layouts  30 us (2%)
  matrix products  23 us (2%)
  starting transfers between devices  22.4 us (2%)
  between operations  15.1 us (1%)
  other arithmetic  14.6 us (1%)
    unnamed x2, waiting for transfers between devices  788 us
    all_gather x1, blocking collectives, local(): lax.all_gather(picked_values, 'seq', axis=0, tiled=True)  129 us
    all_gather x1, blocking collectives, local(): every_doc = lax.all_gather(documents, 'seq', axis=0, tiled=True)  114 us
    all_gather x1, blocking collectives, local(): lax.all_gather(picked_keys, 'seq', axis=0, tiled=True)  114 us
  transfers between devices with their start and end apart: 9, of which 3 were waited for; matrix products, arithmetic and copies ran while one was open for 3% of the time, Pallas kernels for 0%

commit v1 on v0

--- a/solution.py
+++ b/solution.py
@@ -23,16 +23,27 @@
     def split(array):
         return array.reshape(array.shape[0], HEADS, head_size)
 
-    every_doc = lax.all_gather(documents, "seq", axis=0, tiled=True)
-    picked_keys = keys[global_offsets]
-    picked_values = values[global_offsets]
-    global_keys, global_values = (
-        lax.all_gather(picked_keys, "seq", axis=0, tiled=True),
-        lax.all_gather(picked_values, "seq", axis=0, tiled=True),
-    )
-    global_count = global_keys.shape[0]
     per_block = global_offsets.shape[0]
-    owners = jnp.arange(global_count, dtype=jnp.int32) // per_block
+    picked = jnp.stack([keys[global_offsets], values[global_offsets]], 0)
+    gather_bits = [5, 4, 2, 1, 3, 0] if log_shards == 6 else list(range(log_shards))[::-1]
+    gathered = picked
+    owner_bits = []
+    for bit in gather_bits:
+        came = from_partner(gathered, "seq", bit)
+        upper = ((myself >> bit) & 1) == 1
+        gathered = jnp.stack(
+            [jnp.where(upper, came, gathered), jnp.where(upper, gathered, came)], 0
+        )
+        owner_bits.insert(0, bit)
+    global_count = shards * per_block
+    gathered = gathered.reshape((shards,) + picked.shape)
+    global_keys = gathered[:, 0].reshape(global_count, columns)
+    global_values = gathered[:, 1].reshape(global_count, columns)
+    slot = jnp.arange(shards, dtype=jnp.int32)
+    owners_perm = jnp.zeros_like(slot)
+    for position, bit in enumerate(owner_bits):
+        owners_perm = owners_perm | (((slot >> (log_shards - 1 - position)) & 1) << bit)
+    owners = jnp.repeat(owners_perm, per_block)
     distance = owners ^ myself
     nearby = distance == 0
     for level_bit in level_bits:
@@ -43,9 +54,8 @@
     value_list = [values]
     mask_list = [documents[:, None] == documents[None, :]]
     for level_bit in level_bits:
-        partner_keys, partner_values = from_partner((keys, values), "seq", level_bit)
-        partner_docs = lax.dynamic_slice_in_dim(
-            every_doc, (myself ^ 1 << level_bit) * rows_here, rows_here
+        partner_keys, partner_values, partner_docs = from_partner(
+            (keys, values, documents), "seq", level_bit
         )
         key_list.append(partner_keys)
         value_list.append(partner_values)
@@ -123,18 +133,20 @@
     value_part = jnp.einsum(
         "htg,thd->ghd", global_prob_b, dout_heads, preferred_element_type=jnp.float32
     )
-    owned = lax.psum_scatter(
-        jnp.concatenate(
-            [
-                key_part.reshape(per_block * lax.axis_size("seq"), columns),
-                value_part.reshape(per_block * lax.axis_size("seq"), columns),
-            ],
-            1,
-        ),
-        "seq",
-        scatter_dimension=0,
-        tiled=True,
+    owned = jnp.concatenate(
+        [
+            key_part.reshape(global_count, columns),
+            value_part.reshape(global_count, columns),
+        ],
+        1,
     )
+    for bit in owner_bits:
+        owned = owned.reshape((2, -1) + owned.shape[1:])
+        upper = ((myself >> bit) & 1) == 1
+        keep = jnp.where(upper, owned[1], owned[0])
+        send = jnp.where(upper, owned[0], owned[1])
+        owned = keep + from_partner(send, "seq", bit)
+    owned = owned.reshape(per_block, 2 * columns)
     placement = (jnp.arange(rows_here, dtype=jnp.int32)[:, None] == global_offsets[None, :]).astype(
         jnp.float32
     )

time: 1270 us -> 271 us (0.21)
  waiting for transfers between devices: 802 us -> 61.9 us
  blocking collectives: 357 us -> 0 us
  starting transfers between devices: 22.4 us -> 79.9 us
  local copies, waits for them, and re-layouts: 30 us -> 59.9 us
  other arithmetic: 14.6 us -> 41.3 us
  between operations: 15.1 us -> 1.35 us
    unnamed x2 -> x0, waiting for transfers between devices: 788 us -> none
    all_gather x3 -> x0, blocking collectives: 357 us -> none  [the longest x1 129 us: local(): lax.all_gather(picked_values, 'seq', axis=0, tiled=True)]
    ppermute x8 -> x22, starting transfers between devices: 22.4 us -> 79.9 us  [from_partner(): lax.ppermute(array, axis, [(i, i ^ 1 << stride) for i in range(lax.axis_s...]
    ppermute x8 -> x22, waiting for transfers between devices: 14.1 us -> 61.9 us  [from_partner(): lax.ppermute(array, axis, [(i, i ^ 1 << stride) for i in range(lax.axis_s...]
    select_n x0 -> x7, local copies, waits for them, and re-layouts: none -> 13.2 us  [the longest x6 12.6 us: local(): send = jnp.where(upper, owned[0], owned[1])]
    add x0 -> x5, other arithmetic: none -> 12.8 us  [local(): owned = keep + from_partner(send, 'seq', bit)]
  transfers between devices with their start and end apart: 9 -> 22, of which waited for: 3 -> 8; matrix products, arithmetic and copies ran while one was open for 3% -> 35% of each run, Pallas kernels for 0% -> 0%
where the time goes in v1:
time: 271 us; the launch traced here: 268 us
  starting transfers between devices  79.9 us (29%)
  waiting for transfers between devices  61.9 us (23%)
  local copies, waits for them, and re-layouts  59.9 us (22%)
  other arithmetic  41.3 us (15%)
  matrix products  23.8 us (9%)
    ppermute x22, starting transfers between devices, from_partner(): lax.ppermute(array, axis, [(i, i ^ 1 << stride) for i in range(lax.axis_s...  79.9 us
    ppermute x22, waiting for transfers between devices, from_partner(): lax.ppermute(array, axis, [(i, i ^ 1 << stride) for i in range(lax.axis_s...  61.9 us
    add x5, other arithmetic, local(): owned = keep + from_partner(send, 'seq', bit)  12.8 us
    select_n x6, local copies, waits for them, and re-layouts, local(): send = jnp.where(upper, owned[0], owned[1])  12.6 us
    ppermute x5, local copies, waits for them, and re-layouts, from_partner(): lax.ppermute(array, axis, [(i, i ^ 1 << stride) for i in range(lax.axis_s...  12.1 us
    unnamed x51, local copies, waits for them, and re-layouts  11.9 us
    select_n x6, other arithmetic, local(): send = jnp.where(upper, owned[0], owned[1])  10.4 us
    another operation x12, other arithmetic, local(): jnp.stack([jnp.where(upper, came, gathered), jnp.where(upper, gathered, c...  7.2 us
  transfers between devices with their start and end apart: 22, of which 8 were waited for; matrix products, arithmetic and copies ran while one was open for 35% of the time, Pallas kernels for 0%

profile of v1, /device:TPU:24, one launch (start us, length us, event | category | flops | bytes accessed | tf_op | source)
XLA Modules:
  0.0 268.3 jit_solution(3749250107366907164)
XLA Ops:
  4.8 9.2 %collective-permute-start = (bf16[2,2,2048]{2,1,0:T(2,128)(2,1)S(1)}, bf16[2,2,2048]{2,1,0:T(2,128)(2,1)S(1)}, u32[]{:S(2)}, u32[]{:S(2)}) collective-permute-start(bf16[2,2,2048]{2,1,0:T(2,128)(2,1)S(1)} %pad_maximum_fusion.9), channel_id=1, source_target_pairs={{0,256},{8,264},{16,272},{24,280},{32,288},{40,296},{48,304},{56,3... | collective-permute-start | bytes 49160 | tf_op jit(solution)/shard_map/ppermute | solution.py:11
  15.9 5.2 %collective-permute-start.1 = (bf16[2,2,2,2048]{3,2,1,0:T(2,128)(2,1)S(1)}, bf16[2,2,2,2048]{3,2,1,0:T(2,128)(2,1)S(1)}, u32[]{:S(2)}, u32[]{:S(2)}) collective-permute-start(bf16[2,2,2,2048]{3,2,1,0:T(2,128)(2,1)S(1)} %pad_maximum_fusion.8), channel_id=1, source_target_pairs={{0,128},{8,136},{16,144},{24,152},{32,160},{40,168},{48,176},{56,1... | collective-permute-start | bytes 98312 | tf_op jit(solution)/shard_map/ppermute | solution.py:11
  23.1 4.9 %collective-permute-start.2 = (bf16[2,2,2,2,2048]{4,3,2,1,0:T(2,128)(2,1)S(1)}, bf16[2,2,2,2,2048]{4,3,2,1,0:T(2,128)(2,1)S(1)}, u32[]{:S(2)}, u32[]{:S(2)}) collective-permute-start(bf16[2,2,2,2,2048]{4,3,2,1,0:T(2,128)(2,1)S(1)} %pad_maximum_fusion.7), channel_id=1, source_target_pairs={{0,32},{8,40},{16,48},{24,56},{32,0},{40,8},{48,16},{56,24},{64,96... | collective-permute-start | bytes 196616 | tf_op jit(solution)/shard_map/ppermute | solution.py:11
  28.1 2.7 %collective-permute-done.2 = bf16[2,2,2,2,2048]{4,3,2,1,0:T(2,128)(2,1)S(1)} collective-permute-done((bf16[2,2,2,2,2048]{4,3,2,1,0:T(2,128)(2,1)S(1)}, bf16[2,2,2,2,2048]{4,3,2,1,0:T(2,128)(2,1)S(1)}, u32[]{:S(2)}, u32[]{:S(2)}) %collective-permute-start.2) | collective-permute-done | bytes 65568 | tf_op jit(solution)/shard_map/ppermute | solution.py:11
  31.1 3.4 %collective-permute-start.3 = (bf16[2,2,2,2,2,2048]{5,4,3,2,1,0:T(2,128)(2,1)S(1)}, bf16[2,2,2,2,2,2048]{5,4,3,2,1,0:T(2,128)(2,1)S(1)}, u32[]{:S(2)}, u32[]{:S(2)}) collective-permute-start(bf16[2,2,2,2,2,2048]{5,4,3,2,1,0:T(2,128)(2,1)S(1)} %pad_maximum_fusion.6), channel_id=1, source_target_pairs={{0,16},{8,24},{16,0},{24,8},{32,48},{40,56},{48,32},{56,40},{64,80... | collective-permute-start | bytes 393224 | tf_op jit(solution)/shard_map/ppermute | solution.py:11
  34.5 4.8 %collective-permute-start.7 = (s32[128]{0:T(128)}, s32[128]{0:T(128)S(1)}, u32[]{:S(2)}, u32[]{:S(2)}) collective-permute-start(s32[128]{0:T(128)} %param.10), channel_id=1, source_target_pairs={{0,128},{8,136},{16,144},{24,152},{32,160},{40,168},{48,176},{56,1... | collective-permute-start | bytes 1544 | tf_op jit(solution)/shard_map/ppermute | solution.py:11
  48.5 4.5 %collective-permute-start.11 = (bf16[128,2048]{1,0:T(8,128)(2,1)S(1)}, bf16[128,2048]{1,0:T(8,128)(2,1)S(1)}, u32[]{:S(2)}, u32[]{:S(2)}) collective-permute-start(bf16[128,2048]{1,0:T(8,128)(2,1)S(1)} %copy-done.16), channel_id=1, source_target_pairs={{0,128},{8,136},{16,144},{24,152},{32,160},{40,168},{48,176},{56,1... | collective-permute-start | bytes 1572872 | tf_op jit(solution)/shard_map/ppermute | solution.py:11
  55.7 3.8 %collective-permute-start.4 = (bf16[2,2,2,2,2,2,2048]{6,5,4,3,2,1,0:T(2,128)(2,1)S(1)}, bf16[2,2,2,2,2,2,2048]{6,5,4,3,2,1,0:T(2,128)(2,1)S(1)}, u32[]{:S(2)}, u32[]{:S(2)}) collective-permute-start(bf16[2,2,2,2,2,2,2048]{6,5,4,3,2,1,0:T(2,128)(2,1)S(1)} %pad_maximum_fusion.5), channel_id=1, source_target_pairs={{0,64},{8,72},{16,80},{24,88},{32,96},{40,104},{48,112},{56,120},{... | collective-permute-start | bytes 786440 | tf_op jit(solution)/shard_map/ppermute | solution.py:11
  59.7 13.8 %collective-permute-done.4 = bf16[2,2,2,2,2,2,2048]{6,5,4,3,2,1,0:T(2,128)(2,1)S(1)} collective-permute-done((bf16[2,2,2,2,2,2,2048]{6,5,4,3,2,1,0:T(2,128)(2,1)S(1)}, bf16[2,2,2,2,2,2,2048]{6,5,4,3,2,1,0:T(2,128)(2,1)S(1)}, u32[]{:S(2)}, u32[]{:S(2)}) %collective-permute-start.4) | collective-permute-done | bytes 262176 | tf_op jit(solution)/shard_map/ppermute | solution.py:11
  77.8 15.6 %collective-permute-done.11 = bf16[128,2048]{1,0:T(8,128)(2,1)S(1)} collective-permute-done((bf16[128,2048]{1,0:T(8,128)(2,1)S(1)}, bf16[128,2048]{1,0:T(8,128)(2,1)S(1)}, u32[]{:S(2)}, u32[]{:S(2)}) %collective-permute-start.11) | collective-permute-done | bytes 524320 | tf_op jit(solution)/shard_map/ppermute | solution.py:11
  97.6 2.5 fusion.3
  119.2 3.1 %copy.109 = f32[64,4096]{1,0:T(8,128)} copy(f32[64,4096]{0,1:T(8,128)} %fusion.4) | data formatting | bytes 2097152 | tf_op jit(solution)/shard_map/jit(_where)/select_n | solution.py:147
  124.5 3.9 %fusion = bf16[16,128,384]{1,2,0:T(8,128)(2,1)S(1)} fusion(bf16[384,16,128]{0,2,1:T(8,128)(2,1)} %bitcast.136, bf16[128,16,128]{0,2,1:T(8,128)(2,1)} %bitcast.138, f32[16,128]{1,0:T(8,128)S(1)} %bitcast.151, f32[16,128]{1,0:T(8,128)S(1)} %add.56, f32[16,128]{1,0:T(8,128)S(1)} %max.7, f32[16,384,128]{2,1,0:T(8,128)} %get-tuple-element.44, ...), kind=kOutput, calls=%fused_computation.3 | convolution fusion | flops 206831616 | bytes 6889472 | tf_op jit(solution)/shard_map/thd,uhd->htu/dot_general | solution.py:96
  138.4 3.2 %copy.110 = f32[64,4096]{0,1:T(8,128)} copy(f32[64,4096]{1,0:T(8,128)} %collective-permute-done.14) | data formatting | bytes 2097152 | tf_op jit(solution)/shard_map/ppermute | solution.py:11
  141.6 2.8 %select_add_fusion.4 = f32[64,4096]{0,1:T(8,128)S(1)} fusion(f32[64,4096]{0,1:T(8,128)} %copy.110, f32[128,2048]{0,1:T(8,128)} %bitcast.131, f32[128,2048]{0,1:T(8,128)S(1)} %bitcast.129, pred[]{:T(512)S(6)} %eq.104), kind=kLoop, calls=%fused_computation.16 | loop fusion | flops 1048576 | bytes 4194305 | tf_op jit(solution)/shard_map/add | solution.py:148
  148.5 3.4 %collective-permute-start.15 = (f32[32,4096]{1,0:T(8,128)S(1)}, f32[32,4096]{1,0:T(8,128)S(1)}, u32[]{:S(2)}, u32[]{:S(2)}) collective-permute-start(f32[32,4096]{1,0:T(8,128)S(1)} %copy.111), channel_id=1, source_target_pairs={{0,64},{8,72},{16,80},{24,88},{32,96},{40,104},{48,112},{56,120},{... | collective-permute-start | bytes 1572872 | tf_op jit(solution)/shard_map/ppermute | solution.py:11
  151.8 5.1 %fusion.67 = (bf16[384,16,128]{0,2,1:T(8,128)(2,1)}, f32[384,16,128]{0,2,1:T(8,128)}) fusion(bf16[128,16,128]{0,2,1:T(8,128)(2,1)} %bitcast.139, f32[16,128]{1,0:T(8,128)S(1)} %add.56, f32[16,128]{1,0:T(8,128)S(1)} %max.7, f32[16,384,128]{2,1,0:T(8,128)} %get-tuple-element.44, pred[128,384]{0,1:T(8,128)(4,1)S(1)} %pad_add_fusion), kind=kOutput, calls=%fused_computation.131 | convolution fusion | flops 206045184 | bytes 8454144 | tf_op jit(solution)/shard_map/htu,thd->uhd/dot_general | solution.py:106
  156.9 13.1 %collective-permute-done.15 = f32[32,4096]{1,0:T(8,128)S(1)} collective-permute-done((f32[32,4096]{1,0:T(8,128)S(1)}, f32[32,4096]{1,0:T(8,128)S(1)}, u32[]{:S(2)}, u32[]{:S(2)}) %collective-permute-start.15) | collective-permute-done | bytes 524320 | tf_op jit(solution)/shard_map/ppermute | solution.py:11
  179.9 2.4 collective-permute-start.16
  182.4 2.6 fusion.11
  185.0 5.1 %collective-permute-done.16 = f32[16,4096]{1,0:T(8,128)} collective-permute-done((f32[16,4096]{1,0:T(8,128)S(1)}, f32[16,4096]{1,0:T(8,128)}, u32[]{:S(2)}, u32[]{:S(2)}) %collective-permute-start.16) | collective-permute-done | bytes 262176 | tf_op jit(solution)/shard_map/ppermute | solution.py:11
  190.2 2.9 %copy.114 = f32[16,4096]{0,1:T(8,128)} copy(f32[16,4096]{1,0:T(8,128)} %collective-permute-done.16) | data formatting | bytes 524288 | tf_op jit(solution)/shard_map/ppermute | solution.py:11
  193.0 3.5 %select_add_fusion.2 = f32[16,4096]{0,1:T(8,128)S(1)} fusion(f32[16,4096]{0,1:T(8,128)} %copy.114, f32[32,4096]{0,1:T(8,128)} %copy-done.2, pred[]{:T(512)S(6)} %eq.106), kind=kLoop, calls=%fused_computation.14 | loop fusion | flops 131072 | bytes 1048577 | tf_op jit(solution)/shard_map/add | solution.py:148
  200.7 4.8 %collective-permute-start.17 = (f32[8,4096]{1,0:T(8,128)S(1)}, f32[8,4096]{1,0:T(8,128)S(1)}, u32[]{:S(2)}, u32[]{:S(2)}) collective-permute-start(f32[8,4096]{1,0:T(8,128)S(1)} %copy.115), channel_id=1, source_target_pairs={{0,32},{8,40},{16,48},{24,56},{32,0},{40,8},{48,16},{56,24},{64,96... | collective-permute-start | bytes 393224 | tf_op jit(solution)/shard_map/ppermute | solution.py:11
  209.8 2.7 collective-permute-start.21
  225.0 4.1 %collective-permute-start.18 = (f32[4,4096]{1,0:T(4,128)S(1)}, f32[4,4096]{1,0:T(4,128)S(1)}, u32[]{:S(2)}, u32[]{:S(2)}) collective-permute-start(f32[4,4096]{1,0:T(4,128)S(1)} %copy.117), channel_id=1, source_target_pairs={{0,128},{8,136},{16,144},{24,152},{32,160},{40,168},{48,176},{56,1... | collective-permute-start | bytes 196616 | tf_op jit(solution)/shard_map/ppermute | solution.py:11
  229.1 2.7 fusion.17
  231.8 7.8 %collective-permute-done.18 = f32[4,4096]{1,0:T(4,128)S(1)} collective-permute-done((f32[4,4096]{1,0:T(4,128)S(1)}, f32[4,4096]{1,0:T(4,128)S(1)}, u32[]{:S(2)}, u32[]{:S(2)}) %collective-permute-start.18) | collective-permute-done | bytes 65568 | tf_op jit(solution)/shard_map/ppermute | solution.py:11
  248.0 7.8 %collective-permute-start.19 = (f32[2,4096]{1,0:T(2,128)S(1)}, f32[2,4096]{1,0:T(2,128)S(1)}, u32[]{:S(2)}, u32[]{:S(2)}) collective-permute-start(f32[2,4096]{1,0:T(2,128)S(1)} %copy.119), channel_id=1, source_target_pairs={{0,256},{8,264},{16,272},{24,280},{32,288},{40,296},{48,304},{56,3... | collective-permute-start | bytes 98312 | tf_op jit(solution)/shard_map/ppermute | solution.py:11
  255.8 2.7 fusion.15
  260.0 2.6 copy.103
  262.6 2.6 copy.122
  (145 shorter events, 107.5 us)
Async XLA Ops:
  0.6 46.3 %copy-start.17 = (bf16[128,2048]{1,0:T(8,128)(2,1)S(1)}, bf16[128,2048]{1,0:T(8,128)(2,1)}, u32[]{:S(2)}) copy-start(bf16[128,2048]{1,0:T(8,128)(2,1)} %param.9) | copy-start | bytes 1572868
  0.6 47.3 %copy-start.18 = (bf16[128,2048]{1,0:T(8,128)(2,1)S(1)}, bf16[128,2048]{1,0:T(8,128)(2,1)}, u32[]{:S(2)}) copy-start(bf16[128,2048]{1,0:T(8,128)(2,1)} %param.6) | copy-start | bytes 1572868
  4.8 43.7 %copy-start.16 = (bf16[128,2048]{1,0:T(8,128)(2,1)S(1)}, bf16[128,2048]{1,0:T(8,128)(2,1)}, u32[]{:S(2)}) copy-start(bf16[128,2048]{1,0:T(8,128)(2,1)} %param.8) | copy-start | bytes 1572868
  4.8 10.9 %collective-permute-start = (bf16[2,2,2048]{2,1,0:T(2,128)(2,1)S(1)}, bf16[2,2,2048]{2,1,0:T(2,128)(2,1)S(1)}, u32[]{:S(2)}, u32[]{:S(2)}) collective-permute-start(bf16[2,2,2048]{2,1,0:T(2,128)(2,1)S(1)} %pad_maximum_fusion.9), channel_id=1, source_target_pairs={{0,256},{8,264},{16,272},{24,280},{32,288},{40,296},{48,304},{56,3... | collective-permute-start | bytes 49160 | tf_op jit(solution)/shard_map/ppermute | solution.py:11
  15.9 7.1 %collective-permute-start.1 = (bf16[2,2,2,2048]{3,2,1,0:T(2,128)(2,1)S(1)}, bf16[2,2,2,2048]{3,2,1,0:T(2,128)(2,1)S(1)}, u32[]{:S(2)}, u32[]{:S(2)}) collective-permute-start(bf16[2,2,2,2048]{3,2,1,0:T(2,128)(2,1)S(1)} %pad_maximum_fusion.8), channel_id=1, source_target_pairs={{0,128},{8,136},{16,144},{24,152},{32,160},{40,168},{48,176},{56,1... | collective-permute-start | bytes 98312 | tf_op jit(solution)/shard_map/ppermute | solution.py:11
  23.1 7.7 %collective-permute-start.2 = (bf16[2,2,2,2,2048]{4,3,2,1,0:T(2,128)(2,1)S(1)}, bf16[2,2,2,2,2048]{4,3,2,1,0:T(2,128)(2,1)S(1)}, u32[]{:S(2)}, u32[]{:S(2)}) collective-permute-start(bf16[2,2,2,2,2048]{4,3,2,1,0:T(2,128)(2,1)S(1)} %pad_maximum_fusion.7), channel_id=1, source_target_pairs={{0,32},{8,40},{16,48},{24,56},{32,0},{40,8},{48,16},{56,24},{64,96... | collective-permute-start | bytes 196616 | tf_op jit(solution)/shard_map/ppermute | solution.py:11
  31.1 28.4 %copy-start.21 = (s32[128]{0:T(128)S(1)}, s32[128]{0:T(128)}, u32[]{:S(2)}) copy-start(s32[128]{0:T(128)} %param.10) | copy-start | bytes 1540
  31.1 17.4 %collective-permute-start.3 = (bf16[2,2,2,2,2,2048]{5,4,3,2,1,0:T(2,128)(2,1)S(1)}, bf16[2,2,2,2,2,2048]{5,4,3,2,1,0:T(2,128)(2,1)S(1)}, u32[]{:S(2)}, u32[]{:S(2)}) collective-permute-start(bf16[2,2,2,2,2,2048]{5,4,3,2,1,0:T(2,128)(2,1)S(1)} %pad_maximum_fusion.6), channel_id=1, source_target_pairs={{0,16},{8,24},{16,0},{24,8},{32,48},{40,56},{48,32},{56,40},{64,80... | collective-permute-start | bytes 393224 | tf_op jit(solution)/shard_map/ppermute | solution.py:11
  34.5 19.2 %collective-permute-start.7 = (s32[128]{0:T(128)}, s32[128]{0:T(128)S(1)}, u32[]{:S(2)}, u32[]{:S(2)}) collective-permute-start(s32[128]{0:T(128)} %param.10), channel_id=1, source_target_pairs={{0,128},{8,136},{16,144},{24,152},{32,160},{40,168},{48,176},{56,1... | collective-permute-start | bytes 1544 | tf_op jit(solution)/shard_map/ppermute | solution.py:11
  39.4 16.3 %collective-permute-start.6 = (s32[128]{0:T(128)}, s32[128]{0:T(128)S(1)}, u32[]{:S(2)}, u32[]{:S(2)}) collective-permute-start(s32[128]{0:T(128)} %param.10), channel_id=1, source_target_pairs={{0,8},{8,0},{16,24},{24,16},{32,40},{40,32},{48,56},{56,48},{64,72... | collective-permute-start | bytes 1544 | tf_op jit(solution)/shard_map/ppermute | solution.py:11
  42.6 53.6 %collective-permute-start.9 = (bf16[128,2048]{0,1:T(8,128)(2,1)S(1)}, bf16[128,2048]{0,1:T(8,128)(2,1)}, u32[]{:S(2)}, u32[]{:S(2)}) collective-permute-start(bf16[128,2048]{0,1:T(8,128)(2,1)S(1)} %copy.81), channel_id=1, source_target_pairs={{0,128},{8,136},{16,144},{24,152},{32,160},{40,168},{48,176},{56,1... | collective-permute-start | bytes 1572872 | tf_op jit(solution)/shard_map/ppermute | solution.py:11
  44.5 51.6 %collective-permute-start.8 = (bf16[128,2048]{0,1:T(8,128)(2,1)S(1)}, bf16[128,2048]{0,1:T(8,128)(2,1)}, u32[]{:S(2)}, u32[]{:S(2)}) collective-permute-start(bf16[128,2048]{0,1:T(8,128)(2,1)S(1)} %copy.81), channel_id=1, source_target_pairs={{0,8},{8,0},{16,24},{24,16},{32,40},{40,32},{48,56},{56,48},{64,72... | collective-permute-start | bytes 1572872 | tf_op jit(solution)/shard_map/ppermute | solution.py:11
  48.5 44.9 %collective-permute-start.11 = (bf16[128,2048]{1,0:T(8,128)(2,1)S(1)}, bf16[128,2048]{1,0:T(8,128)(2,1)S(1)}, u32[]{:S(2)}, u32[]{:S(2)}) collective-permute-start(bf16[128,2048]{1,0:T(8,128)(2,1)S(1)} %copy-done.16), channel_id=1, source_target_pairs={{0,128},{8,136},{16,144},{24,152},{32,160},{40,168},{48,176},{56,1... | collective-permute-start | bytes 1572872 | tf_op jit(solution)/shard_map/ppermute | solution.py:11
  53.8 39.7 %collective-permute-start.10 = (bf16[128,2048]{1,0:T(8,128)(2,1)S(1)}, bf16[128,2048]{1,0:T(8,128)(2,1)S(1)}, u32[]{:S(2)}, u32[]{:S(2)}) collective-permute-start(bf16[128,2048]{1,0:T(8,128)(2,1)S(1)} %copy-done.16), channel_id=1, source_target_pairs={{0,8},{8,0},{16,24},{24,16},{32,40},{40,32},{48,56},{56,48},{64,72... | collective-permute-start | bytes 1572872 | tf_op jit(solution)/shard_map/ppermute | solution.py:11
  55.7 17.8 %collective-permute-start.4 = (bf16[2,2,2,2,2,2,2048]{6,5,4,3,2,1,0:T(2,128)(2,1)S(1)}, bf16[2,2,2,2,2,2,2048]{6,5,4,3,2,1,0:T(2,128)(2,1)S(1)}, u32[]{:S(2)}, u32[]{:S(2)}) collective-permute-start(bf16[2,2,2,2,2,2,2048]{6,5,4,3,2,1,0:T(2,128)(2,1)S(1)} %pad_maximum_fusion.5), channel_id=1, source_target_pairs={{0,64},{8,72},{16,80},{24,88},{32,96},{40,104},{48,112},{56,120},{... | collective-permute-start | bytes 786440 | tf_op jit(solution)/shard_map/ppermute | solution.py:11
  75.7 24.4 %collective-permute-start.5 = (bf16[2,2,2,2,2,2,2,2048]{7,6,5,4,3,2,1,0:T(2,128)(2,1)}, bf16[2,2,2,2,2,2,2,2048]{7,6,5,4,3,2,1,0:T(2,128)(2,1)}, u32[]{:S(2)}, u32[]{:S(2)}) collective-permute-start(bf16[2,2,2,2,2,2,2,2048]{7,6,5,4,3,2,1,0:T(2,128)(2,1)} %pad_maximum_fusion.4), channel_id=1, source_target_pairs={{0,8},{8,0},{16,24},{24,16},{32,40},{40,32},{48,56},{56,48},{64,72... | collective-permute-start | bytes 1572872 | tf_op jit(solution)/shard_map/ppermute | solution.py:11
  110.1 7.2 %copy-start.10 = (f32[16,128,128]{1,2,0:T(8,128)}, f32[16,128,128]{1,2,0:T(8,128)S(1)}, u32[]{:S(2)}) copy-start(f32[16,128,128]{1,2,0:T(8,128)S(1)} %fusion.59) | copy-start | bytes 3145732
  122.4 16.0 %collective-permute-start.14 = (f32[64,4096]{1,0:T(8,128)}, f32[64,4096]{1,0:T(8,128)}, u32[]{:S(2)}, u32[]{:S(2)}) collective-permute-start(f32[64,4096]{1,0:T(8,128)} %copy.109), channel_id=1, source_target_pairs={{0,8},{8,0},{16,24},{24,16},{32,40},{40,32},{48,56},{56,48},{64,72... | collective-permute-start | bytes 3145736 | tf_op jit(solution)/shard_map/ppermute | solution.py:11
  130.7 6.4 %copy-start.14 = (bf16[16,128,128]{1,2,0:T(8,128)(2,1)S(1)}, bf16[16,128,128]{1,2,0:T(8,128)(2,1)}, u32[]{:S(2)}) copy-start(bf16[16,128,128]{1,2,0:T(8,128)(2,1)} %copy-done.13) | copy-start | bytes 1572868
  131.7 82.9 %collective-permute-start.13 = (bf16[128,2048]{0,1:T(8,128)(2,1)}, bf16[128,2048]{0,1:T(8,128)(2,1)}, u32[]{:S(2)}, u32[]{:S(2)}) collective-permute-start(bf16[128,2048]{0,1:T(8,128)(2,1)} %bitcast.143), channel_id=1, source_target_pairs={{0,128},{8,136},{16,144},{24,152},{32,160},{40,168},{48,176},{56,1... | collective-permute-start | bytes 1572872 | tf_op jit(solution)/shard_map/ppermute | solution.py:11
  134.7 81.3 %collective-permute-start.12 = (bf16[128,2048]{0,1:T(8,128)(2,1)}, bf16[128,2048]{0,1:T(8,128)(2,1)}, u32[]{:S(2)}, u32[]{:S(2)}) collective-permute-start(bf16[128,2048]{0,1:T(8,128)(2,1)} %bitcast.28), channel_id=1, source_target_pairs={{0,8},{8,0},{16,24},{24,16},{32,40},{40,32},{48,56},{56,48},{64,72... | collective-permute-start | bytes 1572872 | tf_op jit(solution)/shard_map/ppermute | solution.py:11
  148.5 21.6 %collective-permute-start.15 = (f32[32,4096]{1,0:T(8,128)S(1)}, f32[32,4096]{1,0:T(8,128)S(1)}, u32[]{:S(2)}, u32[]{:S(2)}) collective-permute-start(f32[32,4096]{1,0:T(8,128)S(1)} %copy.111), channel_id=1, source_target_pairs={{0,64},{8,72},{16,80},{24,88},{32,96},{40,104},{48,112},{56,120},{... | collective-permute-start | bytes 1572872 | tf_op jit(solution)/shard_map/ppermute | solution.py:11
  175.7 6.7 %copy-start.7 = (bf16[16,128,384]{1,2,0:T(8,128)(2,1)S(1)}, bf16[16,128,384]{1,2,0:T(8,128)(2,1)}, u32[]{:S(2)}) copy-start(bf16[16,128,384]{1,2,0:T(8,128)(2,1)} %copy-done.6) | copy-start | bytes 4718596
  179.9 10.2 %collective-permute-start.16 = (f32[16,4096]{1,0:T(8,128)S(1)}, f32[16,4096]{1,0:T(8,128)}, u32[]{:S(2)}, u32[]{:S(2)}) collective-permute-start(f32[16,4096]{1,0:T(8,128)S(1)} %copy.113), channel_id=1, source_target_pairs={{0,16},{8,24},{16,0},{24,8},{32,48},{40,56},{48,32},{56,40},{64,80... | collective-permute-start | bytes 786440 | tf_op jit(solution)/shard_map/ppermute | solution.py:11
  198.5 9.3 %copy-start.20 = (bf16[16,128,128]{2,1,0:T(8,128)(2,1)S(1)}, bf16[16,128,128]{2,1,0:T(8,128)(2,1)}, u32[]{:S(2)}) copy-start(bf16[16,128,128]{2,1,0:T(8,128)(2,1)} %get-tuple-element.46) | copy-start | bytes 1572868
  200.7 8.1 %copy-start.12 = (bf16[16,128,128]{2,1,0:T(8,128)(2,1)S(1)}, bf16[16,128,128]{2,1,0:T(8,128)(2,1)}, u32[]{:S(2)}) copy-start(bf16[16,128,128]{2,1,0:T(8,128)(2,1)} %fusion.11) | copy-start | bytes 1572868
  200.7 17.4 %collective-permute-start.17 = (f32[8,4096]{1,0:T(8,128)S(1)}, f32[8,4096]{1,0:T(8,128)S(1)}, u32[]{:S(2)}, u32[]{:S(2)}) collective-permute-start(f32[8,4096]{1,0:T(8,128)S(1)} %copy.115), channel_id=1, source_target_pairs={{0,32},{8,40},{16,48},{24,56},{32,0},{40,8},{48,16},{56,24},{64,96... | collective-permute-start | bytes 393224 | tf_op jit(solution)/shard_map/ppermute | solution.py:11
  209.8 45.9 %collective-permute-start.21 = (bf16[128,2048]{0,1:T(8,128)(2,1)}, bf16[128,2048]{0,1:T(8,128)(2,1)}, u32[]{:S(2)}, u32[]{:S(2)}) collective-permute-start(bf16[128,2048]{0,1:T(8,128)(2,1)} %bitcast.145), channel_id=1, source_target_pairs={{0,128},{8,136},{16,144},{24,152},{32,160},{40,168},{48,176},{56,1... | collective-permute-start | bytes 1572872 | tf_op jit(solution)/shard_map/ppermute | solution.py:11
  212.5 43.3 %collective-permute-start.20 = (bf16[128,2048]{0,1:T(8,128)(2,1)}, bf16[128,2048]{0,1:T(8,128)(2,1)}, u32[]{:S(2)}, u32[]{:S(2)}) collective-permute-start(bf16[128,2048]{0,1:T(8,128)(2,1)} %bitcast.144), channel_id=1, source_target_pairs={{0,8},{8,0},{16,24},{24,16},{32,40},{40,32},{48,56},{56,48},{64,72... | collective-permute-start | bytes 1572872 | tf_op jit(solution)/shard_map/ppermute | solution.py:11
  225.0 14.6 %collective-permute-start.18 = (f32[4,4096]{1,0:T(4,128)S(1)}, f32[4,4096]{1,0:T(4,128)S(1)}, u32[]{:S(2)}, u32[]{:S(2)}) collective-permute-start(f32[4,4096]{1,0:T(4,128)S(1)} %copy.117), channel_id=1, source_target_pairs={{0,128},{8,136},{16,144},{24,152},{32,160},{40,168},{48,176},{56,1... | collective-permute-start | bytes 196616 | tf_op jit(solution)/shard_map/ppermute | solution.py:11
  231.8 9.8 %copy-start.1 = (f32[8,4096]{0,1:T(8,128)S(1)}, f32[8,4096]{0,1:T(8,128)}, u32[]{:S(2)}) copy-start(f32[8,4096]{0,1:T(8,128)} %copy-done) | copy-start | bytes 393220
  248.0 17.8 %collective-permute-start.19 = (f32[2,4096]{1,0:T(2,128)S(1)}, f32[2,4096]{1,0:T(2,128)S(1)}, u32[]{:S(2)}, u32[]{:S(2)}) collective-permute-start(f32[2,4096]{1,0:T(2,128)S(1)} %copy.119), channel_id=1, source_target_pairs={{0,256},{8,264},{16,272},{24,280},{32,288},{40,296},{48,304},{56,3... | collective-permute-start | bytes 98312 | tf_op jit(solution)/shard_map/ppermute | solution.py:11
  (13 other events, 31.2 us)

commit v2 on v1

--- a/solution.py
+++ b/solution.py
@@ -27,24 +27,18 @@
     picked = jnp.stack([keys[global_offsets], values[global_offsets]], 0)
     gather_bits = [5, 4, 2, 1, 3, 0] if log_shards == 6 else list(range(log_shards))[::-1]
     gathered = picked
-    owner_bits = []
     for bit in gather_bits:
-        came = from_partner(gathered, "seq", bit)
-        upper = ((myself >> bit) & 1) == 1
-        gathered = jnp.stack(
-            [jnp.where(upper, came, gathered), jnp.where(upper, gathered, came)], 0
-        )
-        owner_bits.insert(0, bit)
+        gathered = jnp.stack([gathered, from_partner(gathered, "seq", bit)], 0)
+    owner_bits = gather_bits[::-1]
     global_count = shards * per_block
     gathered = gathered.reshape((shards,) + picked.shape)
     global_keys = gathered[:, 0].reshape(global_count, columns)
     global_values = gathered[:, 1].reshape(global_count, columns)
     slot = jnp.arange(shards, dtype=jnp.int32)
-    owners_perm = jnp.zeros_like(slot)
+    distance = jnp.zeros_like(slot)
     for position, bit in enumerate(owner_bits):
-        owners_perm = owners_perm | (((slot >> (log_shards - 1 - position)) & 1) << bit)
-    owners = jnp.repeat(owners_perm, per_block)
-    distance = owners ^ myself
+        distance = distance | (((slot >> (log_shards - 1 - position)) & 1) << bit)
+    distance = jnp.repeat(distance, per_block)
     nearby = distance == 0
     for level_bit in level_bits:
         nearby = nearby | (distance == 1 << level_bit)
@@ -133,20 +127,14 @@
     value_part = jnp.einsum(
         "htg,thd->ghd", global_prob_b, dout_heads, preferred_element_type=jnp.float32
     )
-    owned = jnp.concatenate(
-        [
-            key_part.reshape(global_count, columns),
-            value_part.reshape(global_count, columns),
-        ],
-        1,
-    )
-    for bit in owner_bits:
-        owned = owned.reshape((2, -1) + owned.shape[1:])
-        upper = ((myself >> bit) & 1) == 1
-        keep = jnp.where(upper, owned[1], owned[0])
-        send = jnp.where(upper, owned[0], owned[1])
-        owned = keep + from_partner(send, "seq", bit)
-    owned = owned.reshape(per_block, 2 * columns)
+    def scatter_rows(part):
+        part = part.reshape(global_count, columns)
+        for bit in owner_bits:
+            half = part.shape[0] // 2
+            part = part[:half] + from_partner(part[half:], "seq", bit)
+        return part
+
+    owned = jnp.concatenate([scatter_rows(key_part), scatter_rows(value_part)], 1)
     placement = (jnp.arange(rows_here, dtype=jnp.int32)[:, None] == global_offsets[None, :]).astype(
         jnp.float32
     )

time: 271 us -> 247 us (0.911)
  starting transfers between devices: 79.9 us -> 118 us
  local copies, waits for them, and re-layouts: 59.9 us -> 35.4 us
  other arithmetic: 41.3 us -> 22.2 us
  waiting for transfers between devices: 61.9 us -> 48.6 us
  matrix products: 23.8 us -> 20.1 us
    ppermute x22 -> x28, starting transfers between devices: 79.9 us -> 118 us  [from_partner(): lax.ppermute(array, axis, [(i, i ^ 1 << stride) for i in range(lax.axis_s...]
    ppermute x22 -> x28, waiting for transfers between devices: 61.9 us -> 48.6 us  [from_partner(): lax.ppermute(array, axis, [(i, i ^ 1 << stride) for i in range(lax.axis_s...]
    select_n x7 -> x0, local copies, waits for them, and re-layouts: 13.2 us -> none  [the longest x6 12.6 us: local(): send = jnp.where(upper, owned[0], owned[1])]
    ppermute x5 -> x0, local copies, waits for them, and re-layouts: 12.1 us -> none  [from_partner(): lax.ppermute(array, axis, [(i, i ^ 1 << stride) for i in range(lax.axis_s...]
    select_n x6 -> x0, other arithmetic: 10.4 us -> none  [local(): send = jnp.where(upper, owned[0], owned[1])]
    add x5 -> x12, other arithmetic: 12.8 us -> 3.38 us  [scatter_rows(): part = part[:half] + from_partner(part[half:], 'seq', bit)]
    slice x0 -> x12, local copies, waits for them, and re-layouts: none -> 3.23 us  [scatter_rows(): part = part[:half] + from_partner(part[half:], 'seq', bit)]
    unnamed x51 -> x31, local copies, waits for them, and re-layouts: 11.9 us -> 13.3 us
  transfers between devices with their start and end apart: 22 -> 28, of which waited for: 8 -> 11; matrix products, arithmetic and copies ran while one was open for 35% -> 21% of each run, Pallas kernels for 0% -> 0%
where the time goes in v2:
time: 247 us; the launch traced here: 246 us
  starting transfers between devices  118 us (48%)
  waiting for transfers between devices  48.6 us (20%)
  local copies, waits for them, and re-layouts  35.4 us (14%)
  other arithmetic  22.2 us (9%)
  matrix products  20.1 us (8%)
    ppermute x28, starting transfers between devices, from_partner(): lax.ppermute(array, axis, [(i, i ^ 1 << stride) for i in range(lax.axis_s...  118 us
    ppermute x28, waiting for transfers between devices, from_partner(): lax.ppermute(array, axis, [(i, i ^ 1 << stride) for i in range(lax.axis_s...  48.6 us
    unnamed x31, local copies, waits for them, and re-layouts  13.3 us
    another operation x12, other arithmetic, local(): gathered = jnp.stack([gathered, from_partner(gathered, 'seq', bit)], 0)  6.32 us
  transfers between devices with their start and end apart: 28, of which 11 were waited for; matrix products, arithmetic and copies ran while one was open for 21% of the time, Pallas kernels for 0%

profile of v2, /device:TPU:24, one launch (start us, length us, event | category | flops | bytes accessed | tf_op | source)
XLA Modules:
  0.0 245.6 jit_solution(8890005436224459939)
XLA Ops:
  0.6 5.3 %collective-permute-start.7 = (s32[128]{0:T(128)}, s32[128]{0:T(128)S(1)}, u32[]{:S(2)}, u32[]{:S(2)}) collective-permute-start(s32[128]{0:T(128)} %param.10), channel_id=1, source_target_pairs={{0,128},{8,136},{16,144},{24,152},{32,160},{40,168},{48,176},{56,1... | collective-permute-start | bytes 1544 | tf_op jit(solution)/shard_map/ppermute | solution.py:11
  11.1 2.4 collective-permute-start.8
  21.9 4.9 %collective-permute-start.11 = (bf16[128,2048]{1,0:T(8,128)(2,1)}, bf16[128,2048]{1,0:T(8,128)(2,1)S(1)}, u32[]{:S(2)}, u32[]{:S(2)}) collective-permute-start(bf16[128,2048]{1,0:T(8,128)(2,1)} %param.8), channel_id=1, source_target_pairs={{0,128},{8,136},{16,144},{24,152},{32,160},{40,168},{48,176},{56,1... | collective-permute-start | bytes 1572872 | tf_op jit(solution)/shard_map/ppermute | solution.py:11
  26.9 9.1 %collective-permute-start = (bf16[2,2,2048]{2,1,0:T(2,128)(2,1)S(1)}, bf16[2,2,2048]{2,1,0:T(2,128)(2,1)S(1)}, u32[]{:S(2)}, u32[]{:S(2)}) collective-permute-start(bf16[2,2,2048]{2,1,0:T(2,128)(2,1)S(1)} %pad_maximum_fusion.8), channel_id=1, source_target_pairs={{0,256},{8,264},{16,272},{24,280},{32,288},{40,296},{48,304},{56,3... | collective-permute-start | bytes 49160 | tf_op jit(solution)/shard_map/ppermute | solution.py:11
  39.0 30.8 %collective-permute-start.1 = (bf16[2,2,2,2048]{3,2,1,0:T(2,128)(2,1)S(1)}, bf16[2,2,2,2048]{3,2,1,0:T(2,128)(2,1)S(1)}, u32[]{:S(2)}, u32[]{:S(2)}) collective-permute-start(bf16[2,2,2,2048]{3,2,1,0:T(2,128)(2,1)S(1)} %pad_maximum_fusion.7), channel_id=1, source_target_pairs={{0,128},{8,136},{16,144},{24,152},{32,160},{40,168},{48,176},{56,1... | collective-permute-start | bytes 98312 | tf_op jit(solution)/shard_map/ppermute | solution.py:11
  71.9 4.9 %collective-permute-start.2 = (bf16[2,2,2,2,2048]{4,3,2,1,0:T(2,128)(2,1)S(1)}, bf16[2,2,2,2,2048]{4,3,2,1,0:T(2,128)(2,1)S(1)}, u32[]{:S(2)}, u32[]{:S(2)}) collective-permute-start(bf16[2,2,2,2,2048]{4,3,2,1,0:T(2,128)(2,1)S(1)} %pad_maximum_fusion.6), channel_id=1, source_target_pairs={{0,32},{8,40},{16,48},{24,56},{32,0},{40,8},{48,16},{56,24},{64,96... | collective-permute-start | bytes 196616 | tf_op jit(solution)/shard_map/ppermute | solution.py:11
  76.9 2.6 %collective-permute-done.2 = bf16[2,2,2,2,2048]{4,3,2,1,0:T(2,128)(2,1)S(1)} collective-permute-done((bf16[2,2,2,2,2048]{4,3,2,1,0:T(2,128)(2,1)S(1)}, bf16[2,2,2,2,2048]{4,3,2,1,0:T(2,128)(2,1)S(1)}, u32[]{:S(2)}, u32[]{:S(2)}) %collective-permute-start.2) | collective-permute-done | bytes 65568 | tf_op jit(solution)/shard_map/ppermute | solution.py:11
  79.7 3.4 %collective-permute-start.3 = (bf16[2,2,2,2,2,2048]{5,4,3,2,1,0:T(2,128)(2,1)S(1)}, bf16[2,2,2,2,2,2048]{5,4,3,2,1,0:T(2,128)(2,1)S(1)}, u32[]{:S(2)}, u32[]{:S(2)}) collective-permute-start(bf16[2,2,2,2,2,2048]{5,4,3,2,1,0:T(2,128)(2,1)S(1)} %pad_maximum_fusion.5), channel_id=1, source_target_pairs={{0,16},{8,24},{16,0},{24,8},{32,48},{40,56},{48,32},{56,40},{64,80... | collective-permute-start | bytes 393224 | tf_op jit(solution)/shard_map/ppermute | solution.py:11
  83.3 3.3 %collective-permute-done.3 = bf16[2,2,2,2,2,2048]{5,4,3,2,1,0:T(2,128)(2,1)S(1)} collective-permute-done((bf16[2,2,2,2,2,2048]{5,4,3,2,1,0:T(2,128)(2,1)S(1)}, bf16[2,2,2,2,2,2048]{5,4,3,2,1,0:T(2,128)(2,1)S(1)}, u32[]{:S(2)}, u32[]{:S(2)}) %collective-permute-start.3) | collective-permute-done | bytes 131104 | tf_op jit(solution)/shard_map/ppermute | solution.py:11
  89.3 5.9 %collective-permute-done.4 = bf16[2,2,2,2,2,2,2048]{6,5,4,3,2,1,0:T(2,128)(2,1)S(1)} collective-permute-done((bf16[2,2,2,2,2,2,2048]{6,5,4,3,2,1,0:T(2,128)(2,1)S(1)}, bf16[2,2,2,2,2,2,2048]{6,5,4,3,2,1,0:T(2,128)(2,1)S(1)}, u32[]{:S(2)}, u32[]{:S(2)}) %collective-permute-start.4) | collective-permute-done | bytes 262176 | tf_op jit(solution)/shard_map/ppermute | solution.py:11
  104.6 2.4 fusion.3
  107.0 2.6 %pad_maximum_fusion.2 = bf16[2,2,2,2,2,2,2,2,2048]{8,7,6,5,4,3,2,1,0:T(2,128)(2,1)S(1)} fusion(bf16[1,2,2,2,2,2,2,2,2048]{8,7,6,5,4,3,2,1,0:T(2,128)(2,1)} %bitcast.13, bf16[1,2,2,2,2,2,2,2,2048]{8,7,6,5,4,3,2,1,0:T(2,128)(2,1)S(1)} %fusion.81), kind=kLoop, calls=%fused_computation.36 | loop fusion | flops 524288 | bytes 2097152 | tf_op jit(solution)/shard_map/stack | solution.py:31
  113.9 2.5 %fusion.2 = f32[16,128]{1,0:T(8,128)S(1)} fusion(f32[16,384,128]{2,1,0:T(8,128)} %get-tuple-element.30, f32[16,128]{1,0:T(8,128)S(1)} %max.7, pred[128,384]{0,1:T(8,128)(4,1)S(1)} %pad_add_fusion), kind=kLoop, calls=%fused_computation.8 | loop fusion | flops 3143680 | bytes 3211264 | tf_op jit(solution)/shard_map/reduce_sum | solution.py:77
  121.7 2.6 %fusion = bf16[16,128,384]{1,2,0:T(8,128)(2,1)} fusion(bf16[384,16,128]{0,2,1:T(8,128)(2,1)S(1)} %bitcast.162, bf16[128,16,128]{0,2,1:T(8,128)(2,1)S(1)} %bitcast.167, f32[16,128]{1,0:T(8,128)S(1)} %bitcast.183, f32[16,128]{1,0:T(8,128)S(1)} %add.74, f32[16,128]{1,0:T(8,128)S(1)} %max.7, f32[16,384,128]{2,1,0:T(8,128)S(1)} %copy-done.1, ...), kind=kOutput, calls=%fused_computation.3 | convolution fusion | flops 206831616 | bytes 6889472 | tf_op jit(solution)/shard_map/thd,uhd->htu/dot_general | solution.py:90
  125.8 3.3 %fusion.64 = (bf16[384,16,128]{0,2,1:T(8,128)(2,1)}, f32[384,16,128]{0,2,1:T(8,128)}) fusion(bf16[128,16,128]{0,2,1:T(8,128)(2,1)S(1)} %bitcast.168, f32[16,128]{1,0:T(8,128)S(1)} %add.74, f32[16,128]{1,0:T(8,128)S(1)} %max.7, f32[16,384,128]{2,1,0:T(8,128)S(1)} %copy-done.1, pred[128,384]{0,1:T(8,128)(4,1)S(1)} %pad_add_fusion), kind=kOutput, calls=%fused_computation.122 | convolution fusion | flops 206045184 | bytes 8454144 | tf_op jit(solution)/shard_map/htu,thd->uhd/dot_general | solution.py:100
  130.9 2.6 %collective-permute-start.20 = (f32[64,2048]{1,0:T(8,128)}, f32[64,2048]{1,0:T(8,128)}, u32[]{:S(2)}, u32[]{:S(2)}) collective-permute-start(f32[64,2048]{1,0:T(8,128)} %bitcast.153), channel_id=1, source_target_pairs={{0,8},{8,0},{16,24},{24,16},{32,40},{40,32},{48,56},{56,48},{64,72... | collective-permute-start | bytes 1572872 | tf_op jit(solution)/shard_map/ppermute | solution.py:11
  135.5 3.1 %fusion.10 = bf16[16,128,128]{2,1,0:T(8,128)(2,1)} fusion(f32[16,128,128]{2,1,0:T(8,128)} %fusion.66, bf16[384,16,128]{0,2,1:T(8,128)(2,1)S(1)} %bitcast.156, bf16[16,128,384]{1,2,0:T(8,128)(2,1)} %fusion), kind=kOutput, calls=%fused_computation.25 | convolution fusion | flops 202113024 | bytes 4718592 | tf_op jit(solution)/shard_map/htu,uhd->thd/dot_general | solution.py:94
  145.7 4.8 %collective-permute-start.27 = (bf16[128,2048]{0,1:T(8,128)(2,1)}, bf16[128,2048]{0,1:T(8,128)(2,1)}, u32[]{:S(2)}, u32[]{:S(2)}) collective-permute-start(bf16[128,2048]{0,1:T(8,128)(2,1)} %bitcast.38), channel_id=1, source_target_pairs={{0,128},{8,136},{16,144},{24,152},{32,160},{40,168},{48,176},{56,1... | collective-permute-start | bytes 1572872 | tf_op jit(solution)/shard_map/ppermute | solution.py:11
  152.7 2.3 fusion.65
  157.1 2.2 collective-permute-start.13
  166.9 18.4 %collective-permute-done.27 = bf16[128,2048]{0,1:T(8,128)(2,1)} collective-permute-done((bf16[128,2048]{0,1:T(8,128)(2,1)}, bf16[128,2048]{0,1:T(8,128)(2,1)}, u32[]{:S(2)}, u32[]{:S(2)}) %collective-permute-start.27) | collective-permute-done | bytes 524320 | tf_op jit(solution)/shard_map/ppermute | solution.py:11
  189.6 7.1 %collective-permute-done.13 = bf16[128,2048]{0,1:T(8,128)(2,1)} collective-permute-done((bf16[128,2048]{0,1:T(8,128)(2,1)}, bf16[128,2048]{0,1:T(8,128)(2,1)}, u32[]{:S(2)}, u32[]{:S(2)}) %collective-permute-start.13) | collective-permute-done | bytes 524320 | tf_op jit(solution)/shard_map/ppermute | solution.py:11
  197.9 2.2 copy.59
  200.1 2.7 %fusion.16 = f32[128,16,128]{2,0,1:T(8,128)} fusion(f32[128,16,128]{2,0,1:T(8,128)S(1)} %copy.61, f32[128,16,128]{2,0,1:T(8,128)} %copy.59, f32[384,16,128]{2,0,1:T(8,128)} %get-tuple-element.36), kind=kLoop, calls=%fused_computation.35 | loop fusion | flops 524288 | bytes 4194304 | tf_op jit(solution)/shard_map/add | solution.py:115
  202.8 2.5 %copy.62 = f32[128,16,128]{0,2,1:T(8,128)} copy(f32[128,16,128]{2,0,1:T(8,128)} %fusion.16) | data formatting | bytes 2097152 | tf_op jit(solution)/shard_map/add | solution.py:115
  207.0 3.4 %collective-permute-start.22 = (f32[16,2048]{1,0:T(8,128)S(1)}, f32[16,2048]{1,0:T(8,128)S(1)}, u32[]{:S(2)}, u32[]{:S(2)}) collective-permute-start(f32[16,2048]{1,0:T(8,128)S(1)} %slice.182), channel_id=1, source_target_pairs={{0,16},{8,24},{16,0},{24,8},{32,48},{40,56},{48,32},{56,40},{64,80... | collective-permute-start | bytes 393224 | tf_op jit(solution)/shard_map/ppermute | solution.py:11
  211.5 2.4 collective-permute-start.16
  214.4 4.9 %collective-permute-start.23 = (f32[8,2048]{1,0:T(8,128)S(1)}, f32[8,2048]{1,0:T(8,128)S(1)}, u32[]{:S(2)}, u32[]{:S(2)}) collective-permute-start(f32[8,2048]{1,0:T(8,128)S(1)} %slice.184), channel_id=1, source_target_pairs={{0,32},{8,40},{16,48},{24,56},{32,0},{40,8},{48,16},{56,24},{64,96... | collective-permute-start | bytes 196616 | tf_op jit(solution)/shard_map/ppermute | solution.py:11
  219.3 3.9 %collective-permute-start.17 = (f32[8,2048]{1,0:T(8,128)S(1)}, f32[8,2048]{1,0:T(8,128)S(1)}, u32[]{:S(2)}, u32[]{:S(2)}) collective-permute-start(f32[8,2048]{1,0:T(8,128)S(1)} %slice.172), channel_id=1, source_target_pairs={{0,32},{8,40},{16,48},{24,56},{32,0},{40,8},{48,16},{56,24},{64,96... | collective-permute-start | bytes 196616 | tf_op jit(solution)/shard_map/ppermute | solution.py:11
  227.0 3.0 %collective-permute-start.18 = (f32[4,2048]{1,0:T(4,128)S(1)}, f32[4,2048]{1,0:T(4,128)S(1)}, u32[]{:S(2)}, u32[]{:S(2)}) collective-permute-start(f32[4,2048]{1,0:T(4,128)S(1)} %slice.174), channel_id=1, source_target_pairs={{0,128},{8,136},{16,144},{24,152},{32,160},{40,168},{48,176},{56,1... | collective-permute-start | bytes 98312 | tf_op jit(solution)/shard_map/ppermute | solution.py:11
  233.8 6.1 %collective-permute-start.19 = (f32[2,2048]{1,0:T(2,128)S(1)}, f32[2,2048]{1,0:T(2,128)S(1)}, u32[]{:S(2)}, u32[]{:S(2)}) collective-permute-start(f32[2,2048]{1,0:T(2,128)S(1)} %slice.176), channel_id=1, source_target_pairs={{0,256},{8,264},{16,272},{24,280},{32,288},{40,296},{48,304},{56,3... | collective-permute-start | bytes 49160 | tf_op jit(solution)/shard_map/ppermute | solution.py:11
  240.0 3.4 %collective-permute-done.19 = f32[2,2048]{1,0:T(2,128)S(1)} collective-permute-done((f32[2,2048]{1,0:T(2,128)S(1)}, f32[2,2048]{1,0:T(2,128)S(1)}, u32[]{:S(2)}, u32[]{:S(2)}) %collective-permute-start.19) | collective-permute-done | bytes 16416 | tf_op jit(solution)/shard_map/ppermute | solution.py:11
  (136 shorter events, 82.9 us)
Async XLA Ops:
  0.6 104.0 %copy-start = (bf16[128,2048]{1,0:T(8,128)(2,1)S(1)}, bf16[128,2048]{1,0:T(8,128)(2,1)}, u32[]{:S(2)}) copy-start(bf16[128,2048]{1,0:T(8,128)(2,1)} %param.6) | copy-start | bytes 1572868
  0.6 21.3 %collective-permute-start.7 = (s32[128]{0:T(128)}, s32[128]{0:T(128)S(1)}, u32[]{:S(2)}, u32[]{:S(2)}) collective-permute-start(s32[128]{0:T(128)} %param.10), channel_id=1, source_target_pairs={{0,128},{8,136},{16,144},{24,152},{32,160},{40,168},{48,176},{56,1... | collective-permute-start | bytes 1544 | tf_op jit(solution)/shard_map/ppermute | solution.py:11
  6.0 20.9 %collective-permute-start.6 = (s32[128]{0:T(128)}, s32[128]{0:T(128)S(1)}, u32[]{:S(2)}, u32[]{:S(2)}) collective-permute-start(s32[128]{0:T(128)} %param.10), channel_id=1, source_target_pairs={{0,8},{8,0},{16,24},{24,16},{32,40},{40,32},{48,56},{56,48},{64,72... | collective-permute-start | bytes 1544 | tf_op jit(solution)/shard_map/ppermute | solution.py:11
  9.2 94.0 %collective-permute-start.9 = (bf16[128,2048]{0,1:T(8,128)(2,1)S(1)}, bf16[128,2048]{0,1:T(8,128)(2,1)}, u32[]{:S(2)}, u32[]{:S(2)}) collective-permute-start(bf16[128,2048]{0,1:T(8,128)(2,1)S(1)} %copy.40), channel_id=1, source_target_pairs={{0,128},{8,136},{16,144},{24,152},{32,160},{40,168},{48,176},{56,1... | collective-permute-start | bytes 1572872 | tf_op jit(solution)/shard_map/ppermute | solution.py:11
  11.1 92.0 %collective-permute-start.8 = (bf16[128,2048]{0,1:T(8,128)(2,1)S(1)}, bf16[128,2048]{0,1:T(8,128)(2,1)}, u32[]{:S(2)}, u32[]{:S(2)}) collective-permute-start(bf16[128,2048]{0,1:T(8,128)(2,1)S(1)} %copy.40), channel_id=1, source_target_pairs={{0,8},{8,0},{16,24},{24,16},{32,40},{40,32},{48,56},{56,48},{64,72... | collective-permute-start | bytes 1572872 | tf_op jit(solution)/shard_map/ppermute | solution.py:11
  13.6 85.9 %collective-permute-start.10 = (bf16[128,2048]{1,0:T(8,128)(2,1)}, bf16[128,2048]{1,0:T(8,128)(2,1)S(1)}, u32[]{:S(2)}, u32[]{:S(2)}) collective-permute-start(bf16[128,2048]{1,0:T(8,128)(2,1)} %param.8), channel_id=1, source_target_pairs={{0,8},{8,0},{16,24},{24,16},{32,40},{40,32},{48,56},{56,48},{64,72... | collective-permute-start | bytes 1572872 | tf_op jit(solution)/shard_map/ppermute | solution.py:11
  21.9 78.4 %copy-start.8 = (bf16[128,2048]{1,0:T(8,128)(2,1)S(1)}, bf16[128,2048]{1,0:T(8,128)(2,1)}, u32[]{:S(2)}) copy-start(bf16[128,2048]{1,0:T(8,128)(2,1)} %param.8) | copy-start | bytes 1572868
  21.9 78.4 %collective-permute-start.11 = (bf16[128,2048]{1,0:T(8,128)(2,1)}, bf16[128,2048]{1,0:T(8,128)(2,1)S(1)}, u32[]{:S(2)}, u32[]{:S(2)}) collective-permute-start(bf16[128,2048]{1,0:T(8,128)(2,1)} %param.8), channel_id=1, source_target_pairs={{0,128},{8,136},{16,144},{24,152},{32,160},{40,168},{48,176},{56,1... | collective-permute-start | bytes 1572872 | tf_op jit(solution)/shard_map/ppermute | solution.py:11
  26.9 12.1 %collective-permute-start = (bf16[2,2,2048]{2,1,0:T(2,128)(2,1)S(1)}, bf16[2,2,2048]{2,1,0:T(2,128)(2,1)S(1)}, u32[]{:S(2)}, u32[]{:S(2)}) collective-permute-start(bf16[2,2,2048]{2,1,0:T(2,128)(2,1)S(1)} %pad_maximum_fusion.8), channel_id=1, source_target_pairs={{0,256},{8,264},{16,272},{24,280},{32,288},{40,296},{48,304},{56,3... | collective-permute-start | bytes 49160 | tf_op jit(solution)/shard_map/ppermute | solution.py:11
  39.0 32.7 %collective-permute-start.1 = (bf16[2,2,2,2048]{3,2,1,0:T(2,128)(2,1)S(1)}, bf16[2,2,2,2048]{3,2,1,0:T(2,128)(2,1)S(1)}, u32[]{:S(2)}, u32[]{:S(2)}) collective-permute-start(bf16[2,2,2,2048]{3,2,1,0:T(2,128)(2,1)S(1)} %pad_maximum_fusion.7), channel_id=1, source_target_pairs={{0,128},{8,136},{16,144},{24,152},{32,160},{40,168},{48,176},{56,1... | collective-permute-start | bytes 98312 | tf_op jit(solution)/shard_map/ppermute | solution.py:11
  71.9 7.7 %collective-permute-start.2 = (bf16[2,2,2,2,2048]{4,3,2,1,0:T(2,128)(2,1)S(1)}, bf16[2,2,2,2,2048]{4,3,2,1,0:T(2,128)(2,1)S(1)}, u32[]{:S(2)}, u32[]{:S(2)}) collective-permute-start(bf16[2,2,2,2,2048]{4,3,2,1,0:T(2,128)(2,1)S(1)} %pad_maximum_fusion.6), channel_id=1, source_target_pairs={{0,32},{8,40},{16,48},{24,56},{32,0},{40,8},{48,16},{56,24},{64,96... | collective-permute-start | bytes 196616 | tf_op jit(solution)/shard_map/ppermute | solution.py:11
  79.7 6.9 %collective-permute-start.3 = (bf16[2,2,2,2,2,2048]{5,4,3,2,1,0:T(2,128)(2,1)S(1)}, bf16[2,2,2,2,2,2048]{5,4,3,2,1,0:T(2,128)(2,1)S(1)}, u32[]{:S(2)}, u32[]{:S(2)}) collective-permute-start(bf16[2,2,2,2,2,2048]{5,4,3,2,1,0:T(2,128)(2,1)S(1)} %pad_maximum_fusion.5), channel_id=1, source_target_pairs={{0,16},{8,24},{16,0},{24,8},{32,48},{40,56},{48,32},{56,40},{64,80... | collective-permute-start | bytes 393224 | tf_op jit(solution)/shard_map/ppermute | solution.py:11
  87.0 8.3 %collective-permute-start.4 = (bf16[2,2,2,2,2,2,2048]{6,5,4,3,2,1,0:T(2,128)(2,1)S(1)}, bf16[2,2,2,2,2,2,2048]{6,5,4,3,2,1,0:T(2,128)(2,1)S(1)}, u32[]{:S(2)}, u32[]{:S(2)}) collective-permute-start(bf16[2,2,2,2,2,2,2048]{6,5,4,3,2,1,0:T(2,128)(2,1)S(1)} %pad_maximum_fusion.4), channel_id=1, source_target_pairs={{0,64},{8,72},{16,80},{24,88},{32,96},{40,104},{48,112},{56,120},{... | collective-permute-start | bytes 786440 | tf_op jit(solution)/shard_map/ppermute | solution.py:11
  96.8 10.2 %collective-permute-start.5 = (bf16[2,2,2,2,2,2,2,2048]{7,6,5,4,3,2,1,0:T(2,128)(2,1)}, bf16[2,2,2,2,2,2,2,2048]{7,6,5,4,3,2,1,0:T(2,128)(2,1)}, u32[]{:S(2)}, u32[]{:S(2)}) collective-permute-start(bf16[2,2,2,2,2,2,2,2048]{7,6,5,4,3,2,1,0:T(2,128)(2,1)} %pad_maximum_fusion.3), channel_id=1, source_target_pairs={{0,8},{8,0},{16,24},{24,16},{32,40},{40,32},{48,56},{56,48},{64,72... | collective-permute-start | bytes 1572872 | tf_op jit(solution)/shard_map/ppermute | solution.py:11
  130.9 28.5 %collective-permute-start.20 = (f32[64,2048]{1,0:T(8,128)}, f32[64,2048]{1,0:T(8,128)}, u32[]{:S(2)}, u32[]{:S(2)}) collective-permute-start(f32[64,2048]{1,0:T(8,128)} %bitcast.153), channel_id=1, source_target_pairs={{0,8},{8,0},{16,24},{24,16},{32,40},{40,32},{48,56},{56,48},{64,72... | collective-permute-start | bytes 1572872 | tf_op jit(solution)/shard_map/ppermute | solution.py:11
  142.5 20.6 %collective-permute-start.14 = (f32[64,2048]{1,0:T(8,128)}, f32[64,2048]{1,0:T(8,128)}, u32[]{:S(2)}, u32[]{:S(2)}) collective-permute-start(f32[64,2048]{1,0:T(8,128)} %bitcast.154), channel_id=1, source_target_pairs={{0,8},{8,0},{16,24},{24,16},{32,40},{40,32},{48,56},{56,48},{64,72... | collective-permute-start | bytes 1572872 | tf_op jit(solution)/shard_map/ppermute | solution.py:11
  145.7 39.6 %collective-permute-start.27 = (bf16[128,2048]{0,1:T(8,128)(2,1)}, bf16[128,2048]{0,1:T(8,128)(2,1)}, u32[]{:S(2)}, u32[]{:S(2)}) collective-permute-start(bf16[128,2048]{0,1:T(8,128)(2,1)} %bitcast.38), channel_id=1, source_target_pairs={{0,128},{8,136},{16,144},{24,152},{32,160},{40,168},{48,176},{56,1... | collective-permute-start | bytes 1572872 | tf_op jit(solution)/shard_map/ppermute | solution.py:11
  150.5 37.0 %collective-permute-start.26 = (bf16[128,2048]{0,1:T(8,128)(2,1)}, bf16[128,2048]{0,1:T(8,128)(2,1)}, u32[]{:S(2)}, u32[]{:S(2)}) collective-permute-start(bf16[128,2048]{0,1:T(8,128)(2,1)} %bitcast.36), channel_id=1, source_target_pairs={{0,8},{8,0},{16,24},{24,16},{32,40},{40,32},{48,56},{56,48},{64,72... | collective-permute-start | bytes 1572872 | tf_op jit(solution)/shard_map/ppermute | solution.py:11
  157.1 39.5 %collective-permute-start.13 = (bf16[128,2048]{0,1:T(8,128)(2,1)}, bf16[128,2048]{0,1:T(8,128)(2,1)}, u32[]{:S(2)}, u32[]{:S(2)}) collective-permute-start(bf16[128,2048]{0,1:T(8,128)(2,1)} %bitcast.30), channel_id=1, source_target_pairs={{0,128},{8,136},{16,144},{24,152},{32,160},{40,168},{48,176},{56,1... | collective-permute-start | bytes 1572872 | tf_op jit(solution)/shard_map/ppermute | solution.py:11
  159.3 38.6 %collective-permute-start.12 = (bf16[128,2048]{0,1:T(8,128)(2,1)}, bf16[128,2048]{0,1:T(8,128)(2,1)}, u32[]{:S(2)}, u32[]{:S(2)}) collective-permute-start(bf16[128,2048]{0,1:T(8,128)(2,1)} %bitcast.28), channel_id=1, source_target_pairs={{0,8},{8,0},{16,24},{24,16},{32,40},{40,32},{48,56},{56,48},{64,72... | collective-permute-start | bytes 1572872 | tf_op jit(solution)/shard_map/ppermute | solution.py:11
  163.1 43.8 %collective-permute-start.21 = (f32[32,2048]{1,0:T(8,128)}, f32[32,2048]{1,0:T(8,128)S(1)}, u32[]{:S(2)}, u32[]{:S(2)}) collective-permute-start(f32[32,2048]{1,0:T(8,128)} %slice.180), channel_id=1, source_target_pairs={{0,64},{8,72},{16,80},{24,88},{32,96},{40,104},{48,112},{56,120},{... | collective-permute-start | bytes 786440 | tf_op jit(solution)/shard_map/ppermute | solution.py:11
  166.1 21.4 %copy-start.3 = (f32[64,2048]{1,0:T(8,128)}, f32[64,2048]{1,0:T(8,128)S(1)}, u32[]{:S(2)}) copy-start(f32[64,2048]{1,0:T(8,128)S(1)} %bitcast_add_fusion.1) | copy-start | bytes 1572868
  185.3 25.1 %collective-permute-start.15 = (f32[32,2048]{1,0:T(8,128)}, f32[32,2048]{1,0:T(8,128)}, u32[]{:S(2)}, u32[]{:S(2)}) collective-permute-start(f32[32,2048]{1,0:T(8,128)} %slice.168), channel_id=1, source_target_pairs={{0,64},{8,72},{16,80},{24,88},{32,96},{40,104},{48,112},{56,120},{... | collective-permute-start | bytes 786440 | tf_op jit(solution)/shard_map/ppermute | solution.py:11
  205.3 38.0 %copy-start.11 = (s32[2]{0:T(128)S(1)}, s32[2]{0:T(128)}, u32[]{:S(2)}) copy-start(s32[2]{0:T(128)} %param.11) | copy-start | bytes 28
  207.0 7.3 %collective-permute-start.22 = (f32[16,2048]{1,0:T(8,128)S(1)}, f32[16,2048]{1,0:T(8,128)S(1)}, u32[]{:S(2)}, u32[]{:S(2)}) collective-permute-start(f32[16,2048]{1,0:T(8,128)S(1)} %slice.182), channel_id=1, source_target_pairs={{0,16},{8,24},{16,0},{24,8},{32,48},{40,56},{48,32},{56,40},{64,80... | collective-permute-start | bytes 393224 | tf_op jit(solution)/shard_map/ppermute | solution.py:11
  211.5 7.8 %collective-permute-start.16 = (f32[16,2048]{1,0:T(8,128)S(1)}, f32[16,2048]{1,0:T(8,128)S(1)}, u32[]{:S(2)}, u32[]{:S(2)}) collective-permute-start(f32[16,2048]{1,0:T(8,128)S(1)} %slice.170), channel_id=1, source_target_pairs={{0,16},{8,24},{16,0},{24,8},{32,48},{40,56},{48,32},{56,40},{64,80... | collective-permute-start | bytes 393224 | tf_op jit(solution)/shard_map/ppermute | solution.py:11
  214.4 8.9 %collective-permute-start.23 = (f32[8,2048]{1,0:T(8,128)S(1)}, f32[8,2048]{1,0:T(8,128)S(1)}, u32[]{:S(2)}, u32[]{:S(2)}) collective-permute-start(f32[8,2048]{1,0:T(8,128)S(1)} %slice.184), channel_id=1, source_target_pairs={{0,32},{8,40},{16,48},{24,56},{32,0},{40,8},{48,16},{56,24},{64,96... | collective-permute-start | bytes 196616 | tf_op jit(solution)/shard_map/ppermute | solution.py:11
  219.3 7.7 %collective-permute-start.17 = (f32[8,2048]{1,0:T(8,128)S(1)}, f32[8,2048]{1,0:T(8,128)S(1)}, u32[]{:S(2)}, u32[]{:S(2)}) collective-permute-start(f32[8,2048]{1,0:T(8,128)S(1)} %slice.172), channel_id=1, source_target_pairs={{0,32},{8,40},{16,48},{24,56},{32,0},{40,8},{48,16},{56,24},{64,96... | collective-permute-start | bytes 196616 | tf_op jit(solution)/shard_map/ppermute | solution.py:11
  223.3 6.8 %collective-permute-start.24 = (f32[4,2048]{1,0:T(4,128)S(1)}, f32[4,2048]{1,0:T(4,128)S(1)}, u32[]{:S(2)}, u32[]{:S(2)}) collective-permute-start(f32[4,2048]{1,0:T(4,128)S(1)} %slice.186), channel_id=1, source_target_pairs={{0,128},{8,136},{16,144},{24,152},{32,160},{40,168},{48,176},{56,1... | collective-permute-start | bytes 98312 | tf_op jit(solution)/shard_map/ppermute | solution.py:11
  227.0 6.7 %collective-permute-start.18 = (f32[4,2048]{1,0:T(4,128)S(1)}, f32[4,2048]{1,0:T(4,128)S(1)}, u32[]{:S(2)}, u32[]{:S(2)}) collective-permute-start(f32[4,2048]{1,0:T(4,128)S(1)} %slice.174), channel_id=1, source_target_pairs={{0,128},{8,136},{16,144},{24,152},{32,160},{40,168},{48,176},{56,1... | collective-permute-start | bytes 98312 | tf_op jit(solution)/shard_map/ppermute | solution.py:11
  230.1 9.8 %collective-permute-start.25 = (f32[2,2048]{1,0:T(2,128)S(1)}, f32[2,2048]{1,0:T(2,128)S(1)}, u32[]{:S(2)}, u32[]{:S(2)}) collective-permute-start(f32[2,2048]{1,0:T(2,128)S(1)} %slice.188), channel_id=1, source_target_pairs={{0,256},{8,264},{16,272},{24,280},{32,288},{40,296},{48,304},{56,3... | collective-permute-start | bytes 49160 | tf_op jit(solution)/shard_map/ppermute | solution.py:11
  233.8 9.5 %collective-permute-start.19 = (f32[2,2048]{1,0:T(2,128)S(1)}, f32[2,2048]{1,0:T(2,128)S(1)}, u32[]{:S(2)}, u32[]{:S(2)}) collective-permute-start(f32[2,2048]{1,0:T(2,128)S(1)} %slice.176), channel_id=1, source_target_pairs={{0,256},{8,264},{16,272},{24,280},{32,288},{40,296},{48,304},{56,3... | collective-permute-start | bytes 49160 | tf_op jit(solution)/shard_map/ppermute | solution.py:11
  (8 other events, 41.6 us)

commit v3 on v2

--- a/solution.py
+++ b/solution.py
@@ -11,12 +11,11 @@
     return lax.ppermute(array, axis, [(i, i ^ 1 << stride) for i in range(lax.axis_size(axis))])
 
 
-def local(queries, keys, values, cotangent, documents, global_offsets):
+def body(queries, keys, values, cotangent, documents, global_offsets):
     rows_here, columns = queries.shape
     head_size = columns // HEADS
     temper = head_size ** (-0.5)
     shards = lax.axis_size("seq")
-    myself = lax.axis_index("seq")
     log_shards = shards.bit_length() - 1
     level_bits = [step * (log_shards - 2) // (LEVELS - 1) for step in range(LEVELS)]
 
@@ -25,10 +24,21 @@
 
     per_block = global_offsets.shape[0]
     picked = jnp.stack([keys[global_offsets], values[global_offsets]], 0)
-    gather_bits = [5, 4, 2, 1, 3, 0] if log_shards == 6 else list(range(log_shards))[::-1]
+    gather_bits = list(range(log_shards))[::-1]
+    z_steps = min(3, log_shards)
+    doc_columns = 128
+    packed = jnp.concatenate(
+        [keys, values, jnp.broadcast_to(documents.astype(keys.dtype)[:, None], (rows_here, doc_columns))],
+        1,
+    )
     gathered = picked
-    for bit in gather_bits:
+    arrived = {}
+    for step, bit in enumerate(gather_bits):
         gathered = jnp.stack([gathered, from_partner(gathered, "seq", bit)], 0)
+        if step == z_steps - 1:
+            gathered, held = lax.optimization_barrier((gathered, packed))
+            for level_bit in level_bits:
+                arrived[level_bit] = from_partner(held, "seq", level_bit)
     owner_bits = gather_bits[::-1]
     global_count = shards * per_block
     gathered = gathered.reshape((shards,) + picked.shape)
@@ -48,9 +58,10 @@
     value_list = [values]
     mask_list = [documents[:, None] == documents[None, :]]
     for level_bit in level_bits:
-        partner_keys, partner_values, partner_docs = from_partner(
-            (keys, values, documents), "seq", level_bit
-        )
+        came = arrived[level_bit]
+        partner_keys = came[:, :columns]
+        partner_values = came[:, columns : 2 * columns]
+        partner_docs = came[:, 2 * columns].astype(documents.dtype)
         key_list.append(partner_keys)
         value_list.append(partner_values)
         mask_list.append(documents[:, None] == partner_docs[None, :])
@@ -104,14 +115,19 @@
     for level, level_bit in enumerate(level_bits):
         lower = (level + 1) * rows_here
         upper = (level + 2) * rows_here
-        back_keys, back_values = from_partner(
-            (
-                key_term[lower:upper].reshape(rows_here, columns).astype(jnp.bfloat16),
-                value_term[lower:upper].reshape(rows_here, columns).astype(jnp.bfloat16),
+        back = from_partner(
+            jnp.concatenate(
+                [
+                    key_term[lower:upper].reshape(rows_here, columns).astype(jnp.bfloat16),
+                    value_term[lower:upper].reshape(rows_here, columns).astype(jnp.bfloat16),
+                ],
+                1,
             ),
             "seq",
             level_bit,
         )
+        back_keys = back[:, :columns]
+        back_values = back[:, columns:]
         key_sum = key_sum + split(back_keys).astype(jnp.float32)
         value_sum = value_sum + split(back_values).astype(jnp.float32)
     global_product = jnp.einsum(
@@ -127,14 +143,12 @@
     value_part = jnp.einsum(
         "htg,thd->ghd", global_prob_b, dout_heads, preferred_element_type=jnp.float32
     )
-    def scatter_rows(part):
-        part = part.reshape(global_count, columns)
-        for bit in owner_bits:
-            half = part.shape[0] // 2
-            part = part[:half] + from_partner(part[half:], "seq", bit)
-        return part
-
-    owned = jnp.concatenate([scatter_rows(key_part), scatter_rows(value_part)], 1)
+    owned = jnp.concatenate(
+        [key_part.reshape(global_count, columns), value_part.reshape(global_count, columns)], 1
+    )
+    for bit in owner_bits:
+        half = owned.shape[0] // 2
+        owned = owned[:half] + from_partner(owned[half:], "seq", bit)
     placement = (jnp.arange(rows_here, dtype=jnp.int32)[:, None] == global_offsets[None, :]).astype(
         jnp.float32
     )
@@ -164,4 +178,4 @@
         P(("dp", "seq"), None),
         P(("dp", "seq"), None),
     )
-    return jax.shard_map(local, mesh=mesh, in_specs=in_specs, out_specs=out_specs, check_vma=False)
+    return jax.shard_map(body, mesh=mesh, in_specs=in_specs, out_specs=out_specs, check_vma=False)

time: 247 us -> 231 us (0.935)
  starting transfers between devices: 118 us -> 58.3 us
  waiting for transfers between devices: 48.6 us -> 87.9 us
  other arithmetic: 22.2 us -> 25.5 us
    ppermute x28 -> x16, starting transfers between devices: 118 us -> 58.3 us  [from_partner(): lax.ppermute(array, axis, [(i, i ^ 1 << stride) for i in range(lax.axis_s...]
    ppermute x28 -> x16, waiting for transfers between devices: 48.6 us -> 87.9 us  [from_partner(): lax.ppermute(array, axis, [(i, i ^ 1 << stride) for i in range(lax.axis_s...]
    slice x16 -> x13, local copies, waits for them, and re-layouts: 6.65 us -> 13.2 us  [the longest x3 4.47 us: body(): key_term[lower:upper].reshape(rows_here, columns).astype(jnp.bfloat16)]
    unnamed x31 -> x36, local copies, waits for them, and re-layouts: 13.3 us -> 7.48 us
    concatenate x3 -> x6, other arithmetic: 2.56 us -> 8.01 us  [the longest x2 4.42 us: body(): jnp.concatenate([key_term[lower:upper].reshape(rows_here, columns).astype...]
    reshape x2 -> x5, local copies, waits for them, and re-layouts: 1.9 us -> 5.33 us  [the longest x1 2.63 us: body(): key_part.reshape(global_count, columns)]
    convert_element_type x2, local copies, waits for them, and re-layouts: 3.46 us -> 0.42 us  [body(): key_sum = key_sum + split(back_keys).astype(jnp.float32)]
    mul x0 -> x1, local copies, waits for them, and re-layouts: none -> 2.58 us  [body(): temper * jnp.einsum('htg,thd->ghd', global_slope, query_heads, preferred_...]
  transfers between devices with their start and end apart: 28 -> 16, of which waited for: 11 -> 10; matrix products, arithmetic and copies ran while one was open for 21% -> 18% of each run, Pallas kernels for 0% -> 0%
where the time goes in v3:
time: 231 us; the launch traced here: 229 us
  waiting for transfers between devices  87.9 us (38%)
  starting transfers between devices  58.3 us (25%)
  local copies, waits for them, and re-layouts  37.2 us (16%)
  other arithmetic  25.5 us (11%)
  matrix products  19 us (8%)
    ppermute x16, waiting for transfers between devices, from_partner(): lax.ppermute(array, axis, [(i, i ^ 1 << stride) for i in range(lax.axis_s...  87.9 us
    ppermute x16, starting transfers between devices, from_partner(): lax.ppermute(array, axis, [(i, i ^ 1 << stride) for i in range(lax.axis_s...  58.3 us
    unnamed x36, local copies, waits for them, and re-layouts  7.48 us
    another operation x11, other arithmetic, body(): gathered = jnp.stack([gathered, from_partner(gathered, 'seq', bit)], 0)  6.13 us
  transfers between devices with their start and end apart: 16, of which 10 were waited for; matrix products, arithmetic and copies ran while one was open for 18% of the time, Pallas kernels for 0%

profile of v3, /device:TPU:24, one launch (start us, length us, event | category | flops | bytes accessed | tf_op | source)
XLA Modules:
  0.0 229.1 jit_solution(17654046699807230468)
XLA Ops:
  4.7 9.1 %collective-permute-start = (bf16[2,2,2048]{2,1,0:T(2,128)(2,1)S(1)}, bf16[2,2,2048]{2,1,0:T(2,128)(2,1)S(1)}, u32[]{:S(2)}, u32[]{:S(2)}) collective-permute-start(bf16[2,2,2048]{2,1,0:T(2,128)(2,1)S(1)} %pad_maximum_fusion.12), channel_id=1, source_target_pairs={{0,256},{8,264},{16,272},{24,280},{32,288},{40,296},{48,304},{56,3... | collective-permute-start | bytes 49160 | tf_op jit(solution)/shard_map/ppermute | solution.py:11
  18.4 5.2 %collective-permute-start.1 = (bf16[2,2,2,2048]{3,2,1,0:T(2,128)(2,1)S(1)}, bf16[2,2,2,2048]{3,2,1,0:T(2,128)(2,1)S(1)}, u32[]{:S(2)}, u32[]{:S(2)}) collective-permute-start(bf16[2,2,2,2048]{3,2,1,0:T(2,128)(2,1)S(1)} %pad_maximum_fusion.11), channel_id=1, source_target_pairs={{0,128},{8,136},{16,144},{24,152},{32,160},{40,168},{48,176},{56,1... | collective-permute-start | bytes 98312 | tf_op jit(solution)/shard_map/ppermute | solution.py:11
  23.7 2.2 collective-permute-done.1
  25.9 3.5 %collective-permute-start.2 = (bf16[2,2,2,2,2048]{4,3,2,1,0:T(2,128)(2,1)S(1)}, bf16[2,2,2,2,2048]{4,3,2,1,0:T(2,128)(2,1)S(1)}, u32[]{:S(2)}, u32[]{:S(2)}) collective-permute-start(bf16[2,2,2,2,2048]{4,3,2,1,0:T(2,128)(2,1)S(1)} %pad_maximum_fusion.10), channel_id=1, source_target_pairs={{0,64},{8,72},{16,80},{24,88},{32,96},{40,104},{48,112},{56,120},{... | collective-permute-start | bytes 196616 | tf_op jit(solution)/shard_map/ppermute | solution.py:11
  29.5 2.6 %collective-permute-done.2 = bf16[2,2,2,2,2048]{4,3,2,1,0:T(2,128)(2,1)S(1)} collective-permute-done((bf16[2,2,2,2,2048]{4,3,2,1,0:T(2,128)(2,1)S(1)}, bf16[2,2,2,2,2048]{4,3,2,1,0:T(2,128)(2,1)S(1)}, u32[]{:S(2)}, u32[]{:S(2)}) %collective-permute-start.2) | collective-permute-done | bytes 65568 | tf_op jit(solution)/shard_map/ppermute | solution.py:11
  32.3 4.9 %collective-permute-start.3 = (bf16[2,2,2,2,2,2048]{5,4,3,2,1,0:T(2,128)(2,1)S(1)}, bf16[2,2,2,2,2,2048]{5,4,3,2,1,0:T(2,128)(2,1)S(1)}, u32[]{:S(2)}, u32[]{:S(2)}) collective-permute-start(bf16[2,2,2,2,2,2048]{5,4,3,2,1,0:T(2,128)(2,1)S(1)} %pad_maximum_fusion.9), channel_id=1, source_target_pairs={{0,32},{8,40},{16,48},{24,56},{32,0},{40,8},{48,16},{56,24},{64,96... | collective-permute-start | bytes 393224 | tf_op jit(solution)/shard_map/ppermute | solution.py:11
  37.2 3.4 %collective-permute-done.3 = bf16[2,2,2,2,2,2048]{5,4,3,2,1,0:T(2,128)(2,1)S(1)} collective-permute-done((bf16[2,2,2,2,2,2048]{5,4,3,2,1,0:T(2,128)(2,1)S(1)}, bf16[2,2,2,2,2,2048]{5,4,3,2,1,0:T(2,128)(2,1)S(1)}, u32[]{:S(2)}, u32[]{:S(2)}) %collective-permute-start.3) | collective-permute-done | bytes 131104 | tf_op jit(solution)/shard_map/ppermute | solution.py:11
  41.0 3.4 %collective-permute-start.4 = (bf16[2,2,2,2,2,2,2048]{6,5,4,3,2,1,0:T(2,128)(2,1)S(1)}, bf16[2,2,2,2,2,2,2048]{6,5,4,3,2,1,0:T(2,128)(2,1)S(1)}, u32[]{:S(2)}, u32[]{:S(2)}) collective-permute-start(bf16[2,2,2,2,2,2,2048]{6,5,4,3,2,1,0:T(2,128)(2,1)S(1)} %pad_maximum_fusion.8), channel_id=1, source_target_pairs={{0,16},{8,24},{16,0},{24,8},{32,48},{40,56},{48,32},{56,40},{64,80... | collective-permute-start | bytes 786440 | tf_op jit(solution)/shard_map/ppermute | solution.py:11
  44.8 4.5 %collective-permute-done.4 = bf16[2,2,2,2,2,2,2048]{6,5,4,3,2,1,0:T(2,128)(2,1)S(1)} collective-permute-done((bf16[2,2,2,2,2,2,2048]{6,5,4,3,2,1,0:T(2,128)(2,1)S(1)}, bf16[2,2,2,2,2,2,2048]{6,5,4,3,2,1,0:T(2,128)(2,1)S(1)}, u32[]{:S(2)}, u32[]{:S(2)}) %collective-permute-start.4) | collective-permute-done | bytes 262176 | tf_op jit(solution)/shard_map/ppermute | solution.py:11
  54.3 4.5 %collective-permute-start.7 = (bf16[128,4224]{0,1:T(8,128)(2,1)}, bf16[128,4224]{0,1:T(8,128)(2,1)}, u32[]{:S(2)}, u32[]{:S(2)}) collective-permute-start(bf16[128,4224]{0,1:T(8,128)(2,1)} %pad_maximum_fusion.2), channel_id=1, source_target_pairs={{0,128},{8,136},{16,144},{24,152},{32,160},{40,168},{48,176},{56,1... | collective-permute-start | bytes 3244040 | tf_op jit(solution)/shard_map/ppermute | solution.py:11
  58.8 2.3 %collective-permute-start.6 = (bf16[128,4224]{0,1:T(8,128)(2,1)}, bf16[128,4224]{0,1:T(8,128)(2,1)}, u32[]{:S(2)}, u32[]{:S(2)}) collective-permute-start(bf16[128,4224]{0,1:T(8,128)(2,1)} %pad_maximum_fusion.2), channel_id=1, source_target_pairs={{0,8},{8,0},{16,24},{24,16},{32,40},{40,32},{48,56},{56,48},{64,72... | collective-permute-start | bytes 3244040 | tf_op jit(solution)/shard_map/ppermute | solution.py:11
  61.8 2.6 %pad_maximum_fusion.4 = bf16[2,2,2,2,2,2,2,2,2048]{8,7,6,5,4,3,2,1,0:T(2,128)(2,1)S(1)} fusion(bf16[1,2,2,2,2,2,2,2,2048]{8,7,6,5,4,3,2,1,0:T(2,128)(2,1)} %bitcast.13, bf16[1,2,2,2,2,2,2,2,2048]{8,7,6,5,4,3,2,1,0:T(2,128)(2,1)S(1)} %fusion.81), kind=kLoop, calls=%fused_computation.41 | loop fusion | flops 524288 | bytes 2097152 | tf_op jit(solution)/shard_map/stack | solution.py:37
  69.4 37.5 %collective-permute-done.7 = bf16[128,4224]{0,1:T(8,128)(2,1)} collective-permute-done((bf16[128,4224]{0,1:T(8,128)(2,1)}, bf16[128,4224]{0,1:T(8,128)(2,1)}, u32[]{:S(2)}, u32[]{:S(2)}) %collective-permute-start.7) | collective-permute-done | bytes 1081376 | tf_op jit(solution)/shard_map/ppermute | solution.py:11
  118.5 2.6 %fusion = bf16[16,128,384]{1,2,0:T(8,128)(2,1)} fusion(bf16[384,16,128]{0,2,1:T(8,128)(2,1)S(1)} %bitcast.145, bf16[128,16,128]{0,2,1:T(8,128)(2,1)S(1)} %bitcast.153, f32[16,128]{1,0:T(8,128)S(1)} %bitcast.168, f32[16,128]{1,0:T(8,128)S(1)} %add.56, f32[16,128]{1,0:T(8,128)S(1)} %max.7, f32[16,384,128]{2,1,0:T(8,128)S(1)} %get-tuple-element.46, ...), kind=kOutput, calls=%fused_computation.3 | convolution fusion | flops 206831616 | bytes 6889472 | tf_op jit(solution)/shard_map/thd,uhd->htu/dot_general | solution.py:101
  121.0 3.2 %fusion.60 = (bf16[384,16,128]{0,2,1:T(8,128)(2,1)}, f32[384,16,128]{0,2,1:T(8,128)}) fusion(bf16[128,16,128]{0,2,1:T(8,128)(2,1)S(1)} %bitcast.154, f32[16,128]{1,0:T(8,128)S(1)} %add.56, f32[16,128]{1,0:T(8,128)S(1)} %max.7, f32[16,384,128]{2,1,0:T(8,128)S(1)} %get-tuple-element.46, pred[128,384]{0,1:T(8,128)(4,1)S(1)} %pad_add_fusion), kind=kOutput, calls=%fused_computation.112 | convolution fusion | flops 206045184 | bytes 8454144 | tf_op jit(solution)/shard_map/htu,thd->uhd/dot_general | solution.py:111
  126.0 2.6 %fusion.4 = f32[128,16,128]{2,0,1:T(8,128)} fusion(bf16[16,128,128]{1,2,0:T(8,128)(2,1)} %fusion.11, bf16[128,16,128]{0,2,1:T(8,128)(2,1)S(1)} %bitcast.129), kind=kOutput, calls=%fused_computation.16 | convolution fusion | flops 67371008 | bytes 2097152 | tf_op jit(solution)/shard_map/htg,thd->ghd/dot_general | solution.py:140
  128.6 2.6 %copy.160 = f32[128,16,128]{0,2,1:T(8,128)} copy(f32[128,16,128]{2,0,1:T(8,128)} %fusion.4) | data formatting | bytes 2097152 | tf_op jit(solution)/shard_map/mul | solution.py:140
  131.2 2.6 %copy.163 = f32[128,2048]{1,0:T(8,128)} copy(f32[128,2048]{0,1:T(8,128)} %bitcast.133) | data formatting | bytes 2097152 | tf_op jit(solution)/shard_map/reshape | solution.py:147
  133.8 2.4 %fusion.54 = (bf16[128,16,128]{0,2,1:T(8,128)(2,1)}, bf16[128,16,128]{0,2,1:T(8,128)(2,1)}) fusion(bf16[384,16,128]{0,2,1:T(8,128)(2,1)} %get-tuple-element.49), kind=kLoop, calls=%fused_computation.106 | loop fusion | bytes 2097152 | tf_op jit(solution)/shard_map/slice | solution.py:122
  140.3 2.3 fusion.61
  144.9 2.1 copy.154
  147.0 2.3 %pad_maximum_fusion.6 = bf16[128,4096]{0,1:T(8,128)(2,1)} fusion(bf16[128,2048]{0,1:T(8,128)(2,1)} %bitcast.143, bf16[128,2048]{0,1:T(8,128)(2,1)} %bitcast.139), kind=kLoop, calls=%fused_computation.43 | loop fusion | flops 2097152 | bytes 2097152 | tf_op jit(solution)/shard_map/concatenate | solution.py:119
  155.8 3.5 %collective-permute-start.11 = (f32[32,4096]{1,0:T(8,128)}, f32[32,4096]{1,0:T(8,128)S(1)}, u32[]{:S(2)}, u32[]{:S(2)}) collective-permute-start(f32[32,4096]{1,0:T(8,128)} %slice.154), channel_id=1, source_target_pairs={{0,16},{8,24},{16,0},{24,8},{32,48},{40,56},{48,32},{56,40},{64,80... | collective-permute-start | bytes 1572872 | tf_op jit(solution)/shard_map/ppermute | solution.py:11
  162.4 2.1 collective-permute-start.8
  164.5 7.9 %collective-permute-done.11 = f32[32,4096]{1,0:T(8,128)S(1)} collective-permute-done((f32[32,4096]{1,0:T(8,128)}, f32[32,4096]{1,0:T(8,128)S(1)}, u32[]{:S(2)}, u32[]{:S(2)}) %collective-permute-start.11) | collective-permute-done | bytes 524320 | tf_op jit(solution)/shard_map/ppermute | solution.py:11
  173.5 4.9 %collective-permute-start.12 = (f32[16,4096]{1,0:T(8,128)S(1)}, f32[16,4096]{1,0:T(8,128)S(1)}, u32[]{:S(2)}, u32[]{:S(2)}) collective-permute-start(f32[16,4096]{1,0:T(8,128)S(1)} %slice.156), channel_id=1, source_target_pairs={{0,32},{8,40},{16,48},{24,56},{32,0},{40,8},{48,16},{56,24},{64,96... | collective-permute-start | bytes 786440 | tf_op jit(solution)/shard_map/ppermute | solution.py:11
  178.4 22.0 %collective-permute-done.9 = bf16[128,4096]{0,1:T(8,128)(2,1)} collective-permute-done((bf16[128,4096]{0,1:T(8,128)(2,1)}, bf16[128,4096]{0,1:T(8,128)(2,1)}, u32[]{:S(2)}, u32[]{:S(2)}) %collective-permute-start.9) | collective-permute-done | bytes 1048608 | tf_op jit(solution)/shard_map/ppermute | solution.py:11
  205.7 3.9 %collective-permute-done.13 = f32[8,4096]{1,0:T(8,128)S(1)} collective-permute-done((f32[8,4096]{1,0:T(8,128)}, f32[8,4096]{1,0:T(8,128)S(1)}, u32[]{:S(2)}, u32[]{:S(2)}) %collective-permute-start.13) | collective-permute-done | bytes 131104 | tf_op jit(solution)/shard_map/ppermute | solution.py:11
  209.6 2.4 %collective-permute-start.14 = (f32[4,4096]{1,0:T(4,128)S(1)}, f32[4,4096]{1,0:T(4,128)S(1)}, u32[]{:S(2)}, u32[]{:S(2)}) collective-permute-start(f32[4,4096]{1,0:T(4,128)S(1)} %slice.160), channel_id=1, source_target_pairs={{0,128},{8,136},{16,144},{24,152},{32,160},{40,168},{48,176},{56,1... | collective-permute-start | bytes 196616 | tf_op jit(solution)/shard_map/ppermute | solution.py:11
  212.0 2.4 %fusion.18 = f32[128,16,128]{2,0,1:T(8,128)} fusion(f32[128,16,128]{2,0,1:T(8,128)S(1)} %copy.155, f32[128,16,128]{2,0,1:T(8,128)S(1)} %copy.153, f32[384,16,128]{2,0,1:T(8,128)} %get-tuple-element.52), kind=kLoop, calls=%fused_computation.40 | loop fusion | flops 524288 | bytes 4194304 | tf_op jit(solution)/shard_map/add | solution.py:131
  214.4 2.8 %collective-permute-done.14 = f32[4,4096]{1,0:T(4,128)S(1)} collective-permute-done((f32[4,4096]{1,0:T(4,128)S(1)}, f32[4,4096]{1,0:T(4,128)S(1)}, u32[]{:S(2)}, u32[]{:S(2)}) %collective-permute-start.14) | collective-permute-done | bytes 65568 | tf_op jit(solution)/shard_map/ppermute | solution.py:11
  217.2 4.9 %collective-permute-start.15 = (f32[2,4096]{1,0:T(2,128)S(1)}, f32[2,4096]{1,0:T(2,128)S(1)}, u32[]{:S(2)}, u32[]{:S(2)}) collective-permute-start(f32[2,4096]{1,0:T(2,128)S(1)} %slice.162), channel_id=1, source_target_pairs={{0,256},{8,264},{16,272},{24,280},{32,288},{40,296},{48,304},{56,3... | collective-permute-start | bytes 98312 | tf_op jit(solution)/shard_map/ppermute | solution.py:11
  (116 shorter events, 62.8 us)
Async XLA Ops:
  4.7 13.6 %collective-permute-start = (bf16[2,2,2048]{2,1,0:T(2,128)(2,1)S(1)}, bf16[2,2,2048]{2,1,0:T(2,128)(2,1)S(1)}, u32[]{:S(2)}, u32[]{:S(2)}) collective-permute-start(bf16[2,2,2048]{2,1,0:T(2,128)(2,1)S(1)} %pad_maximum_fusion.12), channel_id=1, source_target_pairs={{0,256},{8,264},{16,272},{24,280},{32,288},{40,296},{48,304},{56,3... | collective-permute-start | bytes 49160 | tf_op jit(solution)/shard_map/ppermute | solution.py:11
  15.1 37.9 %copy-start.8 = (bf16[128,2048]{1,0:T(8,128)(2,1)S(1)}, bf16[128,2048]{1,0:T(8,128)(2,1)}, u32[]{:S(2)}) copy-start(bf16[128,2048]{1,0:T(8,128)(2,1)} %param.9) | copy-start | bytes 1572868
  16.5 37.5 %copy-start.9 = (bf16[128,2048]{1,0:T(8,128)(2,1)S(1)}, bf16[128,2048]{1,0:T(8,128)(2,1)}, u32[]{:S(2)}) copy-start(bf16[128,2048]{1,0:T(8,128)(2,1)} %param.6) | copy-start | bytes 1572868
  18.4 7.4 %collective-permute-start.1 = (bf16[2,2,2,2048]{3,2,1,0:T(2,128)(2,1)S(1)}, bf16[2,2,2,2048]{3,2,1,0:T(2,128)(2,1)S(1)}, u32[]{:S(2)}, u32[]{:S(2)}) collective-permute-start(bf16[2,2,2,2048]{3,2,1,0:T(2,128)(2,1)S(1)} %pad_maximum_fusion.11), channel_id=1, source_target_pairs={{0,128},{8,136},{16,144},{24,152},{32,160},{40,168},{48,176},{56,1... | collective-permute-start | bytes 98312 | tf_op jit(solution)/shard_map/ppermute | solution.py:11
  25.9 6.2 %collective-permute-start.2 = (bf16[2,2,2,2,2048]{4,3,2,1,0:T(2,128)(2,1)S(1)}, bf16[2,2,2,2,2048]{4,3,2,1,0:T(2,128)(2,1)S(1)}, u32[]{:S(2)}, u32[]{:S(2)}) collective-permute-start(bf16[2,2,2,2,2048]{4,3,2,1,0:T(2,128)(2,1)S(1)} %pad_maximum_fusion.10), channel_id=1, source_target_pairs={{0,64},{8,72},{16,80},{24,88},{32,96},{40,104},{48,112},{56,120},{... | collective-permute-start | bytes 196616 | tf_op jit(solution)/shard_map/ppermute | solution.py:11
  32.3 8.4 %collective-permute-start.3 = (bf16[2,2,2,2,2,2048]{5,4,3,2,1,0:T(2,128)(2,1)S(1)}, bf16[2,2,2,2,2,2048]{5,4,3,2,1,0:T(2,128)(2,1)S(1)}, u32[]{:S(2)}, u32[]{:S(2)}) collective-permute-start(bf16[2,2,2,2,2,2048]{5,4,3,2,1,0:T(2,128)(2,1)S(1)} %pad_maximum_fusion.9), channel_id=1, source_target_pairs={{0,32},{8,40},{16,48},{24,56},{32,0},{40,8},{48,16},{56,24},{64,96... | collective-permute-start | bytes 393224 | tf_op jit(solution)/shard_map/ppermute | solution.py:11
  41.0 8.3 %collective-permute-start.4 = (bf16[2,2,2,2,2,2,2048]{6,5,4,3,2,1,0:T(2,128)(2,1)S(1)}, bf16[2,2,2,2,2,2,2048]{6,5,4,3,2,1,0:T(2,128)(2,1)S(1)}, u32[]{:S(2)}, u32[]{:S(2)}) collective-permute-start(bf16[2,2,2,2,2,2,2048]{6,5,4,3,2,1,0:T(2,128)(2,1)S(1)} %pad_maximum_fusion.8), channel_id=1, source_target_pairs={{0,16},{8,24},{16,0},{24,8},{32,48},{40,56},{48,32},{56,40},{64,80... | collective-permute-start | bytes 786440 | tf_op jit(solution)/shard_map/ppermute | solution.py:11
  50.8 11.0 %collective-permute-start.5 = (bf16[2,2,2,2,2,2,2,2048]{7,6,5,4,3,2,1,0:T(2,128)(2,1)}, bf16[2,2,2,2,2,2,2,2048]{7,6,5,4,3,2,1,0:T(2,128)(2,1)}, u32[]{:S(2)}, u32[]{:S(2)}) collective-permute-start(bf16[2,2,2,2,2,2,2,2048]{7,6,5,4,3,2,1,0:T(2,128)(2,1)} %pad_maximum_fusion.7), channel_id=1, source_target_pairs={{0,8},{8,0},{16,24},{24,16},{32,40},{40,32},{48,56},{56,48},{64,72... | collective-permute-start | bytes 1572872 | tf_op jit(solution)/shard_map/ppermute | solution.py:11
  54.3 52.5 %collective-permute-start.7 = (bf16[128,4224]{0,1:T(8,128)(2,1)}, bf16[128,4224]{0,1:T(8,128)(2,1)}, u32[]{:S(2)}, u32[]{:S(2)}) collective-permute-start(bf16[128,4224]{0,1:T(8,128)(2,1)} %pad_maximum_fusion.2), channel_id=1, source_target_pairs={{0,128},{8,136},{16,144},{24,152},{32,160},{40,168},{48,176},{56,1... | collective-permute-start | bytes 3244040 | tf_op jit(solution)/shard_map/ppermute | solution.py:11
  58.8 48.8 %collective-permute-start.6 = (bf16[128,4224]{0,1:T(8,128)(2,1)}, bf16[128,4224]{0,1:T(8,128)(2,1)}, u32[]{:S(2)}, u32[]{:S(2)}) collective-permute-start(bf16[128,4224]{0,1:T(8,128)(2,1)} %pad_maximum_fusion.2), channel_id=1, source_target_pairs={{0,8},{8,0},{16,24},{24,16},{32,40},{40,32},{48,56},{56,48},{64,72... | collective-permute-start | bytes 3244040 | tf_op jit(solution)/shard_map/ppermute | solution.py:11
  66.0 42.2 %copy-start.13 = (s32[128]{0:T(128)S(1)}, s32[128]{0:T(128)}, u32[]{:S(2)}) copy-start(s32[128]{0:T(128)} %param.10) | copy-start | bytes 1540
  67.8 43.0 %copy-start.3 = (bf16[128,16,128]{0,2,1:T(8,128)(2,1)}, bf16[128,16,128]{0,2,1:T(8,128)(2,1)S(1)}, u32[]{:S(2)}) copy-start(bf16[128,16,128]{0,2,1:T(8,128)(2,1)S(1)} %copy.146) | copy-start | bytes 1572868
  112.1 1.0 copy-start.10
  112.8 1.9 copy-start.12
  133.8 6.4 %copy-start.1 = (bf16[16,128,384]{1,2,0:T(8,128)(2,1)S(1)}, bf16[16,128,384]{1,2,0:T(8,128)(2,1)}, u32[]{:S(2)}) copy-start(bf16[16,128,384]{1,2,0:T(8,128)(2,1)} %fusion) | copy-start | bytes 4718596
  138.3 15.0 %collective-permute-start.10 = (f32[64,4096]{1,0:T(8,128)}, f32[64,4096]{1,0:T(8,128)}, u32[]{:S(2)}, u32[]{:S(2)}) collective-permute-start(f32[64,4096]{1,0:T(8,128)} %pad_maximum_fusion.3), channel_id=1, source_target_pairs={{0,8},{8,0},{16,24},{24,16},{32,40},{40,32},{48,56},{56,48},{64,72... | collective-permute-start | bytes 3145736 | tf_op jit(solution)/shard_map/ppermute | solution.py:11
  147.0 6.4 %copy-start = (f32[128,2048]{1,0:T(8,128)S(1)}, f32[128,2048]{1,0:T(8,128)}, u32[]{:S(2)}) copy-start(f32[128,2048]{1,0:T(8,128)} %copy.163) | copy-start | bytes 3145732
  149.3 51.1 %collective-permute-start.9 = (bf16[128,4096]{0,1:T(8,128)(2,1)}, bf16[128,4096]{0,1:T(8,128)(2,1)}, u32[]{:S(2)}, u32[]{:S(2)}) collective-permute-start(bf16[128,4096]{0,1:T(8,128)(2,1)} %pad_maximum_fusion.6), channel_id=1, source_target_pairs={{0,128},{8,136},{16,144},{24,152},{32,160},{40,168},{48,176},{56,1... | collective-permute-start | bytes 3145736 | tf_op jit(solution)/shard_map/ppermute | solution.py:11
  153.3 6.0 %copy-start.4 = (bf16[128,16,128]{0,2,1:T(8,128)(2,1)S(1)}, bf16[128,16,128]{0,2,1:T(8,128)(2,1)}, u32[]{:S(2)}) copy-start(bf16[128,16,128]{0,2,1:T(8,128)(2,1)} %copy-done.3) | copy-start | bytes 1572868
  153.3 6.0 %copy-start.6 = (bf16[16,128,128]{1,2,0:T(8,128)(2,1)S(1)}, bf16[16,128,128]{1,2,0:T(8,128)(2,1)}, u32[]{:S(2)}) copy-start(bf16[16,128,128]{1,2,0:T(8,128)(2,1)} %fusion.11) | copy-start | bytes 1572868
  153.3 6.3 %copy-start.2 = (bf16[16,128,384]{1,2,0:T(8,128)(2,1)S(1)}, bf16[16,128,384]{1,2,0:T(8,128)(2,1)}, u32[]{:S(2)}) copy-start(bf16[16,128,384]{1,2,0:T(8,128)(2,1)} %fusion) | copy-start | bytes 4718596
  154.9 5.4 %copy-start.5 = (f32[64,4096]{1,0:T(8,128)}, f32[64,4096]{1,0:T(8,128)S(1)}, u32[]{:S(2)}) copy-start(f32[64,4096]{1,0:T(8,128)S(1)} %fusion.14) | copy-start | bytes 3145732
  155.8 4.5 %copy-start.11 = (bf16[16,128,128]{2,1,0:T(8,128)(2,1)S(1)}, bf16[16,128,128]{2,1,0:T(8,128)(2,1)}, u32[]{:S(2)}) copy-start(bf16[16,128,128]{2,1,0:T(8,128)(2,1)} %get-tuple-element.48) | copy-start | bytes 1572868
  155.8 16.6 %collective-permute-start.11 = (f32[32,4096]{1,0:T(8,128)}, f32[32,4096]{1,0:T(8,128)S(1)}, u32[]{:S(2)}, u32[]{:S(2)}) collective-permute-start(f32[32,4096]{1,0:T(8,128)} %slice.154), channel_id=1, source_target_pairs={{0,16},{8,24},{16,0},{24,8},{32,48},{40,56},{48,32},{56,40},{64,80... | collective-permute-start | bytes 1572872 | tf_op jit(solution)/shard_map/ppermute | solution.py:11
  162.4 42.0 %collective-permute-start.8 = (bf16[128,4096]{0,1:T(8,128)(2,1)}, bf16[128,4096]{0,1:T(8,128)(2,1)S(1)}, u32[]{:S(2)}, u32[]{:S(2)}) collective-permute-start(bf16[128,4096]{0,1:T(8,128)(2,1)} %pad_maximum_fusion.5), channel_id=1, source_target_pairs={{0,8},{8,0},{16,24},{24,16},{32,40},{40,32},{48,56},{56,48},{64,72... | collective-permute-start | bytes 3145736 | tf_op jit(solution)/shard_map/ppermute | solution.py:11
  173.5 28.3 %collective-permute-start.12 = (f32[16,4096]{1,0:T(8,128)S(1)}, f32[16,4096]{1,0:T(8,128)S(1)}, u32[]{:S(2)}, u32[]{:S(2)}) collective-permute-start(f32[16,4096]{1,0:T(8,128)S(1)} %slice.156), channel_id=1, source_target_pairs={{0,32},{8,40},{16,48},{24,56},{32,0},{40,8},{48,16},{56,24},{64,96... | collective-permute-start | bytes 786440 | tf_op jit(solution)/shard_map/ppermute | solution.py:11
  202.5 7.1 %collective-permute-start.13 = (f32[8,4096]{1,0:T(8,128)}, f32[8,4096]{1,0:T(8,128)S(1)}, u32[]{:S(2)}, u32[]{:S(2)}) collective-permute-start(f32[8,4096]{1,0:T(8,128)} %slice.158), channel_id=1, source_target_pairs={{0,64},{8,72},{16,80},{24,88},{32,96},{40,104},{48,112},{56,120},{... | collective-permute-start | bytes 393224 | tf_op jit(solution)/shard_map/ppermute | solution.py:11
  205.7 16.4 %copy-start.7 = (bf16[128,2048]{0,1:T(8,128)(2,1)S(1)}, bf16[128,2048]{0,1:T(8,128)(2,1)}, u32[]{:S(2)}) copy-start(bf16[128,2048]{0,1:T(8,128)(2,1)} %get-tuple-element.34) | copy-start | bytes 1572868
  209.6 7.5 %collective-permute-start.14 = (f32[4,4096]{1,0:T(4,128)S(1)}, f32[4,4096]{1,0:T(4,128)S(1)}, u32[]{:S(2)}, u32[]{:S(2)}) collective-permute-start(f32[4,4096]{1,0:T(4,128)S(1)} %slice.160), channel_id=1, source_target_pairs={{0,128},{8,136},{16,144},{24,152},{32,160},{40,168},{48,176},{56,1... | collective-permute-start | bytes 196616 | tf_op jit(solution)/shard_map/ppermute | solution.py:11
  217.2 9.8 %collective-permute-start.15 = (f32[2,4096]{1,0:T(2,128)S(1)}, f32[2,4096]{1,0:T(2,128)S(1)}, u32[]{:S(2)}, u32[]{:S(2)}) collective-permute-start(f32[2,4096]{1,0:T(2,128)S(1)} %slice.162), channel_id=1, source_target_pairs={{0,256},{8,264},{16,272},{24,280},{32,288},{40,296},{48,304},{56,3... | collective-permute-start | bytes 98312 | tf_op jit(solution)/shard_map/ppermute | solution.py:11
  223.5 3.4 %copy-start.14 = (s32[2]{0:T(128)S(1)}, s32[2]{0:T(128)}, u32[]{:S(2)}) copy-start(s32[2]{0:T(128)} %param.11) | copy-start | bytes 28

commit v4 on v3

--- a/solution.py
+++ b/solution.py
@@ -115,19 +115,15 @@
     for level, level_bit in enumerate(level_bits):
         lower = (level + 1) * rows_here
         upper = (level + 2) * rows_here
-        back = from_partner(
-            jnp.concatenate(
-                [
-                    key_term[lower:upper].reshape(rows_here, columns).astype(jnp.bfloat16),
-                    value_term[lower:upper].reshape(rows_here, columns).astype(jnp.bfloat16),
-                ],
-                1,
-            ),
-            "seq",
-            level_bit,
-        )
-        back_keys = back[:, :columns]
-        back_values = back[:, columns:]
+        key_back = key_term[lower:upper].reshape(rows_here, columns).astype(jnp.bfloat16)
+        value_back = value_term[lower:upper].reshape(rows_here, columns).astype(jnp.bfloat16)
+        if level_bit == 0:
+            back = from_partner(jnp.concatenate([key_back, value_back], 1), "seq", level_bit)
+            back_keys = back[:, :columns]
+            back_values = back[:, columns:]
+        else:
+            back_values = from_partner(value_back, "seq", level_bit)
+            back_keys = from_partner(key_back, "seq", level_bit)
         key_sum = key_sum + split(back_keys).astype(jnp.float32)
         value_sum = value_sum + split(back_values).astype(jnp.float32)
     global_product = jnp.einsum(

time: 231 us -> 218 us (0.944)
  waiting for transfers between devices: 87.9 us -> 71.8 us
  starting transfers between devices: 58.3 us -> 68.1 us
  local copies, waits for them, and re-layouts: 37.2 us -> 32.6 us
  other arithmetic: 25.5 us -> 22.3 us
    ppermute x16 -> x17, waiting for transfers between devices: 87.9 us -> 71.8 us  [from_partner(): lax.ppermute(array, axis, [(i, i ^ 1 << stride) for i in range(lax.axis_s...]
    ppermute x16 -> x17, starting transfers between devices: 58.3 us -> 68.1 us  [from_partner(): lax.ppermute(array, axis, [(i, i ^ 1 << stride) for i in range(lax.axis_s...]
    concatenate x2 -> x1, other arithmetic: 4.42 us -> 1.03 us  [body(): jnp.concatenate([key_back, value_back], 1)]
  transfers between devices with their start and end apart: 16 -> 17, of which waited for: 10 -> 9; matrix products, arithmetic and copies ran while one was open for 18% -> 19% of each run, Pallas kernels for 0% -> 0%
where the time goes in v4:
time: 218 us; the launch traced here: 216 us
  waiting for transfers between devices  71.8 us (33%)
  starting transfers between devices  68.1 us (31%)
  local copies, waits for them, and re-layouts  32.6 us (15%)
  other arithmetic  22.3 us (10%)
  matrix products  20.3 us (9%)
    ppermute x17, waiting for transfers between devices, from_partner(): lax.ppermute(array, axis, [(i, i ^ 1 << stride) for i in range(lax.axis_s...  71.8 us
    ppermute x17, starting transfers between devices, from_partner(): lax.ppermute(array, axis, [(i, i ^ 1 << stride) for i in range(lax.axis_s...  68.1 us
    unnamed x36, local copies, waits for them, and re-layouts  7.03 us
    another operation x11, other arithmetic, body(): gathered = jnp.stack([gathered, from_partner(gathered, 'seq', bit)], 0)  6.13 us
    dot_general x1, matrix products, body(): jnp.einsum('htu,thd->uhd', probs_b, dout_heads, preferred_element_type=jn...  4.7 us
  transfers between devices with their start and end apart: 17, of which 9 were waited for; matrix products, arithmetic and copies ran while one was open for 19% of the time, Pallas kernels for 0%

profile of v4, /device:TPU:24, one launch (start us, length us, event | category | flops | bytes accessed | tf_op | source)
XLA Modules:
  0.0 216.4 jit_solution(16812449305676905972)
XLA Ops:
  4.7 9.1 %collective-permute-start = (bf16[2,2,2048]{2,1,0:T(2,128)(2,1)S(1)}, bf16[2,2,2048]{2,1,0:T(2,128)(2,1)S(1)}, u32[]{:S(2)}, u32[]{:S(2)}) collective-permute-start(bf16[2,2,2048]{2,1,0:T(2,128)(2,1)S(1)} %pad_maximum_fusion.11), channel_id=1, source_target_pairs={{0,256},{8,264},{16,272},{24,280},{32,288},{40,296},{48,304},{56,3... | collective-permute-start | bytes 49160 | tf_op jit(solution)/shard_map/ppermute | solution.py:11
  18.4 5.2 %collective-permute-start.1 = (bf16[2,2,2,2048]{3,2,1,0:T(2,128)(2,1)S(1)}, bf16[2,2,2,2048]{3,2,1,0:T(2,128)(2,1)S(1)}, u32[]{:S(2)}, u32[]{:S(2)}) collective-permute-start(bf16[2,2,2,2048]{3,2,1,0:T(2,128)(2,1)S(1)} %pad_maximum_fusion.10), channel_id=1, source_target_pairs={{0,128},{8,136},{16,144},{24,152},{32,160},{40,168},{48,176},{56,1... | collective-permute-start | bytes 98312 | tf_op jit(solution)/shard_map/ppermute | solution.py:11
  23.7 2.2 %collective-permute-done.1 = bf16[2,2,2,2048]{3,2,1,0:T(2,128)(2,1)S(1)} collective-permute-done((bf16[2,2,2,2048]{3,2,1,0:T(2,128)(2,1)S(1)}, bf16[2,2,2,2048]{3,2,1,0:T(2,128)(2,1)S(1)}, u32[]{:S(2)}, u32[]{:S(2)}) %collective-permute-start.1) | collective-permute-done | bytes 32800 | tf_op jit(solution)/shard_map/ppermute | solution.py:11
  25.9 3.5 %collective-permute-start.2 = (bf16[2,2,2,2,2048]{4,3,2,1,0:T(2,128)(2,1)S(1)}, bf16[2,2,2,2,2048]{4,3,2,1,0:T(2,128)(2,1)S(1)}, u32[]{:S(2)}, u32[]{:S(2)}) collective-permute-start(bf16[2,2,2,2,2048]{4,3,2,1,0:T(2,128)(2,1)S(1)} %pad_maximum_fusion.9), channel_id=1, source_target_pairs={{0,64},{8,72},{16,80},{24,88},{32,96},{40,104},{48,112},{56,120},{... | collective-permute-start | bytes 196616 | tf_op jit(solution)/shard_map/ppermute | solution.py:11
  29.5 2.6 %collective-permute-done.2 = bf16[2,2,2,2,2048]{4,3,2,1,0:T(2,128)(2,1)S(1)} collective-permute-done((bf16[2,2,2,2,2048]{4,3,2,1,0:T(2,128)(2,1)S(1)}, bf16[2,2,2,2,2048]{4,3,2,1,0:T(2,128)(2,1)S(1)}, u32[]{:S(2)}, u32[]{:S(2)}) %collective-permute-start.2) | collective-permute-done | bytes 65568 | tf_op jit(solution)/shard_map/ppermute | solution.py:11
  32.3 4.9 %collective-permute-start.3 = (bf16[2,2,2,2,2,2048]{5,4,3,2,1,0:T(2,128)(2,1)S(1)}, bf16[2,2,2,2,2,2048]{5,4,3,2,1,0:T(2,128)(2,1)S(1)}, u32[]{:S(2)}, u32[]{:S(2)}) collective-permute-start(bf16[2,2,2,2,2,2048]{5,4,3,2,1,0:T(2,128)(2,1)S(1)} %pad_maximum_fusion.8), channel_id=1, source_target_pairs={{0,32},{8,40},{16,48},{24,56},{32,0},{40,8},{48,16},{56,24},{64,96... | collective-permute-start | bytes 393224 | tf_op jit(solution)/shard_map/ppermute | solution.py:11
  37.2 3.4 %collective-permute-done.3 = bf16[2,2,2,2,2,2048]{5,4,3,2,1,0:T(2,128)(2,1)S(1)} collective-permute-done((bf16[2,2,2,2,2,2048]{5,4,3,2,1,0:T(2,128)(2,1)S(1)}, bf16[2,2,2,2,2,2048]{5,4,3,2,1,0:T(2,128)(2,1)S(1)}, u32[]{:S(2)}, u32[]{:S(2)}) %collective-permute-start.3) | collective-permute-done | bytes 131104 | tf_op jit(solution)/shard_map/ppermute | solution.py:11
  41.0 3.4 %collective-permute-start.4 = (bf16[2,2,2,2,2,2,2048]{6,5,4,3,2,1,0:T(2,128)(2,1)S(1)}, bf16[2,2,2,2,2,2,2048]{6,5,4,3,2,1,0:T(2,128)(2,1)S(1)}, u32[]{:S(2)}, u32[]{:S(2)}) collective-permute-start(bf16[2,2,2,2,2,2,2048]{6,5,4,3,2,1,0:T(2,128)(2,1)S(1)} %pad_maximum_fusion.7), channel_id=1, source_target_pairs={{0,16},{8,24},{16,0},{24,8},{32,48},{40,56},{48,32},{56,40},{64,80... | collective-permute-start | bytes 786440 | tf_op jit(solution)/shard_map/ppermute | solution.py:11
  44.8 4.5 %collective-permute-done.4 = bf16[2,2,2,2,2,2,2048]{6,5,4,3,2,1,0:T(2,128)(2,1)S(1)} collective-permute-done((bf16[2,2,2,2,2,2,2048]{6,5,4,3,2,1,0:T(2,128)(2,1)S(1)}, bf16[2,2,2,2,2,2,2048]{6,5,4,3,2,1,0:T(2,128)(2,1)S(1)}, u32[]{:S(2)}, u32[]{:S(2)}) %collective-permute-start.4) | collective-permute-done | bytes 262176 | tf_op jit(solution)/shard_map/ppermute | solution.py:11
  54.3 4.5 %collective-permute-start.7 = (bf16[128,4224]{0,1:T(8,128)(2,1)}, bf16[128,4224]{0,1:T(8,128)(2,1)}, u32[]{:S(2)}, u32[]{:S(2)}) collective-permute-start(bf16[128,4224]{0,1:T(8,128)(2,1)} %pad_maximum_fusion.2), channel_id=1, source_target_pairs={{0,128},{8,136},{16,144},{24,152},{32,160},{40,168},{48,176},{56,1... | collective-permute-start | bytes 3244040 | tf_op jit(solution)/shard_map/ppermute | solution.py:11
  58.8 2.3 %collective-permute-start.6 = (bf16[128,4224]{0,1:T(8,128)(2,1)}, bf16[128,4224]{0,1:T(8,128)(2,1)}, u32[]{:S(2)}, u32[]{:S(2)}) collective-permute-start(bf16[128,4224]{0,1:T(8,128)(2,1)} %pad_maximum_fusion.2), channel_id=1, source_target_pairs={{0,8},{8,0},{16,24},{24,16},{32,40},{40,32},{48,56},{56,48},{64,72... | collective-permute-start | bytes 3244040 | tf_op jit(solution)/shard_map/ppermute | solution.py:11
  61.8 2.6 %pad_maximum_fusion.4 = bf16[2,2,2,2,2,2,2,2,2048]{8,7,6,5,4,3,2,1,0:T(2,128)(2,1)S(1)} fusion(bf16[1,2,2,2,2,2,2,2,2048]{8,7,6,5,4,3,2,1,0:T(2,128)(2,1)} %bitcast.13, bf16[1,2,2,2,2,2,2,2,2048]{8,7,6,5,4,3,2,1,0:T(2,128)(2,1)S(1)} %fusion.80), kind=kLoop, calls=%fused_computation.41 | loop fusion | flops 524288 | bytes 2097152 | tf_op jit(solution)/shard_map/stack | solution.py:37
  67.5 39.3 %collective-permute-done.7 = bf16[128,4224]{0,1:T(8,128)(2,1)} collective-permute-done((bf16[128,4224]{0,1:T(8,128)(2,1)}, bf16[128,4224]{0,1:T(8,128)(2,1)}, u32[]{:S(2)}, u32[]{:S(2)}) %collective-permute-start.7) | collective-permute-done | bytes 1081376 | tf_op jit(solution)/shard_map/ppermute | solution.py:11
  115.5 2.1 multiply_reduce_fusion
  118.8 2.6 %fusion = bf16[16,128,384]{1,2,0:T(8,128)(2,1)} fusion(bf16[384,16,128]{0,2,1:T(8,128)(2,1)S(1)} %bitcast.141, bf16[128,16,128]{0,2,1:T(8,128)(2,1)S(1)} %bitcast.150, f32[16,128]{1,0:T(8,128)S(1)} %bitcast.166, f32[16,128]{1,0:T(8,128)S(1)} %add.56, f32[16,128]{1,0:T(8,128)S(1)} %max.7, f32[16,384,128]{2,1,0:T(8,128)S(1)} %get-tuple-element.44, ...), kind=kOutput, calls=%fused_computation.3 | convolution fusion | flops 206831616 | bytes 6889472 | tf_op jit(solution)/shard_map/thd,uhd->htu/dot_general | solution.py:101
  122.9 2.5 %fusion.4 = f32[128,16,128]{2,0,1:T(8,128)} fusion(bf16[16,128,128]{1,2,0:T(8,128)(2,1)} %fusion.11, bf16[128,16,128]{0,2,1:T(8,128)(2,1)S(1)} %bitcast.129), kind=kOutput, calls=%fused_computation.16 | convolution fusion | flops 67371008 | bytes 2097152 | tf_op jit(solution)/shard_map/htg,thd->ghd/dot_general | solution.py:136
  125.4 2.5 %copy.160 = f32[128,16,128]{0,2,1:T(8,128)} copy(f32[128,16,128]{2,0,1:T(8,128)} %fusion.4) | data formatting | bytes 2097152 | tf_op jit(solution)/shard_map/mul | solution.py:136
  128.0 2.5 %copy.163 = f32[128,2048]{1,0:T(8,128)} copy(f32[128,2048]{0,1:T(8,128)} %bitcast.133) | data formatting | bytes 2097152 | tf_op jit(solution)/shard_map/reshape | solution.py:143
  130.5 2.2 %pad_maximum_fusion.3 = f32[64,4096]{1,0:T(8,128)} fusion(f32[128,2048]{1,0:T(8,128)S(1)} %copy.182, f32[128,2048]{1,0:T(8,128)} %copy.163), kind=kLoop, calls=%fused_computation.38 | loop fusion | flops 262144 | bytes 3145728 | tf_op jit(solution)/shard_map/concatenate | solution.py:142
  134.6 2.2 %fusion.60 = (bf16[384,16,128]{2,0,1:T(8,128)(2,1)S(1)}, f32[384,16,128]{2,0,1:T(8,128)}) fusion(bf16[16,128,384]{1,2,0:T(8,128)(2,1)S(1)} %copy-done.2, bf16[128,16,128]{0,2,1:T(8,128)(2,1)S(1)} %bitcast.130), kind=kOutput, calls=%fused_computation.111 | convolution fusion | flops 202899456 | bytes 6815744 | tf_op jit(solution)/shard_map/htu,thd->uhd/dot_general | solution.py:108
  142.9 4.7 %fusion.59 = (bf16[384,16,128]{0,2,1:T(8,128)(2,1)S(1)}, f32[384,16,128]{0,2,1:T(8,128)}) fusion(bf16[128,16,128]{0,2,1:T(8,128)(2,1)} %bitcast.147, f32[16,128]{1,0:T(8,128)S(1)} %add.56, f32[16,128]{1,0:T(8,128)S(1)} %max.7, f32[16,384,128]{2,1,0:T(8,128)} %copy-done, pred[128,384]{0,1:T(8,128)(4,1)S(1)} %pad_add_fusion), kind=kOutput, calls=%fused_computation.110 | convolution fusion | flops 206045184 | bytes 8454144 | tf_op jit(solution)/shard_map/htu,thd->uhd/dot_general | solution.py:111
  150.1 3.4 %collective-permute-start.11 = (f32[32,4096]{1,0:T(8,128)S(1)}, f32[32,4096]{1,0:T(8,128)S(1)}, u32[]{:S(2)}, u32[]{:S(2)}) collective-permute-start(f32[32,4096]{1,0:T(8,128)S(1)} %slice.144), channel_id=1, source_target_pairs={{0,16},{8,24},{16,0},{24,8},{32,48},{40,56},{48,32},{56,40},{64,80... | collective-permute-start | bytes 1572872 | tf_op jit(solution)/shard_map/ppermute | solution.py:11
  154.5 2.1 collective-permute-start.8
  157.0 9.3 %collective-permute-done.11 = f32[32,4096]{1,0:T(8,128)S(1)} collective-permute-done((f32[32,4096]{1,0:T(8,128)S(1)}, f32[32,4096]{1,0:T(8,128)S(1)}, u32[]{:S(2)}, u32[]{:S(2)}) %collective-permute-start.11) | collective-permute-done | bytes 524320 | tf_op jit(solution)/shard_map/ppermute | solution.py:11
  166.4 4.9 %collective-permute-start.12 = (f32[16,4096]{1,0:T(8,128)S(1)}, f32[16,4096]{1,0:T(8,128)}, u32[]{:S(2)}, u32[]{:S(2)}) collective-permute-start(f32[16,4096]{1,0:T(8,128)S(1)} %slice.146), channel_id=1, source_target_pairs={{0,32},{8,40},{16,48},{24,56},{32,0},{40,8},{48,16},{56,24},{64,96... | collective-permute-start | bytes 786440 | tf_op jit(solution)/shard_map/ppermute | solution.py:11
  174.0 4.5 %collective-permute-start.16 = (bf16[128,2048]{0,1:T(8,128)(2,1)}, bf16[128,2048]{0,1:T(8,128)(2,1)}, u32[]{:S(2)}, u32[]{:S(2)}) collective-permute-start(bf16[128,2048]{0,1:T(8,128)(2,1)} %bitcast.153), channel_id=1, source_target_pairs={{0,128},{8,136},{16,144},{24,152},{32,160},{40,168},{48,176},{56,1... | collective-permute-start | bytes 1572872 | tf_op jit(solution)/shard_map/ppermute | solution.py:11
  181.5 3.3 %collective-permute-start.13 = (f32[8,4096]{1,0:T(8,128)}, f32[8,4096]{1,0:T(8,128)S(1)}, u32[]{:S(2)}, u32[]{:S(2)}) collective-permute-start(f32[8,4096]{1,0:T(8,128)} %slice.148), channel_id=1, source_target_pairs={{0,64},{8,72},{16,80},{24,88},{32,96},{40,104},{48,112},{56,120},{... | collective-permute-start | bytes 393224 | tf_op jit(solution)/shard_map/ppermute | solution.py:11
  186.3 5.9 %collective-permute-done.13 = f32[8,4096]{1,0:T(8,128)S(1)} collective-permute-done((f32[8,4096]{1,0:T(8,128)}, f32[8,4096]{1,0:T(8,128)S(1)}, u32[]{:S(2)}, u32[]{:S(2)}) %collective-permute-start.13) | collective-permute-done | bytes 131104 | tf_op jit(solution)/shard_map/ppermute | solution.py:11
  192.2 6.2 %collective-permute-start.14 = (f32[4,4096]{1,0:T(4,128)S(1)}, f32[4,4096]{1,0:T(4,128)S(1)}, u32[]{:S(2)}, u32[]{:S(2)}) collective-permute-start(f32[4,4096]{1,0:T(4,128)S(1)} %slice.150), channel_id=1, source_target_pairs={{0,128},{8,136},{16,144},{24,152},{32,160},{40,168},{48,176},{56,1... | collective-permute-start | bytes 196616 | tf_op jit(solution)/shard_map/ppermute | solution.py:11
  198.4 2.4 %fusion.18 = f32[128,16,128]{2,0,1:T(8,128)} fusion(f32[128,16,128]{2,0,1:T(8,128)S(1)} %copy.155, f32[128,16,128]{2,0,1:T(8,128)S(1)} %copy.153, f32[384,16,128]{2,0,1:T(8,128)} %get-tuple-element.50), kind=kLoop, calls=%fused_computation.40 | loop fusion | flops 524288 | bytes 4194304 | tf_op jit(solution)/shard_map/add | solution.py:127
  200.8 3.6 %collective-permute-done.14 = f32[4,4096]{1,0:T(4,128)S(1)} collective-permute-done((f32[4,4096]{1,0:T(4,128)S(1)}, f32[4,4096]{1,0:T(4,128)S(1)}, u32[]{:S(2)}, u32[]{:S(2)}) %collective-permute-start.14) | collective-permute-done | bytes 65568 | tf_op jit(solution)/shard_map/ppermute | solution.py:11
  204.4 4.9 %collective-permute-start.15 = (f32[2,4096]{1,0:T(2,128)S(1)}, f32[2,4096]{1,0:T(2,128)S(1)}, u32[]{:S(2)}, u32[]{:S(2)}) collective-permute-start(f32[2,4096]{1,0:T(2,128)S(1)} %slice.152), channel_id=1, source_target_pairs={{0,256},{8,264},{16,272},{24,280},{32,288},{40,296},{48,304},{56,3... | collective-permute-start | bytes 98312 | tf_op jit(solution)/shard_map/ppermute | solution.py:11
  (116 shorter events, 55.9 us)
Async XLA Ops:
  4.7 13.6 %collective-permute-start = (bf16[2,2,2048]{2,1,0:T(2,128)(2,1)S(1)}, bf16[2,2,2048]{2,1,0:T(2,128)(2,1)S(1)}, u32[]{:S(2)}, u32[]{:S(2)}) collective-permute-start(bf16[2,2,2048]{2,1,0:T(2,128)(2,1)S(1)} %pad_maximum_fusion.11), channel_id=1, source_target_pairs={{0,256},{8,264},{16,272},{24,280},{32,288},{40,296},{48,304},{56,3... | collective-permute-start | bytes 49160 | tf_op jit(solution)/shard_map/ppermute | solution.py:11
  15.1 37.9 %copy-start.8 = (bf16[128,2048]{1,0:T(8,128)(2,1)S(1)}, bf16[128,2048]{1,0:T(8,128)(2,1)}, u32[]{:S(2)}) copy-start(bf16[128,2048]{1,0:T(8,128)(2,1)} %param.9) | copy-start | bytes 1572868
  16.5 37.5 %copy-start.9 = (bf16[128,2048]{1,0:T(8,128)(2,1)S(1)}, bf16[128,2048]{1,0:T(8,128)(2,1)}, u32[]{:S(2)}) copy-start(bf16[128,2048]{1,0:T(8,128)(2,1)} %param.6) | copy-start | bytes 1572868
  18.4 7.4 %collective-permute-start.1 = (bf16[2,2,2,2048]{3,2,1,0:T(2,128)(2,1)S(1)}, bf16[2,2,2,2048]{3,2,1,0:T(2,128)(2,1)S(1)}, u32[]{:S(2)}, u32[]{:S(2)}) collective-permute-start(bf16[2,2,2,2048]{3,2,1,0:T(2,128)(2,1)S(1)} %pad_maximum_fusion.10), channel_id=1, source_target_pairs={{0,128},{8,136},{16,144},{24,152},{32,160},{40,168},{48,176},{56,1... | collective-permute-start | bytes 98312 | tf_op jit(solution)/shard_map/ppermute | solution.py:11
  25.9 6.2 %collective-permute-start.2 = (bf16[2,2,2,2,2048]{4,3,2,1,0:T(2,128)(2,1)S(1)}, bf16[2,2,2,2,2048]{4,3,2,1,0:T(2,128)(2,1)S(1)}, u32[]{:S(2)}, u32[]{:S(2)}) collective-permute-start(bf16[2,2,2,2,2048]{4,3,2,1,0:T(2,128)(2,1)S(1)} %pad_maximum_fusion.9), channel_id=1, source_target_pairs={{0,64},{8,72},{16,80},{24,88},{32,96},{40,104},{48,112},{56,120},{... | collective-permute-start | bytes 196616 | tf_op jit(solution)/shard_map/ppermute | solution.py:11
  32.3 8.4 %collective-permute-start.3 = (bf16[2,2,2,2,2,2048]{5,4,3,2,1,0:T(2,128)(2,1)S(1)}, bf16[2,2,2,2,2,2048]{5,4,3,2,1,0:T(2,128)(2,1)S(1)}, u32[]{:S(2)}, u32[]{:S(2)}) collective-permute-start(bf16[2,2,2,2,2,2048]{5,4,3,2,1,0:T(2,128)(2,1)S(1)} %pad_maximum_fusion.8), channel_id=1, source_target_pairs={{0,32},{8,40},{16,48},{24,56},{32,0},{40,8},{48,16},{56,24},{64,96... | collective-permute-start | bytes 393224 | tf_op jit(solution)/shard_map/ppermute | solution.py:11
  41.0 8.3 %collective-permute-start.4 = (bf16[2,2,2,2,2,2,2048]{6,5,4,3,2,1,0:T(2,128)(2,1)S(1)}, bf16[2,2,2,2,2,2,2048]{6,5,4,3,2,1,0:T(2,128)(2,1)S(1)}, u32[]{:S(2)}, u32[]{:S(2)}) collective-permute-start(bf16[2,2,2,2,2,2,2048]{6,5,4,3,2,1,0:T(2,128)(2,1)S(1)} %pad_maximum_fusion.7), channel_id=1, source_target_pairs={{0,16},{8,24},{16,0},{24,8},{32,48},{40,56},{48,32},{56,40},{64,80... | collective-permute-start | bytes 786440 | tf_op jit(solution)/shard_map/ppermute | solution.py:11
  50.8 11.0 %collective-permute-start.5 = (bf16[2,2,2,2,2,2,2,2048]{7,6,5,4,3,2,1,0:T(2,128)(2,1)}, bf16[2,2,2,2,2,2,2,2048]{7,6,5,4,3,2,1,0:T(2,128)(2,1)}, u32[]{:S(2)}, u32[]{:S(2)}) collective-permute-start(bf16[2,2,2,2,2,2,2,2048]{7,6,5,4,3,2,1,0:T(2,128)(2,1)} %pad_maximum_fusion.6), channel_id=1, source_target_pairs={{0,8},{8,0},{16,24},{24,16},{32,40},{40,32},{48,56},{56,48},{64,72... | collective-permute-start | bytes 1572872 | tf_op jit(solution)/shard_map/ppermute | solution.py:11
  54.3 52.5 %collective-permute-start.7 = (bf16[128,4224]{0,1:T(8,128)(2,1)}, bf16[128,4224]{0,1:T(8,128)(2,1)}, u32[]{:S(2)}, u32[]{:S(2)}) collective-permute-start(bf16[128,4224]{0,1:T(8,128)(2,1)} %pad_maximum_fusion.2), channel_id=1, source_target_pairs={{0,128},{8,136},{16,144},{24,152},{32,160},{40,168},{48,176},{56,1... | collective-permute-start | bytes 3244040 | tf_op jit(solution)/shard_map/ppermute | solution.py:11
  58.8 48.8 %collective-permute-start.6 = (bf16[128,4224]{0,1:T(8,128)(2,1)}, bf16[128,4224]{0,1:T(8,128)(2,1)}, u32[]{:S(2)}, u32[]{:S(2)}) collective-permute-start(bf16[128,4224]{0,1:T(8,128)(2,1)} %pad_maximum_fusion.2), channel_id=1, source_target_pairs={{0,8},{8,0},{16,24},{24,16},{32,40},{40,32},{48,56},{56,48},{64,72... | collective-permute-start | bytes 3244040 | tf_op jit(solution)/shard_map/ppermute | solution.py:11
  65.2 43.0 %copy-start.13 = (s32[128]{0:T(128)S(1)}, s32[128]{0:T(128)}, u32[]{:S(2)}) copy-start(s32[128]{0:T(128)} %param.10) | copy-start | bytes 1540
  66.0 44.9 %copy-start.4 = (bf16[128,16,128]{0,2,1:T(8,128)(2,1)}, bf16[128,16,128]{0,2,1:T(8,128)(2,1)S(1)}, u32[]{:S(2)}) copy-start(bf16[128,16,128]{0,2,1:T(8,128)(2,1)S(1)} %copy.146) | copy-start | bytes 1572868
  112.1 6.7 %copy-start = (f32[16,384,128]{2,1,0:T(8,128)}, f32[16,384,128]{2,1,0:T(8,128)S(1)}, u32[]{:S(2)}) copy-start(f32[16,384,128]{2,1,0:T(8,128)S(1)} %get-tuple-element.44) | copy-start | bytes 9437188
  112.2 1.4 copy-start.10
  112.8 2.2 %copy-start.12 = (bf16[128,16,128]{2,1,0:T(8,128)(2,1)S(1)}, bf16[128,16,128]{2,1,0:T(8,128)(2,1)}, u32[]{:S(2)}) copy-start(bf16[128,16,128]{2,1,0:T(8,128)(2,1)} %reshape_reshape_squeeze.8) | copy-start | bytes 1572868
  130.5 4.1 %copy-start.2 = (bf16[16,128,384]{1,2,0:T(8,128)(2,1)S(1)}, bf16[16,128,384]{1,2,0:T(8,128)(2,1)}, u32[]{:S(2)}) copy-start(bf16[16,128,384]{1,2,0:T(8,128)(2,1)} %fusion) | copy-start | bytes 4718596
  132.7 15.8 %collective-permute-start.10 = (f32[64,4096]{1,0:T(8,128)}, f32[64,4096]{1,0:T(8,128)}, u32[]{:S(2)}, u32[]{:S(2)}) collective-permute-start(f32[64,4096]{1,0:T(8,128)} %pad_maximum_fusion.3), channel_id=1, source_target_pairs={{0,8},{8,0},{16,24},{24,16},{32,40},{40,32},{48,56},{56,48},{64,72... | collective-permute-start | bytes 3145736 | tf_op jit(solution)/shard_map/ppermute | solution.py:11
  140.8 7.7 %copy-start.1 = (f32[128,2048]{1,0:T(8,128)S(1)}, f32[128,2048]{1,0:T(8,128)}, u32[]{:S(2)}) copy-start(f32[128,2048]{1,0:T(8,128)} %copy.163) | copy-start | bytes 3145732
  140.8 37.7 %collective-permute-start.9 = (bf16[128,2048]{0,1:T(8,128)(2,1)}, bf16[128,2048]{0,1:T(8,128)(2,1)}, u32[]{:S(2)}, u32[]{:S(2)}) collective-permute-start(bf16[128,2048]{0,1:T(8,128)(2,1)} %bitcast.152), channel_id=1, source_target_pairs={{0,128},{8,136},{16,144},{24,152},{32,160},{40,168},{48,176},{56,1... | collective-permute-start | bytes 1572872 | tf_op jit(solution)/shard_map/ppermute | solution.py:11
  148.5 5.0 %copy-start.6 = (bf16[128,16,128]{0,2,1:T(8,128)(2,1)S(1)}, bf16[128,16,128]{0,2,1:T(8,128)(2,1)}, u32[]{:S(2)}) copy-start(bf16[128,16,128]{0,2,1:T(8,128)(2,1)} %copy.151) | copy-start | bytes 1572868
  148.5 8.1 %copy-start.5 = (bf16[128,16,128]{0,2,1:T(8,128)(2,1)S(1)}, bf16[128,16,128]{0,2,1:T(8,128)(2,1)}, u32[]{:S(2)}) copy-start(bf16[128,16,128]{0,2,1:T(8,128)(2,1)} %copy-done.4) | copy-start | bytes 1572868
  148.5 8.1 %copy-start.7 = (bf16[16,128,128]{1,2,0:T(8,128)(2,1)S(1)}, bf16[16,128,128]{1,2,0:T(8,128)(2,1)}, u32[]{:S(2)}) copy-start(bf16[16,128,128]{1,2,0:T(8,128)(2,1)} %fusion.11) | copy-start | bytes 1572868
  150.1 16.2 %collective-permute-start.11 = (f32[32,4096]{1,0:T(8,128)S(1)}, f32[32,4096]{1,0:T(8,128)S(1)}, u32[]{:S(2)}, u32[]{:S(2)}) collective-permute-start(f32[32,4096]{1,0:T(8,128)S(1)} %slice.144), channel_id=1, source_target_pairs={{0,16},{8,24},{16,0},{24,8},{32,48},{40,56},{48,32},{56,40},{64,80... | collective-permute-start | bytes 1572872 | tf_op jit(solution)/shard_map/ppermute | solution.py:11
  153.5 17.8 %copy-start.3 = (bf16[16,128,384]{1,2,0:T(8,128)(2,1)S(1)}, bf16[16,128,384]{1,2,0:T(8,128)(2,1)}, u32[]{:S(2)}) copy-start(bf16[16,128,384]{1,2,0:T(8,128)(2,1)} %fusion) | copy-start | bytes 4718596
  154.5 30.2 %collective-permute-start.8 = (bf16[128,4096]{0,1:T(8,128)(2,1)}, bf16[128,4096]{0,1:T(8,128)(2,1)}, u32[]{:S(2)}, u32[]{:S(2)}) collective-permute-start(bf16[128,4096]{0,1:T(8,128)(2,1)} %pad_maximum_fusion.5), channel_id=1, source_target_pairs={{0,8},{8,0},{16,24},{24,16},{32,40},{40,32},{48,56},{56,48},{64,72... | collective-permute-start | bytes 3145736 | tf_op jit(solution)/shard_map/ppermute | solution.py:11
  157.0 15.0 %copy-start.11 = (bf16[16,128,128]{2,1,0:T(8,128)(2,1)S(1)}, bf16[16,128,128]{2,1,0:T(8,128)(2,1)}, u32[]{:S(2)}) copy-start(bf16[16,128,128]{2,1,0:T(8,128)(2,1)} %get-tuple-element.46) | copy-start | bytes 1572868
  166.4 13.4 %collective-permute-start.12 = (f32[16,4096]{1,0:T(8,128)S(1)}, f32[16,4096]{1,0:T(8,128)}, u32[]{:S(2)}, u32[]{:S(2)}) collective-permute-start(f32[16,4096]{1,0:T(8,128)S(1)} %slice.146), channel_id=1, source_target_pairs={{0,32},{8,40},{16,48},{24,56},{32,0},{40,8},{48,16},{56,24},{64,96... | collective-permute-start | bytes 786440 | tf_op jit(solution)/shard_map/ppermute | solution.py:11
  174.0 35.3 %collective-permute-start.16 = (bf16[128,2048]{0,1:T(8,128)(2,1)}, bf16[128,2048]{0,1:T(8,128)(2,1)}, u32[]{:S(2)}, u32[]{:S(2)}) collective-permute-start(bf16[128,2048]{0,1:T(8,128)(2,1)} %bitcast.153), channel_id=1, source_target_pairs={{0,128},{8,136},{16,144},{24,152},{32,160},{40,168},{48,176},{56,1... | collective-permute-start | bytes 1572872 | tf_op jit(solution)/shard_map/ppermute | solution.py:11
  181.5 10.7 %collective-permute-start.13 = (f32[8,4096]{1,0:T(8,128)}, f32[8,4096]{1,0:T(8,128)S(1)}, u32[]{:S(2)}, u32[]{:S(2)}) collective-permute-start(f32[8,4096]{1,0:T(8,128)} %slice.148), channel_id=1, source_target_pairs={{0,64},{8,72},{16,80},{24,88},{32,96},{40,104},{48,112},{56,120},{... | collective-permute-start | bytes 393224 | tf_op jit(solution)/shard_map/ppermute | solution.py:11
  192.2 12.2 %collective-permute-start.14 = (f32[4,4096]{1,0:T(4,128)S(1)}, f32[4,4096]{1,0:T(4,128)S(1)}, u32[]{:S(2)}, u32[]{:S(2)}) collective-permute-start(f32[4,4096]{1,0:T(4,128)S(1)} %slice.150), channel_id=1, source_target_pairs={{0,128},{8,136},{16,144},{24,152},{32,160},{40,168},{48,176},{56,1... | collective-permute-start | bytes 196616 | tf_op jit(solution)/shard_map/ppermute | solution.py:11
  204.4 9.8 %collective-permute-start.15 = (f32[2,4096]{1,0:T(2,128)S(1)}, f32[2,4096]{1,0:T(2,128)S(1)}, u32[]{:S(2)}, u32[]{:S(2)}) collective-permute-start(f32[2,4096]{1,0:T(2,128)S(1)} %slice.152), channel_id=1, source_target_pairs={{0,256},{8,264},{16,272},{24,280},{32,288},{40,296},{48,304},{56,3... | collective-permute-start | bytes 98312 | tf_op jit(solution)/shard_map/ppermute | solution.py:11
  210.9 3.4 %copy-start.14 = (s32[2]{0:T(128)S(1)}, s32[2]{0:T(128)}, u32[]{:S(2)}) copy-start(s32[2]{0:T(128)} %param.11) | copy-start | bytes 28

commit v5 on v4

--- a/solution.py
+++ b/solution.py
@@ -38,7 +38,21 @@
         if step == z_steps - 1:
             gathered, held = lax.optimization_barrier((gathered, packed))
             for level_bit in level_bits:
-                arrived[level_bit] = from_partner(held, "seq", level_bit)
+                if level_bit == 0:
+                    came = from_partner(held, "seq", level_bit)
+                    arrived[level_bit] = (
+                        came[:, :columns],
+                        came[:, columns : 2 * columns],
+                        came[:, 2 * columns],
+                    )
+                    continue
+                first = from_partner(
+                    jnp.concatenate([held[:, :columns], held[:, 2 * columns :]], 1),
+                    "seq",
+                    level_bit,
+                )
+                second = from_partner(held[:, columns : 2 * columns], "seq", level_bit)
+                arrived[level_bit] = (first[:, :columns], second, first[:, columns])
     owner_bits = gather_bits[::-1]
     global_count = shards * per_block
     gathered = gathered.reshape((shards,) + picked.shape)
@@ -58,10 +72,8 @@
     value_list = [values]
     mask_list = [documents[:, None] == documents[None, :]]
     for level_bit in level_bits:
-        came = arrived[level_bit]
-        partner_keys = came[:, :columns]
-        partner_values = came[:, columns : 2 * columns]
-        partner_docs = came[:, 2 * columns].astype(documents.dtype)
+        partner_keys, partner_values, partner_docs = arrived[level_bit]
+        partner_docs = partner_docs.astype(documents.dtype)
         key_list.append(partner_keys)
         value_list.append(partner_values)
         mask_list.append(documents[:, None] == partner_docs[None, :])
@@ -144,7 +156,8 @@
     )
     for bit in owner_bits:
         half = owned.shape[0] // 2
-        owned = owned[:half] + from_partner(owned[half:], "seq", bit)
+        sent = owned[half:].astype(jnp.bfloat16)
+        owned = owned[:half] + from_partner(sent, "seq", bit).astype(jnp.float32)
     placement = (jnp.arange(rows_here, dtype=jnp.int32)[:, None] == global_offsets[None, :]).astype(
         jnp.float32
     )

time: 218 us -> 236 us (1.083)
  local copies, waits for them, and re-layouts: 32.6 us -> 48.4 us
  other arithmetic: 22.3 us -> 25.8 us
  starting transfers between devices: 68.1 us -> 65.1 us
    ppermute x17 -> x18, starting transfers between devices: 68.1 us -> 65.1 us  [from_partner(): lax.ppermute(array, axis, [(i, i ^ 1 << stride) for i in range(lax.axis_s...]
    convert_element_type x2, local copies, waits for them, and re-layouts: 1.46 us -> 4.41 us  [body(): key_sum = key_sum + split(back_keys).astype(jnp.float32)]
    slice x7 -> x9, local copies, waits for them, and re-layouts: 3.3 us -> 6.05 us  [the longest x1 2.06 us: body(): second = from_partner(held[:, columns:2 * columns], 'seq', level_bit)]
    unnamed x36 -> x32, local copies, waits for them, and re-layouts: 7.03 us -> 8.84 us
    ppermute x17 -> x18, waiting for transfers between devices: 71.8 us -> 72.4 us  [from_partner(): lax.ppermute(array, axis, [(i, i ^ 1 << stride) for i in range(lax.axis_s...]
  transfers between devices with their start and end apart: 17 -> 18, of which waited for: 9 -> 8; matrix products, arithmetic and copies ran while one was open for 19% -> 23% of each run, Pallas kernels for 0% -> 0%
where the time goes in v5:
time: 236 us; the launch traced here: 233 us
  waiting for transfers between devices  72.4 us (31%)
  starting transfers between devices  65.1 us (28%)
  local copies, waits for them, and re-layouts  48.4 us (21%)
  other arithmetic  25.8 us (11%)
  matrix products  19.7 us (8%)
    ppermute x18, waiting for transfers between devices, from_partner(): lax.ppermute(array, axis, [(i, i ^ 1 << stride) for i in range(lax.axis_s...  72.4 us
    ppermute x18, starting transfers between devices, from_partner(): lax.ppermute(array, axis, [(i, i ^ 1 << stride) for i in range(lax.axis_s...  65.1 us
    unnamed x32, local copies, waits for them, and re-layouts  8.84 us
    another operation x11, other arithmetic, body(): gathered = jnp.stack([gathered, from_partner(gathered, 'seq', bit)], 0)  6.13 us
  transfers between devices with their start and end apart: 18, of which 8 were waited for; matrix products, arithmetic and copies ran while one was open for 23% of the time, Pallas kernels for 0%

profile of v5, /device:TPU:24, one launch (start us, length us, event | category | flops | bytes accessed | tf_op | source)
XLA Modules:
  0.0 232.6 jit_solution(9561455738096367248)
XLA Ops:
  4.7 9.1 %collective-permute-start = (bf16[2,2,2048]{2,1,0:T(2,128)(2,1)S(1)}, bf16[2,2,2048]{2,1,0:T(2,128)(2,1)S(1)}, u32[]{:S(2)}, u32[]{:S(2)}) collective-permute-start(bf16[2,2,2048]{2,1,0:T(2,128)(2,1)S(1)} %pad_maximum_fusion.12), channel_id=1, source_target_pairs={{0,256},{8,264},{16,272},{24,280},{32,288},{40,296},{48,304},{56,3... | collective-permute-start | bytes 49160 | tf_op jit(solution)/shard_map/ppermute | solution.py:11
  18.3 5.3 %collective-permute-start.1 = (bf16[2,2,2,2048]{3,2,1,0:T(2,128)(2,1)S(1)}, bf16[2,2,2,2048]{3,2,1,0:T(2,128)(2,1)S(1)}, u32[]{:S(2)}, u32[]{:S(2)}) collective-permute-start(bf16[2,2,2,2048]{3,2,1,0:T(2,128)(2,1)S(1)} %pad_maximum_fusion.11), channel_id=1, source_target_pairs={{0,128},{8,136},{16,144},{24,152},{32,160},{40,168},{48,176},{56,1... | collective-permute-start | bytes 98312 | tf_op jit(solution)/shard_map/ppermute | solution.py:11
  25.9 3.5 %collective-permute-start.2 = (bf16[2,2,2,2,2048]{4,3,2,1,0:T(2,128)(2,1)S(1)}, bf16[2,2,2,2,2048]{4,3,2,1,0:T(2,128)(2,1)S(1)}, u32[]{:S(2)}, u32[]{:S(2)}) collective-permute-start(bf16[2,2,2,2,2048]{4,3,2,1,0:T(2,128)(2,1)S(1)} %pad_maximum_fusion.10), channel_id=1, source_target_pairs={{0,64},{8,72},{16,80},{24,88},{32,96},{40,104},{48,112},{56,120},{... | collective-permute-start | bytes 196616 | tf_op jit(solution)/shard_map/ppermute | solution.py:11
  29.5 2.6 %collective-permute-done.2 = bf16[2,2,2,2,2048]{4,3,2,1,0:T(2,128)(2,1)S(1)} collective-permute-done((bf16[2,2,2,2,2048]{4,3,2,1,0:T(2,128)(2,1)S(1)}, bf16[2,2,2,2,2048]{4,3,2,1,0:T(2,128)(2,1)S(1)}, u32[]{:S(2)}, u32[]{:S(2)}) %collective-permute-start.2) | collective-permute-done | bytes 65568 | tf_op jit(solution)/shard_map/ppermute | solution.py:11
  32.3 4.9 %collective-permute-start.3 = (bf16[2,2,2,2,2,2048]{5,4,3,2,1,0:T(2,128)(2,1)S(1)}, bf16[2,2,2,2,2,2048]{5,4,3,2,1,0:T(2,128)(2,1)S(1)}, u32[]{:S(2)}, u32[]{:S(2)}) collective-permute-start(bf16[2,2,2,2,2,2048]{5,4,3,2,1,0:T(2,128)(2,1)S(1)} %pad_maximum_fusion.9), channel_id=1, source_target_pairs={{0,32},{8,40},{16,48},{24,56},{32,0},{40,8},{48,16},{56,24},{64,96... | collective-permute-start | bytes 393224 | tf_op jit(solution)/shard_map/ppermute | solution.py:11
  41.0 3.4 %collective-permute-start.4 = (bf16[2,2,2,2,2,2,2048]{6,5,4,3,2,1,0:T(2,128)(2,1)S(1)}, bf16[2,2,2,2,2,2,2048]{6,5,4,3,2,1,0:T(2,128)(2,1)S(1)}, u32[]{:S(2)}, u32[]{:S(2)}) collective-permute-start(bf16[2,2,2,2,2,2,2048]{6,5,4,3,2,1,0:T(2,128)(2,1)S(1)} %pad_maximum_fusion.8), channel_id=1, source_target_pairs={{0,16},{8,24},{16,0},{24,8},{32,48},{40,56},{48,32},{56,40},{64,80... | collective-permute-start | bytes 786440 | tf_op jit(solution)/shard_map/ppermute | solution.py:11
  45.3 4.5 %collective-permute-start.7 = (bf16[128,2176]{0,1:T(8,128)(2,1)}, bf16[128,2176]{0,1:T(8,128)(2,1)}, u32[]{:S(2)}, u32[]{:S(2)}) collective-permute-start(bf16[128,2176]{0,1:T(8,128)(2,1)} %pad_maximum_fusion.6), channel_id=1, source_target_pairs={{0,128},{8,136},{16,144},{24,152},{32,160},{40,168},{48,176},{56,1... | collective-permute-start | bytes 1671176 | tf_op jit(solution)/shard_map/ppermute | solution.py:11
  56.2 2.4 %collective-permute-start.6 = (bf16[128,4224]{0,1:T(8,128)(2,1)}, bf16[128,4224]{0,1:T(8,128)(2,1)}, u32[]{:S(2)}, u32[]{:S(2)}) collective-permute-start(bf16[128,4224]{0,1:T(8,128)(2,1)} %pad_maximum_fusion.2), channel_id=1, source_target_pairs={{0,8},{8,0},{16,24},{24,16},{32,40},{40,32},{48,56},{56,48},{64,72... | collective-permute-start | bytes 3244040 | tf_op jit(solution)/shard_map/ppermute | solution.py:11
  58.6 3.8 %collective-permute-start.8 = (bf16[128,2048]{0,1:T(8,128)(2,1)}, bf16[128,2048]{0,1:T(8,128)(2,1)}, u32[]{:S(2)}, u32[]{:S(2)}) collective-permute-start(bf16[128,2048]{0,1:T(8,128)(2,1)} %get-tuple-element.32), channel_id=1, source_target_pairs={{0,128},{8,136},{16,144},{24,152},{32,160},{40,168},{48,176},{56,1... | collective-permute-start | bytes 1572872 | tf_op jit(solution)/shard_map/ppermute | solution.py:11
  63.1 20.2 %collective-permute-done.7 = bf16[128,2176]{0,1:T(8,128)(2,1)} collective-permute-done((bf16[128,2176]{0,1:T(8,128)(2,1)}, bf16[128,2176]{0,1:T(8,128)(2,1)}, u32[]{:S(2)}, u32[]{:S(2)}) %collective-permute-start.7) | collective-permute-done | bytes 557088 | tf_op jit(solution)/shard_map/ppermute | solution.py:11
  85.9 2.6 %pad_maximum_fusion.4 = bf16[2,2,2,2,2,2,2,2,2048]{8,7,6,5,4,3,2,1,0:T(2,128)(2,1)S(1)} fusion(bf16[1,2,2,2,2,2,2,2,2048]{8,7,6,5,4,3,2,1,0:T(2,128)(2,1)} %bitcast.13, bf16[1,2,2,2,2,2,2,2,2048]{8,7,6,5,4,3,2,1,0:T(2,128)(2,1)S(1)} %fusion.82), kind=kLoop, calls=%fused_computation.42 | loop fusion | flops 524288 | bytes 2097152 | tf_op jit(solution)/shard_map/stack | solution.py:37
  105.6 2.6 %fusion = bf16[16,128,384]{1,2,0:T(8,128)(2,1)} fusion(bf16[384,16,128]{0,2,1:T(8,128)(2,1)S(1)} %bitcast.141, bf16[128,16,128]{0,2,1:T(8,128)(2,1)S(1)} %bitcast.150, f32[16,128]{1,0:T(8,128)S(1)} %bitcast.167, f32[16,128]{1,0:T(8,128)S(1)} %add.56, f32[16,128]{1,0:T(8,128)S(1)} %max.7, f32[16,384,128]{2,1,0:T(8,128)S(1)} %get-tuple-element.44, ...), kind=kOutput, calls=%fused_computation.3 | convolution fusion | flops 206831616 | bytes 6889472 | tf_op jit(solution)/shard_map/thd,uhd->htu/dot_general | solution.py:113
  109.7 2.5 %fusion.4 = f32[128,16,128]{2,0,1:T(8,128)} fusion(bf16[16,128,128]{1,2,0:T(8,128)(2,1)} %fusion.11, bf16[128,16,128]{0,2,1:T(8,128)(2,1)S(1)} %bitcast.129), kind=kOutput, calls=%fused_computation.16 | convolution fusion | flops 67371008 | bytes 2097152 | tf_op jit(solution)/shard_map/htg,thd->ghd/dot_general | solution.py:148
  112.2 2.6 %copy.160 = f32[128,16,128]{0,2,1:T(8,128)} copy(f32[128,16,128]{2,0,1:T(8,128)} %fusion.4) | data formatting | bytes 2097152 | tf_op jit(solution)/shard_map/mul | solution.py:148
  114.8 2.6 %copy.163 = f32[128,2048]{1,0:T(8,128)} copy(f32[128,2048]{0,1:T(8,128)} %bitcast.133) | data formatting | bytes 2097152 | tf_op jit(solution)/shard_map/reshape | solution.py:155
  118.7 2.4 %collective-permute-start.11 = (bf16[64,4096]{1,0:T(8,128)(2,1)S(1)}, bf16[64,4096]{1,0:T(8,128)(2,1)S(1)}, u32[]{:S(2)}, u32[]{:S(2)}) collective-permute-start(bf16[64,4096]{1,0:T(8,128)(2,1)S(1)} %fusion.18), channel_id=1, source_target_pairs={{0,8},{8,0},{16,24},{24,16},{32,40},{40,32},{48,56},{56,48},{64,72... | collective-permute-start | bytes 1572872 | tf_op jit(solution)/shard_map/ppermute | solution.py:11
  121.1 2.2 fusion.62
  123.3 2.7 %fusion.61 = (bf16[384,16,128]{0,2,1:T(8,128)(2,1)S(1)}, f32[384,16,128]{0,2,1:T(8,128)}) fusion(bf16[128,16,128]{0,2,1:T(8,128)(2,1)S(1)} %bitcast.151, f32[16,128]{1,0:T(8,128)S(1)} %add.56, f32[16,128]{1,0:T(8,128)S(1)} %max.7, f32[16,384,128]{2,1,0:T(8,128)S(1)} %copy-done.1, pred[128,384]{0,1:T(8,128)(4,1)S(1)} %pad_add_fusion), kind=kOutput, calls=%fused_computation.118 | convolution fusion | flops 206045184 | bytes 8454144 | tf_op jit(solution)/shard_map/htu,thd->uhd/dot_general | solution.py:123
  126.2 2.8 %collective-permute-start.12 = (bf16[32,4096]{1,0:T(8,128)(2,1)S(1)}, bf16[32,4096]{1,0:T(8,128)(2,1)S(1)}, u32[]{:S(2)}, u32[]{:S(2)}) collective-permute-start(bf16[32,4096]{1,0:T(8,128)(2,1)S(1)} %slice.210), channel_id=1, source_target_pairs={{0,16},{8,24},{16,0},{24,8},{32,48},{40,56},{48,32},{56,40},{64,80... | collective-permute-start | bytes 786440 | tf_op jit(solution)/shard_map/ppermute | solution.py:11
  129.4 7.6 %collective-permute-done.12 = bf16[32,4096]{1,0:T(8,128)(2,1)S(1)} collective-permute-done((bf16[32,4096]{1,0:T(8,128)(2,1)S(1)}, bf16[32,4096]{1,0:T(8,128)(2,1)S(1)}, u32[]{:S(2)}, u32[]{:S(2)}) %collective-permute-start.12) | collective-permute-done | bytes 262176 | tf_op jit(solution)/shard_map/ppermute | solution.py:11
  137.0 4.6 %collective-permute-start.13 = (bf16[16,4096]{1,0:T(8,128)(2,1)S(1)}, bf16[16,4096]{1,0:T(8,128)(2,1)S(1)}, u32[]{:S(2)}, u32[]{:S(2)}) collective-permute-start(bf16[16,4096]{1,0:T(8,128)(2,1)S(1)} %slice.211), channel_id=1, source_target_pairs={{0,32},{8,40},{16,48},{24,56},{32,0},{40,8},{48,16},{56,24},{64,96... | collective-permute-start | bytes 393224 | tf_op jit(solution)/shard_map/ppermute | solution.py:11
  142.9 2.5 %collective-permute-done.13 = bf16[16,4096]{1,0:T(8,128)(2,1)S(1)} collective-permute-done((bf16[16,4096]{1,0:T(8,128)(2,1)S(1)}, bf16[16,4096]{1,0:T(8,128)(2,1)S(1)}, u32[]{:S(2)}, u32[]{:S(2)}) %collective-permute-start.13) | collective-permute-done | bytes 131104 | tf_op jit(solution)/shard_map/ppermute | solution.py:11
  152.0 4.7 %collective-permute-start.10 = (bf16[128,2048]{0,1:T(8,128)(2,1)}, bf16[128,2048]{0,1:T(8,128)(2,1)}, u32[]{:S(2)}, u32[]{:S(2)}) collective-permute-start(bf16[128,2048]{0,1:T(8,128)(2,1)} %bitcast.152), channel_id=1, source_target_pairs={{0,128},{8,136},{16,144},{24,152},{32,160},{40,168},{48,176},{56,1... | collective-permute-start | bytes 1572872 | tf_op jit(solution)/shard_map/ppermute | solution.py:11
  162.9 17.3 %collective-permute-done.15 = bf16[4,4096]{1,0:T(4,128)(2,1)S(1)} collective-permute-done((bf16[4,4096]{1,0:T(4,128)(2,1)S(1)}, bf16[4,4096]{1,0:T(4,128)(2,1)S(1)}, u32[]{:S(2)}, u32[]{:S(2)}) %collective-permute-start.15) | collective-permute-done | bytes 32800 | tf_op jit(solution)/shard_map/ppermute | solution.py:11
  180.3 4.0 %collective-permute-start.16 = (bf16[2,4096]{1,0:T(2,128)(2,1)S(1)}, bf16[2,4096]{1,0:T(2,128)(2,1)S(1)}, u32[]{:S(2)}, u32[]{:S(2)}) collective-permute-start(bf16[2,4096]{1,0:T(2,128)(2,1)S(1)} %slice.214), channel_id=1, source_target_pairs={{0,256},{8,264},{16,272},{24,280},{32,288},{40,296},{48,304},{56,3... | collective-permute-start | bytes 49160 | tf_op jit(solution)/shard_map/ppermute | solution.py:11
  196.6 19.3 %collective-permute-done.17 = bf16[128,2048]{0,1:T(8,128)(2,1)S(1)} collective-permute-done((bf16[128,2048]{0,1:T(8,128)(2,1)}, bf16[128,2048]{0,1:T(8,128)(2,1)S(1)}, u32[]{:S(2)}, u32[]{:S(2)}) %collective-permute-start.17) | collective-permute-done | bytes 524320 | tf_op jit(solution)/shard_map/ppermute | solution.py:11
  215.8 2.5 %fusion.16 = f32[128,16,128]{0,2,1:T(8,128)} fusion(f32[384,16,128]{0,2,1:T(8,128)} %get-tuple-element.48, bf16[128,16,128]{0,2,1:T(8,128)(2,1)S(1)} %bitcast.154, bf16[128,16,128]{0,2,1:T(8,128)(2,1)S(1)} %bitcast.139), kind=kLoop, calls=%fused_computation.35 | loop fusion | flops 1048576 | bytes 3145728 | tf_op jit(solution)/shard_map/add | solution.py:140
  219.9 2.2 copy.153
  222.1 3.0 %fusion.19 = f32[128,16,128]{2,0,1:T(8,128)} fusion(f32[128,16,128]{2,0,1:T(8,128)} %copy.155, f32[128,16,128]{2,0,1:T(8,128)} %copy.153, f32[384,16,128]{2,0,1:T(8,128)} %get-tuple-element.50), kind=kLoop, calls=%fused_computation.41 | loop fusion | flops 524288 | bytes 4194304 | tf_op jit(solution)/shard_map/add | solution.py:139
  225.1 2.6 %copy.156 = f32[128,16,128]{0,2,1:T(8,128)} copy(f32[128,16,128]{2,0,1:T(8,128)} %fusion.19) | data formatting | bytes 2097152 | tf_op jit(solution)/shard_map/add | solution.py:139
  227.6 2.5 %copy.164 = f32[128,2048]{1,0:T(8,128)} copy(f32[128,2048]{0,1:T(8,128)} %bitcast.134) | data formatting | bytes 2097152 | tf_op jit(solution)/shard_map/reshape | solution.py:167
  230.1 2.4 %fusion.15 = (bf16[128,2048]{1,0:T(8,128)(2,1)}, bf16[128,2048]{1,0:T(8,128)(2,1)}) fusion(f32[128,2048]{1,0:T(8,128)S(1)} %copy.165, f32[128,4096]{1,0:T(8,128)S(1)} %fusion.28, f32[128,2048]{1,0:T(8,128)} %copy.164), kind=kLoop, calls=%fused_computation.33 | loop fusion | flops 1048576 | bytes 5242880 | tf_op jit(solution)/shard_map/convert_element_type | solution.py:168
  (118 shorter events, 73.3 us)
Async XLA Ops:
  4.7 13.5 %collective-permute-start = (bf16[2,2,2048]{2,1,0:T(2,128)(2,1)S(1)}, bf16[2,2,2048]{2,1,0:T(2,128)(2,1)S(1)}, u32[]{:S(2)}, u32[]{:S(2)}) collective-permute-start(bf16[2,2,2048]{2,1,0:T(2,128)(2,1)S(1)} %pad_maximum_fusion.12), channel_id=1, source_target_pairs={{0,256},{8,264},{16,272},{24,280},{32,288},{40,296},{48,304},{56,3... | collective-permute-start | bytes 49160 | tf_op jit(solution)/shard_map/ppermute | solution.py:11
  18.2 35.7 %copy-start.7 = (bf16[128,2048]{1,0:T(8,128)(2,1)S(1)}, bf16[128,2048]{1,0:T(8,128)(2,1)}, u32[]{:S(2)}) copy-start(bf16[128,2048]{1,0:T(8,128)(2,1)} %param.9) | copy-start | bytes 1572868
  18.3 7.5 %collective-permute-start.1 = (bf16[2,2,2,2048]{3,2,1,0:T(2,128)(2,1)S(1)}, bf16[2,2,2,2048]{3,2,1,0:T(2,128)(2,1)S(1)}, u32[]{:S(2)}, u32[]{:S(2)}) collective-permute-start(bf16[2,2,2,2048]{3,2,1,0:T(2,128)(2,1)S(1)} %pad_maximum_fusion.11), channel_id=1, source_target_pairs={{0,128},{8,136},{16,144},{24,152},{32,160},{40,168},{48,176},{56,1... | collective-permute-start | bytes 98312 | tf_op jit(solution)/shard_map/ppermute | solution.py:11
  25.9 6.2 %collective-permute-start.2 = (bf16[2,2,2,2,2048]{4,3,2,1,0:T(2,128)(2,1)S(1)}, bf16[2,2,2,2,2048]{4,3,2,1,0:T(2,128)(2,1)S(1)}, u32[]{:S(2)}, u32[]{:S(2)}) collective-permute-start(bf16[2,2,2,2,2048]{4,3,2,1,0:T(2,128)(2,1)S(1)} %pad_maximum_fusion.10), channel_id=1, source_target_pairs={{0,64},{8,72},{16,80},{24,88},{32,96},{40,104},{48,112},{56,120},{... | collective-permute-start | bytes 196616 | tf_op jit(solution)/shard_map/ppermute | solution.py:11
  32.3 8.4 %collective-permute-start.3 = (bf16[2,2,2,2,2,2048]{5,4,3,2,1,0:T(2,128)(2,1)S(1)}, bf16[2,2,2,2,2,2048]{5,4,3,2,1,0:T(2,128)(2,1)S(1)}, u32[]{:S(2)}, u32[]{:S(2)}) collective-permute-start(bf16[2,2,2,2,2,2048]{5,4,3,2,1,0:T(2,128)(2,1)S(1)} %pad_maximum_fusion.9), channel_id=1, source_target_pairs={{0,32},{8,40},{16,48},{24,56},{32,0},{40,8},{48,16},{56,24},{64,96... | collective-permute-start | bytes 393224 | tf_op jit(solution)/shard_map/ppermute | solution.py:11
  41.0 9.1 %collective-permute-start.4 = (bf16[2,2,2,2,2,2,2048]{6,5,4,3,2,1,0:T(2,128)(2,1)S(1)}, bf16[2,2,2,2,2,2,2048]{6,5,4,3,2,1,0:T(2,128)(2,1)S(1)}, u32[]{:S(2)}, u32[]{:S(2)}) collective-permute-start(bf16[2,2,2,2,2,2,2048]{6,5,4,3,2,1,0:T(2,128)(2,1)S(1)} %pad_maximum_fusion.8), channel_id=1, source_target_pairs={{0,16},{8,24},{16,0},{24,8},{32,48},{40,56},{48,32},{56,40},{64,80... | collective-permute-start | bytes 786440 | tf_op jit(solution)/shard_map/ppermute | solution.py:11
  45.3 38.1 %collective-permute-start.7 = (bf16[128,2176]{0,1:T(8,128)(2,1)}, bf16[128,2176]{0,1:T(8,128)(2,1)}, u32[]{:S(2)}, u32[]{:S(2)}) collective-permute-start(bf16[128,2176]{0,1:T(8,128)(2,1)} %pad_maximum_fusion.6), channel_id=1, source_target_pairs={{0,128},{8,136},{16,144},{24,152},{32,160},{40,168},{48,176},{56,1... | collective-permute-start | bytes 1671176 | tf_op jit(solution)/shard_map/ppermute | solution.py:11
  51.7 34.2 %collective-permute-start.5 = (bf16[2,2,2,2,2,2,2,2048]{7,6,5,4,3,2,1,0:T(2,128)(2,1)}, bf16[2,2,2,2,2,2,2,2048]{7,6,5,4,3,2,1,0:T(2,128)(2,1)}, u32[]{:S(2)}, u32[]{:S(2)}) collective-permute-start(bf16[2,2,2,2,2,2,2,2048]{7,6,5,4,3,2,1,0:T(2,128)(2,1)} %pad_maximum_fusion.7), channel_id=1, source_target_pairs={{0,8},{8,0},{16,24},{24,16},{32,40},{40,32},{48,56},{56,48},{64,72... | collective-permute-start | bytes 1572872 | tf_op jit(solution)/shard_map/ppermute | solution.py:11
  56.2 37.3 %collective-permute-start.6 = (bf16[128,4224]{0,1:T(8,128)(2,1)}, bf16[128,4224]{0,1:T(8,128)(2,1)}, u32[]{:S(2)}, u32[]{:S(2)}) collective-permute-start(bf16[128,4224]{0,1:T(8,128)(2,1)} %pad_maximum_fusion.2), channel_id=1, source_target_pairs={{0,8},{8,0},{16,24},{24,16},{32,40},{40,32},{48,56},{56,48},{64,72... | collective-permute-start | bytes 3244040 | tf_op jit(solution)/shard_map/ppermute | solution.py:11
  58.6 42.5 %collective-permute-start.8 = (bf16[128,2048]{0,1:T(8,128)(2,1)}, bf16[128,2048]{0,1:T(8,128)(2,1)}, u32[]{:S(2)}, u32[]{:S(2)}) collective-permute-start(bf16[128,2048]{0,1:T(8,128)(2,1)} %get-tuple-element.32), channel_id=1, source_target_pairs={{0,128},{8,136},{16,144},{24,152},{32,160},{40,168},{48,176},{56,1... | collective-permute-start | bytes 1572872 | tf_op jit(solution)/shard_map/ppermute | solution.py:11
  90.1 4.1 %copy-start.11 = (s32[128]{0:T(128)S(1)}, s32[128]{0:T(128)}, u32[]{:S(2)}) copy-start(s32[128]{0:T(128)} %param.10) | copy-start | bytes 1540
  92.0 3.6 %copy-start.4 = (bf16[128,16,128]{0,2,1:T(8,128)(2,1)}, bf16[128,16,128]{0,2,1:T(8,128)(2,1)S(1)}, u32[]{:S(2)}) copy-start(bf16[128,16,128]{0,2,1:T(8,128)(2,1)S(1)} %copy.146) | copy-start | bytes 1572868
  97.7 8.0 %copy-start = (f32[16,384,128]{2,1,0:T(8,128)}, f32[16,384,128]{2,1,0:T(8,128)S(1)}, u32[]{:S(2)}) copy-start(f32[16,384,128]{2,1,0:T(8,128)S(1)} %get-tuple-element.44) | copy-start | bytes 9437188
  97.7 1.4 copy-start.8
  98.4 2.2 copy-start.10
  117.4 3.7 %copy-start.3 = (bf16[16,128,384]{1,2,0:T(8,128)(2,1)S(1)}, bf16[16,128,384]{1,2,0:T(8,128)(2,1)}, u32[]{:S(2)}) copy-start(bf16[16,128,384]{1,2,0:T(8,128)(2,1)} %fusion) | copy-start | bytes 4718596
  118.6 4.7 %copy-start.1 = (f32[16,384,128]{2,1,0:T(8,128)S(1)}, f32[16,384,128]{2,1,0:T(8,128)}, u32[]{:S(2)}) copy-start(f32[16,384,128]{2,1,0:T(8,128)} %copy-done) | copy-start | bytes 9437188
  118.6 4.7 %copy-start.9 = (bf16[128,2048]{0,1:T(8,128)(2,1)S(1)}, bf16[128,2048]{0,1:T(8,128)(2,1)}, u32[]{:S(2)}) copy-start(bf16[128,2048]{0,1:T(8,128)(2,1)} %copy.140) | copy-start | bytes 1572868
  118.7 7.4 %collective-permute-start.11 = (bf16[64,4096]{1,0:T(8,128)(2,1)S(1)}, bf16[64,4096]{1,0:T(8,128)(2,1)S(1)}, u32[]{:S(2)}, u32[]{:S(2)}) collective-permute-start(bf16[64,4096]{1,0:T(8,128)(2,1)S(1)} %fusion.18), channel_id=1, source_target_pairs={{0,8},{8,0},{16,24},{24,16},{32,40},{40,32},{48,56},{56,48},{64,72... | collective-permute-start | bytes 1572872 | tf_op jit(solution)/shard_map/ppermute | solution.py:11
  123.3 2.8 %copy-start.2 = (f32[128,2048]{1,0:T(8,128)S(1)}, f32[128,2048]{1,0:T(8,128)}, u32[]{:S(2)}) copy-start(f32[128,2048]{1,0:T(8,128)} %copy.163) | copy-start | bytes 3145732
  126.0 3.0 %copy-start.5 = (bf16[128,16,128]{0,2,1:T(8,128)(2,1)S(1)}, bf16[128,16,128]{0,2,1:T(8,128)(2,1)}, u32[]{:S(2)}) copy-start(bf16[128,16,128]{0,2,1:T(8,128)(2,1)} %copy-done.4) | copy-start | bytes 1572868
  126.1 3.0 %copy-start.6 = (bf16[16,128,128]{1,2,0:T(8,128)(2,1)S(1)}, bf16[16,128,128]{1,2,0:T(8,128)(2,1)}, u32[]{:S(2)}) copy-start(bf16[16,128,128]{1,2,0:T(8,128)(2,1)} %fusion.11) | copy-start | bytes 1572868
  126.2 10.7 %collective-permute-start.12 = (bf16[32,4096]{1,0:T(8,128)(2,1)S(1)}, bf16[32,4096]{1,0:T(8,128)(2,1)S(1)}, u32[]{:S(2)}, u32[]{:S(2)}) collective-permute-start(bf16[32,4096]{1,0:T(8,128)(2,1)S(1)} %slice.210), channel_id=1, source_target_pairs={{0,16},{8,24},{16,0},{24,8},{32,48},{40,56},{48,32},{56,40},{64,80... | collective-permute-start | bytes 786440 | tf_op jit(solution)/shard_map/ppermute | solution.py:11
  137.0 8.4 %collective-permute-start.13 = (bf16[16,4096]{1,0:T(8,128)(2,1)S(1)}, bf16[16,4096]{1,0:T(8,128)(2,1)S(1)}, u32[]{:S(2)}, u32[]{:S(2)}) collective-permute-start(bf16[16,4096]{1,0:T(8,128)(2,1)S(1)} %slice.211), channel_id=1, source_target_pairs={{0,32},{8,40},{16,48},{24,56},{32,0},{40,8},{48,16},{56,24},{64,96... | collective-permute-start | bytes 393224 | tf_op jit(solution)/shard_map/ppermute | solution.py:11
  145.5 11.2 %collective-permute-start.14 = (bf16[8,4096]{1,0:T(8,128)(2,1)S(1)}, bf16[8,4096]{1,0:T(8,128)(2,1)S(1)}, u32[]{:S(2)}, u32[]{:S(2)}) collective-permute-start(bf16[8,4096]{1,0:T(8,128)(2,1)S(1)} %slice.212), channel_id=1, source_target_pairs={{0,64},{8,72},{16,80},{24,88},{32,96},{40,104},{48,112},{56,120},{... | collective-permute-start | bytes 196616 | tf_op jit(solution)/shard_map/ppermute | solution.py:11
  152.0 39.3 %collective-permute-start.10 = (bf16[128,2048]{0,1:T(8,128)(2,1)}, bf16[128,2048]{0,1:T(8,128)(2,1)}, u32[]{:S(2)}, u32[]{:S(2)}) collective-permute-start(bf16[128,2048]{0,1:T(8,128)(2,1)} %bitcast.152), channel_id=1, source_target_pairs={{0,128},{8,136},{16,144},{24,152},{32,160},{40,168},{48,176},{56,1... | collective-permute-start | bytes 1572872 | tf_op jit(solution)/shard_map/ppermute | solution.py:11
  156.8 23.5 %collective-permute-start.15 = (bf16[4,4096]{1,0:T(4,128)(2,1)S(1)}, bf16[4,4096]{1,0:T(4,128)(2,1)S(1)}, u32[]{:S(2)}, u32[]{:S(2)}) collective-permute-start(bf16[4,4096]{1,0:T(4,128)(2,1)S(1)} %slice.213), channel_id=1, source_target_pairs={{0,128},{8,136},{16,144},{24,152},{32,160},{40,168},{48,176},{56,1... | collective-permute-start | bytes 98312 | tf_op jit(solution)/shard_map/ppermute | solution.py:11
  161.0 33.5 %collective-permute-start.9 = (bf16[128,4096]{0,1:T(8,128)(2,1)}, bf16[128,4096]{0,1:T(8,128)(2,1)}, u32[]{:S(2)}, u32[]{:S(2)}) collective-permute-start(bf16[128,4096]{0,1:T(8,128)(2,1)} %pad_maximum_fusion.5), channel_id=1, source_target_pairs={{0,8},{8,0},{16,24},{24,16},{32,40},{40,32},{48,56},{56,48},{64,72... | collective-permute-start | bytes 3145736 | tf_op jit(solution)/shard_map/ppermute | solution.py:11
  180.3 13.2 %copy-start.12 = (s32[2]{0:T(128)S(1)}, s32[2]{0:T(128)}, u32[]{:S(2)}) copy-start(s32[2]{0:T(128)} %param.11) | copy-start | bytes 28
  180.3 13.2 %collective-permute-start.16 = (bf16[2,4096]{1,0:T(2,128)(2,1)S(1)}, bf16[2,4096]{1,0:T(2,128)(2,1)S(1)}, u32[]{:S(2)}, u32[]{:S(2)}) collective-permute-start(bf16[2,4096]{1,0:T(2,128)(2,1)S(1)} %slice.214), channel_id=1, source_target_pairs={{0,256},{8,264},{16,272},{24,280},{32,288},{40,296},{48,304},{56,3... | collective-permute-start | bytes 49160 | tf_op jit(solution)/shard_map/ppermute | solution.py:11
  189.4 26.4 %collective-permute-start.17 = (bf16[128,2048]{0,1:T(8,128)(2,1)}, bf16[128,2048]{0,1:T(8,128)(2,1)S(1)}, u32[]{:S(2)}, u32[]{:S(2)}) collective-permute-start(bf16[128,2048]{0,1:T(8,128)(2,1)} %bitcast.153), channel_id=1, source_target_pairs={{0,128},{8,136},{16,144},{24,152},{32,160},{40,168},{48,176},{56,1... | collective-permute-start | bytes 1572872 | tf_op jit(solution)/shard_map/ppermute | solution.py:11

commit v6 on v4

--- a/solution.py
+++ b/solution.py
@@ -68,12 +68,20 @@
     block_keys = jnp.concatenate(key_list, 0)
     block_values = jnp.concatenate(value_list, 0)
     block_mask = jnp.concatenate(mask_list, 1)
-    raw = (
-        jnp.einsum(
-            "thd,uhd->htu", query_heads, split(block_keys), preferred_element_type=jnp.float32
-        )
-        * temper
-    )
+    raws = [
+        jnp.einsum("thd,uhd->htu", query_heads, split(group), preferred_element_type=jnp.float32)
+        for group in key_list
+    ]
+    products = [
+        jnp.einsum("thd,uhd->htu", dout_heads, split(group), preferred_element_type=jnp.float32)
+        for group in value_list
+    ]
+    early = [0] + [level + 1 for level, level_bit in enumerate(level_bits) if level_bit == 0]
+    held = lax.optimization_barrier(([raws[i] for i in early], [products[i] for i in early]))
+    for position, i in enumerate(early):
+        raws[i] = held[0][position]
+        products[i] = held[1][position]
+    raw = jnp.concatenate(raws, 2) * temper
     block_scores = jnp.where(block_mask[None], raw, -jnp.inf)
     global_raw = (
         jnp.einsum(
@@ -98,9 +106,7 @@
     )
     attended = summed.astype(jnp.bfloat16).reshape(rows_here, columns)
     delta = jnp.sum(dout_heads.astype(jnp.float32) * split(attended).astype(jnp.float32), axis=-1).T
-    product = jnp.einsum(
-        "thd,uhd->htu", dout_heads, split(block_values), preferred_element_type=jnp.float32
-    )
+    product = jnp.concatenate(products, 2)
     slope = (probs * (product - delta[:, :, None])).astype(jnp.bfloat16)
     query_term = jnp.einsum(
         "htu,uhd->thd", slope, split(block_keys), preferred_element_type=jnp.float32
@@ -133,7 +139,7 @@
     query_sum = query_sum + jnp.einsum(
         "htg,ghd->thd", global_slope, split(global_keys), preferred_element_type=jnp.float32
     )
-    key_part = temper * jnp.einsum(
+    key_part = jnp.einsum(
         "htg,thd->ghd", global_slope, query_heads, preferred_element_type=jnp.float32
     )
     value_part = jnp.einsum(
@@ -145,6 +151,7 @@
     for bit in owner_bits:
         half = owned.shape[0] // 2
         owned = owned[:half] + from_partner(owned[half:], "seq", bit)
+    owned = jnp.concatenate([temper * owned[:, :columns], owned[:, columns:]], 1)
     placement = (jnp.arange(rows_here, dtype=jnp.int32)[:, None] == global_offsets[None, :]).astype(
         jnp.float32
     )

time: 218 us -> 240 us (1.10)
  waiting for transfers between devices: 71.8 us -> 92 us
  other arithmetic: 22.3 us -> 24.9 us
    ppermute x17, waiting for transfers between devices: 71.8 us -> 92 us  [from_partner(): lax.ppermute(array, axis, [(i, i ^ 1 << stride) for i in range(lax.axis_s...]
    unnamed x36 -> x62, local copies, waits for them, and re-layouts: 7.03 us -> 10.6 us
    dot_general x2 -> x6, matrix products: 3.37 us -> 6.43 us  [the longest x3 4.17 us: body(): jnp.einsum('thd,uhd->htu', dout_heads, split(group), preferred_element_ty...]
    slice x3 -> x1, local copies, waits for them, and re-layouts: 3.95 us -> 0.99 us  [body(): key_term[lower:upper].reshape(rows_here, columns).astype(jnp.bfloat16)]
    mul x1 -> x0, local copies, waits for them, and re-layouts: 2.54 us -> none  [body(): temper * jnp.einsum('htg,thd->ghd', global_slope, query_heads, preferred_...]
    dot_general x1, matrix products: 4.7 us -> 2.21 us  [body(): jnp.einsum('htu,thd->uhd', probs_b, dout_heads, preferred_element_type=jn...]
  transfers between devices with their start and end apart: 17 -> 17, of which waited for: 9 -> 10; matrix products, arithmetic and copies ran while one was open for 19% -> 17% of each run, Pallas kernels for 0% -> 0%
where the time goes in v6:
time: 240 us; the launch traced here: 238 us
  waiting for transfers between devices  92 us (38%)
  starting transfers between devices  68.7 us (29%)
  local copies, waits for them, and re-layouts  31.3 us (13%)
  other arithmetic  24.9 us (10%)
  matrix products  19.9 us (8%)
    ppermute x17, waiting for transfers between devices, from_partner(): lax.ppermute(array, axis, [(i, i ^ 1 << stride) for i in range(lax.axis_s...  92 us
    ppermute x17, starting transfers between devices, from_partner(): lax.ppermute(array, axis, [(i, i ^ 1 << stride) for i in range(lax.axis_s...  68.7 us
    unnamed x62, local copies, waits for them, and re-layouts  10.6 us
    another operation x11, other arithmetic, body(): gathered = jnp.stack([gathered, from_partner(gathered, 'seq', bit)], 0)  7.06 us
  transfers between devices with their start and end apart: 17, of which 10 were waited for; matrix products, arithmetic and copies ran while one was open for 17% of the time, Pallas kernels for 0%

profile of v6, /device:TPU:24, one launch (start us, length us, event | category | flops | bytes accessed | tf_op | source)
XLA Modules:
  0.0 238.3 jit_solution(14476558110563264115)
XLA Ops:
  4.8 9.2 %collective-permute-start = (bf16[2,2,2048]{2,1,0:T(2,128)(2,1)S(1)}, bf16[2,2,2048]{2,1,0:T(2,128)(2,1)S(1)}, u32[]{:S(2)}, u32[]{:S(2)}) collective-permute-start(bf16[2,2,2048]{2,1,0:T(2,128)(2,1)S(1)} %pad_maximum_fusion.11), channel_id=1, source_target_pairs={{0,256},{8,264},{16,272},{24,280},{32,288},{40,296},{48,304},{56,3... | collective-permute-start | bytes 49160 | tf_op jit(solution)/shard_map/ppermute | solution.py:11
  18.7 5.2 %collective-permute-start.1 = (bf16[2,2,2,2048]{3,2,1,0:T(2,128)(2,1)S(1)}, bf16[2,2,2,2048]{3,2,1,0:T(2,128)(2,1)S(1)}, u32[]{:S(2)}, u32[]{:S(2)}) collective-permute-start(bf16[2,2,2,2048]{3,2,1,0:T(2,128)(2,1)S(1)} %pad_maximum_fusion.10), channel_id=1, source_target_pairs={{0,128},{8,136},{16,144},{24,152},{32,160},{40,168},{48,176},{56,1... | collective-permute-start | bytes 98312 | tf_op jit(solution)/shard_map/ppermute | solution.py:11
  24.0 2.2 collective-permute-done.1
  26.3 3.5 %collective-permute-start.2 = (bf16[2,2,2,2,2048]{4,3,2,1,0:T(2,128)(2,1)S(1)}, bf16[2,2,2,2,2048]{4,3,2,1,0:T(2,128)(2,1)S(1)}, u32[]{:S(2)}, u32[]{:S(2)}) collective-permute-start(bf16[2,2,2,2,2048]{4,3,2,1,0:T(2,128)(2,1)S(1)} %pad_maximum_fusion.9), channel_id=1, source_target_pairs={{0,64},{8,72},{16,80},{24,88},{32,96},{40,104},{48,112},{56,120},{... | collective-permute-start | bytes 196616 | tf_op jit(solution)/shard_map/ppermute | solution.py:11
  29.8 2.6 %collective-permute-done.2 = bf16[2,2,2,2,2048]{4,3,2,1,0:T(2,128)(2,1)S(1)} collective-permute-done((bf16[2,2,2,2,2048]{4,3,2,1,0:T(2,128)(2,1)S(1)}, bf16[2,2,2,2,2048]{4,3,2,1,0:T(2,128)(2,1)S(1)}, u32[]{:S(2)}, u32[]{:S(2)}) %collective-permute-start.2) | collective-permute-done | bytes 65568 | tf_op jit(solution)/shard_map/ppermute | solution.py:11
  32.6 5.1 %collective-permute-start.3 = (bf16[2,2,2,2,2,2048]{5,4,3,2,1,0:T(2,128)(2,1)S(1)}, bf16[2,2,2,2,2,2048]{5,4,3,2,1,0:T(2,128)(2,1)S(1)}, u32[]{:S(2)}, u32[]{:S(2)}) collective-permute-start(bf16[2,2,2,2,2,2048]{5,4,3,2,1,0:T(2,128)(2,1)S(1)} %pad_maximum_fusion.8), channel_id=1, source_target_pairs={{0,32},{8,40},{16,48},{24,56},{32,0},{40,8},{48,16},{56,24},{64,96... | collective-permute-start | bytes 393224 | tf_op jit(solution)/shard_map/ppermute | solution.py:11
  38.0 3.1 %collective-permute-done.3 = bf16[2,2,2,2,2,2048]{5,4,3,2,1,0:T(2,128)(2,1)S(1)} collective-permute-done((bf16[2,2,2,2,2,2048]{5,4,3,2,1,0:T(2,128)(2,1)S(1)}, bf16[2,2,2,2,2,2048]{5,4,3,2,1,0:T(2,128)(2,1)S(1)}, u32[]{:S(2)}, u32[]{:S(2)}) %collective-permute-start.3) | collective-permute-done | bytes 131104 | tf_op jit(solution)/shard_map/ppermute | solution.py:11
  41.5 3.4 %collective-permute-start.4 = (bf16[2,2,2,2,2,2,2048]{6,5,4,3,2,1,0:T(2,128)(2,1)S(1)}, bf16[2,2,2,2,2,2,2048]{6,5,4,3,2,1,0:T(2,128)(2,1)S(1)}, u32[]{:S(2)}, u32[]{:S(2)}) collective-permute-start(bf16[2,2,2,2,2,2,2048]{6,5,4,3,2,1,0:T(2,128)(2,1)S(1)} %pad_maximum_fusion.7), channel_id=1, source_target_pairs={{0,16},{8,24},{16,0},{24,8},{32,48},{40,56},{48,32},{56,40},{64,80... | collective-permute-start | bytes 786440 | tf_op jit(solution)/shard_map/ppermute | solution.py:11
  46.8 3.0 %collective-permute-done.4 = bf16[2,2,2,2,2,2,2048]{6,5,4,3,2,1,0:T(2,128)(2,1)S(1)} collective-permute-done((bf16[2,2,2,2,2,2,2048]{6,5,4,3,2,1,0:T(2,128)(2,1)S(1)}, bf16[2,2,2,2,2,2,2048]{6,5,4,3,2,1,0:T(2,128)(2,1)S(1)}, u32[]{:S(2)}, u32[]{:S(2)}) %collective-permute-start.4) | collective-permute-done | bytes 262176 | tf_op jit(solution)/shard_map/ppermute | solution.py:11
  56.3 4.5 %collective-permute-start.7 = (bf16[128,4224]{0,1:T(8,128)(2,1)}, bf16[128,4224]{0,1:T(8,128)(2,1)}, u32[]{:S(2)}, u32[]{:S(2)}) collective-permute-start(bf16[128,4224]{0,1:T(8,128)(2,1)} %pad_maximum_fusion.2), channel_id=1, source_target_pairs={{0,128},{8,136},{16,144},{24,152},{32,160},{40,168},{48,176},{56,1... | collective-permute-start | bytes 3244040 | tf_op jit(solution)/shard_map/ppermute | solution.py:11
  60.8 2.3 collective-permute-start.6
  63.9 2.6 %pad_maximum_fusion.4 = bf16[2,2,2,2,2,2,2,2,2048]{8,7,6,5,4,3,2,1,0:T(2,128)(2,1)S(1)} fusion(bf16[1,2,2,2,2,2,2,2,2048]{8,7,6,5,4,3,2,1,0:T(2,128)(2,1)} %bitcast.13, bf16[1,2,2,2,2,2,2,2,2048]{8,7,6,5,4,3,2,1,0:T(2,128)(2,1)S(1)} %fusion.97), kind=kLoop, calls=%fused_computation.44 | loop fusion | flops 524288 | bytes 2097152 | tf_op jit(solution)/shard_map/stack | solution.py:37
  69.5 39.3 %collective-permute-done.7 = bf16[128,4224]{0,1:T(8,128)(2,1)} collective-permute-done((bf16[128,4224]{0,1:T(8,128)(2,1)}, bf16[128,4224]{0,1:T(8,128)(2,1)}, u32[]{:S(2)}, u32[]{:S(2)}) %collective-permute-start.7) | collective-permute-done | bytes 1081376 | tf_op jit(solution)/shard_map/ppermute | solution.py:11
  127.1 2.6 %copy.115 = f32[128,2048]{1,0:T(8,128)} copy(f32[128,2048]{0,1:T(8,128)} %bitcast.165) | data formatting | bytes 2097152 | tf_op jit(solution)/shard_map/reshape | solution.py:149
  129.7 2.6 %fusion.70 = f32[16,128,128]{1,2,0:T(8,128)} fusion(bf16[16,128,128]{1,2,0:T(8,128)(2,1)} %fusion.11, bf16[128,16,128]{0,2,1:T(8,128)(2,1)} %bitcast.139), kind=kOutput, calls=%fused_computation.127 | convolution fusion | flops 67108864 | bytes 2097152 | tf_op jit(solution)/shard_map/htg,thd->ghd/dot_general | solution.py:142
  132.3 2.6 %copy.114 = f32[128,2048]{1,0:T(8,128)} copy(f32[128,2048]{0,1:T(8,128)} %bitcast.156) | data formatting | bytes 2097152 | tf_op jit(solution)/shard_map/reshape | solution.py:149
  136.4 2.3 collective-permute-start.10
  140.0 2.2 fusion.67
  145.0 3.5 %collective-permute-start.11 = (f32[32,4096]{1,0:T(8,128)S(1)}, f32[32,4096]{1,0:T(8,128)S(1)}, u32[]{:S(2)}, u32[]{:S(2)}) collective-permute-start(f32[32,4096]{1,0:T(8,128)S(1)} %slice.152), channel_id=1, source_target_pairs={{0,16},{8,24},{16,0},{24,8},{32,48},{40,56},{48,32},{56,40},{64,80... | collective-permute-start | bytes 1572872 | tf_op jit(solution)/shard_map/ppermute | solution.py:11
  149.6 2.1 collective-permute-start.8
  152.0 9.3 %collective-permute-done.11 = f32[32,4096]{1,0:T(8,128)S(1)} collective-permute-done((f32[32,4096]{1,0:T(8,128)S(1)}, f32[32,4096]{1,0:T(8,128)S(1)}, u32[]{:S(2)}, u32[]{:S(2)}) %collective-permute-start.11) | collective-permute-done | bytes 524320 | tf_op jit(solution)/shard_map/ppermute | solution.py:11
  163.0 4.9 %collective-permute-start.12 = (f32[16,4096]{1,0:T(8,128)}, f32[16,4096]{1,0:T(8,128)S(1)}, u32[]{:S(2)}, u32[]{:S(2)}) collective-permute-start(f32[16,4096]{1,0:T(8,128)} %slice.154), channel_id=1, source_target_pairs={{0,32},{8,40},{16,48},{24,56},{32,0},{40,8},{48,16},{56,24},{64,96... | collective-permute-start | bytes 786440 | tf_op jit(solution)/shard_map/ppermute | solution.py:11
  169.5 2.0 copy.118
  171.5 2.0 copy.119
  175.5 4.8 %collective-permute-start.9 = (bf16[128,2048]{0,1:T(8,128)(2,1)}, bf16[128,2048]{0,1:T(8,128)(2,1)S(1)}, u32[]{:S(2)}, u32[]{:S(2)}) collective-permute-start(bf16[128,2048]{0,1:T(8,128)(2,1)} %bitcast.168), channel_id=1, source_target_pairs={{0,128},{8,136},{16,144},{24,152},{32,160},{40,168},{48,176},{56,1... | collective-permute-start | bytes 1572872 | tf_op jit(solution)/shard_map/ppermute | solution.py:11
  181.3 3.0 %collective-permute-start.13 = (f32[8,4096]{1,0:T(8,128)S(1)}, f32[8,4096]{1,0:T(8,128)S(1)}, u32[]{:S(2)}, u32[]{:S(2)}) collective-permute-start(f32[8,4096]{1,0:T(8,128)S(1)} %slice.156), channel_id=1, source_target_pairs={{0,64},{8,72},{16,80},{24,88},{32,96},{40,104},{48,112},{56,120},{... | collective-permute-start | bytes 393224 | tf_op jit(solution)/shard_map/ppermute | solution.py:11
  185.6 15.1 %collective-permute-done.13 = f32[8,4096]{1,0:T(8,128)S(1)} collective-permute-done((f32[8,4096]{1,0:T(8,128)S(1)}, f32[8,4096]{1,0:T(8,128)S(1)}, u32[]{:S(2)}, u32[]{:S(2)}) %collective-permute-start.13) | collective-permute-done | bytes 131104 | tf_op jit(solution)/shard_map/ppermute | solution.py:11
  200.8 6.3 %collective-permute-start.14 = (f32[4,4096]{1,0:T(4,128)S(1)}, f32[4,4096]{1,0:T(4,128)S(1)}, u32[]{:S(2)}, u32[]{:S(2)}) collective-permute-start(f32[4,4096]{1,0:T(4,128)S(1)} %slice.158), channel_id=1, source_target_pairs={{0,128},{8,136},{16,144},{24,152},{32,160},{40,168},{48,176},{56,1... | collective-permute-start | bytes 196616 | tf_op jit(solution)/shard_map/ppermute | solution.py:11
  207.1 7.4 %collective-permute-done.16 = bf16[128,2048]{0,1:T(8,128)(2,1)S(1)} collective-permute-done((bf16[128,2048]{0,1:T(8,128)(2,1)}, bf16[128,2048]{0,1:T(8,128)(2,1)S(1)}, u32[]{:S(2)}, u32[]{:S(2)}) %collective-permute-start.16) | collective-permute-done | bytes 524320 | tf_op jit(solution)/shard_map/ppermute | solution.py:11
  214.5 2.4 fusion.16
  216.9 9.4 %collective-permute-done.14 = f32[4,4096]{1,0:T(4,128)S(1)} collective-permute-done((f32[4,4096]{1,0:T(4,128)S(1)}, f32[4,4096]{1,0:T(4,128)S(1)}, u32[]{:S(2)}, u32[]{:S(2)}) %collective-permute-start.14) | collective-permute-done | bytes 65568 | tf_op jit(solution)/shard_map/ppermute | solution.py:11
  226.3 4.8 %collective-permute-start.15 = (f32[2,4096]{1,0:T(2,128)S(1)}, f32[2,4096]{1,0:T(2,128)S(1)}, u32[]{:S(2)}, u32[]{:S(2)}) collective-permute-start(f32[2,4096]{1,0:T(2,128)S(1)} %slice.160), channel_id=1, source_target_pairs={{0,256},{8,264},{16,272},{24,280},{32,288},{40,296},{48,304},{56,3... | collective-permute-start | bytes 98312 | tf_op jit(solution)/shard_map/ppermute | solution.py:11
  (145 shorter events, 61.5 us)
Async XLA Ops:
  0.6 37.1 %copy-start.23 = (bf16[128,2048]{1,0:T(8,128)(2,1)S(1)}, bf16[128,2048]{1,0:T(8,128)(2,1)}, u32[]{:S(2)}) copy-start(bf16[128,2048]{1,0:T(8,128)(2,1)} %param.6) | copy-start | bytes 1572868
  4.8 40.2 %copy-start.19 = (bf16[128,2048]{1,0:T(8,128)(2,1)S(1)}, bf16[128,2048]{1,0:T(8,128)(2,1)}, u32[]{:S(2)}) copy-start(bf16[128,2048]{1,0:T(8,128)(2,1)} %param.7) | copy-start | bytes 1572868
  4.8 13.9 %collective-permute-start = (bf16[2,2,2048]{2,1,0:T(2,128)(2,1)S(1)}, bf16[2,2,2048]{2,1,0:T(2,128)(2,1)S(1)}, u32[]{:S(2)}, u32[]{:S(2)}) collective-permute-start(bf16[2,2,2048]{2,1,0:T(2,128)(2,1)S(1)} %pad_maximum_fusion.11), channel_id=1, source_target_pairs={{0,256},{8,264},{16,272},{24,280},{32,288},{40,296},{48,304},{56,3... | collective-permute-start | bytes 49160 | tf_op jit(solution)/shard_map/ppermute | solution.py:11
  15.3 29.6 %copy-start.10 = (bf16[128,2048]{0,1:T(8,128)(2,1)}, bf16[128,2048]{0,1:T(8,128)(2,1)S(1)}, u32[]{:S(2)}) copy-start(bf16[128,2048]{0,1:T(8,128)(2,1)S(1)} %copy.80) | copy-start | bytes 1572868
  16.9 28.1 %copy-start.12 = (bf16[128,2048]{0,1:T(8,128)(2,1)}, bf16[128,2048]{0,1:T(8,128)(2,1)S(1)}, u32[]{:S(2)}) copy-start(bf16[128,2048]{0,1:T(8,128)(2,1)S(1)} %copy.79) | copy-start | bytes 1572868
  18.7 7.4 %collective-permute-start.1 = (bf16[2,2,2,2048]{3,2,1,0:T(2,128)(2,1)S(1)}, bf16[2,2,2,2048]{3,2,1,0:T(2,128)(2,1)S(1)}, u32[]{:S(2)}, u32[]{:S(2)}) collective-permute-start(bf16[2,2,2,2048]{3,2,1,0:T(2,128)(2,1)S(1)} %pad_maximum_fusion.10), channel_id=1, source_target_pairs={{0,128},{8,136},{16,144},{24,152},{32,160},{40,168},{48,176},{56,1... | collective-permute-start | bytes 98312 | tf_op jit(solution)/shard_map/ppermute | solution.py:11
  26.3 6.2 %collective-permute-start.2 = (bf16[2,2,2,2,2048]{4,3,2,1,0:T(2,128)(2,1)S(1)}, bf16[2,2,2,2,2048]{4,3,2,1,0:T(2,128)(2,1)S(1)}, u32[]{:S(2)}, u32[]{:S(2)}) collective-permute-start(bf16[2,2,2,2,2048]{4,3,2,1,0:T(2,128)(2,1)S(1)} %pad_maximum_fusion.9), channel_id=1, source_target_pairs={{0,64},{8,72},{16,80},{24,88},{32,96},{40,104},{48,112},{56,120},{... | collective-permute-start | bytes 196616 | tf_op jit(solution)/shard_map/ppermute | solution.py:11
  32.6 22.2 %copy-start.20 = (bf16[128,2048]{1,0:T(8,128)(2,1)S(1)}, bf16[128,2048]{1,0:T(8,128)(2,1)}, u32[]{:S(2)}) copy-start(bf16[128,2048]{1,0:T(8,128)(2,1)} %param.8) | copy-start | bytes 1572868
  32.6 8.5 %collective-permute-start.3 = (bf16[2,2,2,2,2,2048]{5,4,3,2,1,0:T(2,128)(2,1)S(1)}, bf16[2,2,2,2,2,2048]{5,4,3,2,1,0:T(2,128)(2,1)S(1)}, u32[]{:S(2)}, u32[]{:S(2)}) collective-permute-start(bf16[2,2,2,2,2,2048]{5,4,3,2,1,0:T(2,128)(2,1)S(1)} %pad_maximum_fusion.8), channel_id=1, source_target_pairs={{0,32},{8,40},{16,48},{24,56},{32,0},{40,8},{48,16},{56,24},{64,96... | collective-permute-start | bytes 393224 | tf_op jit(solution)/shard_map/ppermute | solution.py:11
  38.0 72.2 %copy-start = (bf16[128,2048]{0,1:T(8,128)(2,1)}, bf16[128,2048]{0,1:T(8,128)(2,1)S(1)}, u32[]{:S(2)}) copy-start(bf16[128,2048]{0,1:T(8,128)(2,1)S(1)} %copy.138) | copy-start | bytes 1572868
  41.1 3.8 %copy-start.25 = (bf16[2,2,2,2,2,2048]{5,4,3,2,1,0:T(2,128)(2,1)}, bf16[2,2,2,2,2,2048]{5,4,3,2,1,0:T(2,128)(2,1)S(1)}, u32[]{:S(2)}) copy-start(bf16[2,2,2,2,2,2048]{5,4,3,2,1,0:T(2,128)(2,1)S(1)} %collective-permute-done.3) | copy-start | bytes 393220
  41.5 8.3 %collective-permute-start.4 = (bf16[2,2,2,2,2,2,2048]{6,5,4,3,2,1,0:T(2,128)(2,1)S(1)}, bf16[2,2,2,2,2,2,2048]{6,5,4,3,2,1,0:T(2,128)(2,1)S(1)}, u32[]{:S(2)}, u32[]{:S(2)}) collective-permute-start(bf16[2,2,2,2,2,2,2048]{6,5,4,3,2,1,0:T(2,128)(2,1)S(1)} %pad_maximum_fusion.7), channel_id=1, source_target_pairs={{0,16},{8,24},{16,0},{24,8},{32,48},{40,56},{48,32},{56,40},{64,80... | collective-permute-start | bytes 786440 | tf_op jit(solution)/shard_map/ppermute | solution.py:11
  51.3 12.5 %collective-permute-start.5 = (bf16[2,2,2,2,2,2,2,2048]{7,6,5,4,3,2,1,0:T(2,128)(2,1)}, bf16[2,2,2,2,2,2,2,2048]{7,6,5,4,3,2,1,0:T(2,128)(2,1)}, u32[]{:S(2)}, u32[]{:S(2)}) collective-permute-start(bf16[2,2,2,2,2,2,2,2048]{7,6,5,4,3,2,1,0:T(2,128)(2,1)} %pad_maximum_fusion.6), channel_id=1, source_target_pairs={{0,8},{8,0},{16,24},{24,16},{32,40},{40,32},{48,56},{56,48},{64,72... | collective-permute-start | bytes 1572872 | tf_op jit(solution)/shard_map/ppermute | solution.py:11
  54.6 12.6 %copy-start.2 = (bf16[128,2048]{0,1:T(8,128)(2,1)}, bf16[128,2048]{0,1:T(8,128)(2,1)S(1)}, u32[]{:S(2)}) copy-start(bf16[128,2048]{0,1:T(8,128)(2,1)S(1)} %copy.90) | copy-start | bytes 1572868
  56.3 52.5 %collective-permute-start.7 = (bf16[128,4224]{0,1:T(8,128)(2,1)}, bf16[128,4224]{0,1:T(8,128)(2,1)}, u32[]{:S(2)}, u32[]{:S(2)}) collective-permute-start(bf16[128,4224]{0,1:T(8,128)(2,1)} %pad_maximum_fusion.2), channel_id=1, source_target_pairs={{0,128},{8,136},{16,144},{24,152},{32,160},{40,168},{48,176},{56,1... | collective-permute-start | bytes 3244040 | tf_op jit(solution)/shard_map/ppermute | solution.py:11
  60.8 49.7 %collective-permute-start.6 = (bf16[128,4224]{0,1:T(8,128)(2,1)}, bf16[128,4224]{0,1:T(8,128)(2,1)}, u32[]{:S(2)}, u32[]{:S(2)}) collective-permute-start(bf16[128,4224]{0,1:T(8,128)(2,1)} %pad_maximum_fusion.2), channel_id=1, source_target_pairs={{0,8},{8,0},{16,24},{24,16},{32,40},{40,32},{48,56},{56,48},{64,72... | collective-permute-start | bytes 3244040 | tf_op jit(solution)/shard_map/ppermute | solution.py:11
  69.2 41.0 %copy-start.14 = (bf16[128,16,128]{0,2,1:T(8,128)(2,1)}, bf16[128,16,128]{0,2,1:T(8,128)(2,1)S(1)}, u32[]{:S(2)}) copy-start(bf16[128,16,128]{0,2,1:T(8,128)(2,1)S(1)} %copy.108) | copy-start | bytes 1572868
  110.5 5.4 %copy-start.26 = (s32[128]{0:T(128)S(1)}, s32[128]{0:T(128)}, u32[]{:S(2)}) copy-start(s32[128]{0:T(128)} %param.10) | copy-start | bytes 1540
  118.6 4.3 %copy-start.5 = (bf16[16,128,384]{2,1,0:T(8,128)(2,1)}, bf16[16,128,384]{2,1,0:T(8,128)(2,1)S(1)}, u32[]{:S(2)}) copy-start(bf16[16,128,384]{2,1,0:T(8,128)(2,1)S(1)} %fusion.21) | copy-start | bytes 4718596
  136.4 8.4 %collective-permute-start.10 = (f32[64,4096]{1,0:T(8,128)S(1)}, f32[64,4096]{1,0:T(8,128)S(1)}, u32[]{:S(2)}, u32[]{:S(2)}) collective-permute-start(f32[64,4096]{1,0:T(8,128)S(1)} %pad_maximum_fusion.3), channel_id=1, source_target_pairs={{0,8},{8,0},{16,24},{24,16},{32,40},{40,32},{48,56},{56,48},{64,72... | collective-permute-start | bytes 3145736 | tf_op jit(solution)/shard_map/ppermute | solution.py:11
  144.8 7.0 %copy-start.15 = (bf16[128,16,128]{0,2,1:T(8,128)(2,1)S(1)}, bf16[128,16,128]{0,2,1:T(8,128)(2,1)}, u32[]{:S(2)}) copy-start(bf16[128,16,128]{0,2,1:T(8,128)(2,1)} %copy-done.14) | copy-start | bytes 1572868
  144.8 7.0 %copy-start.22 = (bf16[16,128,128]{1,2,0:T(8,128)(2,1)S(1)}, bf16[16,128,128]{1,2,0:T(8,128)(2,1)}, u32[]{:S(2)}) copy-start(bf16[16,128,128]{1,2,0:T(8,128)(2,1)} %fusion.11) | copy-start | bytes 1572868
  145.0 16.4 %collective-permute-start.11 = (f32[32,4096]{1,0:T(8,128)S(1)}, f32[32,4096]{1,0:T(8,128)S(1)}, u32[]{:S(2)}, u32[]{:S(2)}) collective-permute-start(f32[32,4096]{1,0:T(8,128)S(1)} %slice.152), channel_id=1, source_target_pairs={{0,16},{8,24},{16,0},{24,8},{32,48},{40,56},{48,32},{56,40},{64,80... | collective-permute-start | bytes 1572872 | tf_op jit(solution)/shard_map/ppermute | solution.py:11
  148.5 19.4 %copy-start.9 = (bf16[384,2048]{0,1:T(8,128)(2,1)S(1)}, bf16[384,2048]{0,1:T(8,128)(2,1)}, u32[]{:S(2)}) copy-start(bf16[384,2048]{0,1:T(8,128)(2,1)} %get-tuple-element.56) | copy-start | bytes 4718596
  149.6 34.8 %collective-permute-start.8 = (bf16[128,4096]{0,1:T(8,128)(2,1)}, bf16[128,4096]{0,1:T(8,128)(2,1)}, u32[]{:S(2)}, u32[]{:S(2)}) collective-permute-start(bf16[128,4096]{0,1:T(8,128)(2,1)} %pad_maximum_fusion.5), channel_id=1, source_target_pairs={{0,8},{8,0},{16,24},{24,16},{32,40},{40,32},{48,56},{56,48},{64,72... | collective-permute-start | bytes 3145736 | tf_op jit(solution)/shard_map/ppermute | solution.py:11
  163.0 17.3 %collective-permute-start.12 = (f32[16,4096]{1,0:T(8,128)}, f32[16,4096]{1,0:T(8,128)S(1)}, u32[]{:S(2)}, u32[]{:S(2)}) collective-permute-start(f32[16,4096]{1,0:T(8,128)} %slice.154), channel_id=1, source_target_pairs={{0,32},{8,40},{16,48},{24,56},{32,0},{40,8},{48,16},{56,24},{64,96... | collective-permute-start | bytes 786440 | tf_op jit(solution)/shard_map/ppermute | solution.py:11
  173.6 40.9 %collective-permute-start.16 = (bf16[128,2048]{0,1:T(8,128)(2,1)}, bf16[128,2048]{0,1:T(8,128)(2,1)S(1)}, u32[]{:S(2)}, u32[]{:S(2)}) collective-permute-start(bf16[128,2048]{0,1:T(8,128)(2,1)} %bitcast.169), channel_id=1, source_target_pairs={{0,128},{8,136},{16,144},{24,152},{32,160},{40,168},{48,176},{56,1... | collective-permute-start | bytes 1572872 | tf_op jit(solution)/shard_map/ppermute | solution.py:11
  175.5 55.6 %collective-permute-start.9 = (bf16[128,2048]{0,1:T(8,128)(2,1)}, bf16[128,2048]{0,1:T(8,128)(2,1)S(1)}, u32[]{:S(2)}, u32[]{:S(2)}) collective-permute-start(bf16[128,2048]{0,1:T(8,128)(2,1)} %bitcast.168), channel_id=1, source_target_pairs={{0,128},{8,136},{16,144},{24,152},{32,160},{40,168},{48,176},{56,1... | collective-permute-start | bytes 1572872 | tf_op jit(solution)/shard_map/ppermute | solution.py:11
  181.3 19.4 %collective-permute-start.13 = (f32[8,4096]{1,0:T(8,128)S(1)}, f32[8,4096]{1,0:T(8,128)S(1)}, u32[]{:S(2)}, u32[]{:S(2)}) collective-permute-start(f32[8,4096]{1,0:T(8,128)S(1)} %slice.156), channel_id=1, source_target_pairs={{0,64},{8,72},{16,80},{24,88},{32,96},{40,104},{48,112},{56,120},{... | collective-permute-start | bytes 393224 | tf_op jit(solution)/shard_map/ppermute | solution.py:11
  200.8 25.5 %collective-permute-start.14 = (f32[4,4096]{1,0:T(4,128)S(1)}, f32[4,4096]{1,0:T(4,128)S(1)}, u32[]{:S(2)}, u32[]{:S(2)}) collective-permute-start(f32[4,4096]{1,0:T(4,128)S(1)} %slice.158), channel_id=1, source_target_pairs={{0,128},{8,136},{16,144},{24,152},{32,160},{40,168},{48,176},{56,1... | collective-permute-start | bytes 196616 | tf_op jit(solution)/shard_map/ppermute | solution.py:11
  226.3 9.7 %collective-permute-start.15 = (f32[2,4096]{1,0:T(2,128)S(1)}, f32[2,4096]{1,0:T(2,128)S(1)}, u32[]{:S(2)}, u32[]{:S(2)}) collective-permute-start(f32[2,4096]{1,0:T(2,128)S(1)} %slice.160), channel_id=1, source_target_pairs={{0,256},{8,264},{16,272},{24,280},{32,288},{40,296},{48,304},{56,3... | collective-permute-start | bytes 98312 | tf_op jit(solution)/shard_map/ppermute | solution.py:11
  231.1 5.0 %copy-start.27 = (s32[2]{0:T(128)S(1)}, s32[2]{0:T(128)}, u32[]{:S(2)}) copy-start(s32[2]{0:T(128)} %param.11) | copy-start | bytes 28
  (13 other events, 32.5 us)

commit v7 on v6

--- a/solution.py
+++ b/solution.py
@@ -23,7 +23,15 @@
         return array.reshape(array.shape[0], HEADS, head_size)
 
     per_block = global_offsets.shape[0]
-    picked = jnp.stack([keys[global_offsets], values[global_offsets]], 0)
+    picked = jnp.stack(
+        [
+            jnp.concatenate(
+                [lax.dynamic_slice_in_dim(array, global_offsets[j], 1) for j in range(per_block)], 0
+            )
+            for array in (keys, values)
+        ],
+        0,
+    )
     gather_bits = list(range(log_shards))[::-1]
     z_steps = min(3, log_shards)
     doc_columns = 128
@@ -152,12 +160,12 @@
         half = owned.shape[0] // 2
         owned = owned[:half] + from_partner(owned[half:], "seq", bit)
     owned = jnp.concatenate([temper * owned[:, :columns], owned[:, columns:]], 1)
-    placement = (jnp.arange(rows_here, dtype=jnp.int32)[:, None] == global_offsets[None, :]).astype(
-        jnp.float32
-    )
-    spread_rows = jnp.dot(
-        placement, owned, precision=lax.Precision.HIGHEST, preferred_element_type=jnp.float32
-    )
+    positions = jnp.arange(rows_here, dtype=jnp.int32)[:, None]
+    spread_rows = jnp.zeros((rows_here, 2 * columns), jnp.float32)
+    for j in range(per_block):
+        spread_rows = spread_rows + jnp.where(
+            positions == global_offsets[j], owned[j][None, :], 0.0
+        )
     key_grad = (key_sum.reshape(rows_here, columns) + spread_rows[:, :columns]).astype(jnp.bfloat16)
     value_grad = (value_sum.reshape(rows_here, columns) + spread_rows[:, columns:]).astype(
         jnp.bfloat16

time: 240 us -> 243 us (1.012)
  between operations: 1.44 us -> 5.37 us
    gather x2 -> x0, local copies, waits for them, and re-layouts: 3.36 us -> none  [body(): picked = jnp.stack([keys[global_offsets], values[global_offsets]], 0)]
    unnamed x62 -> x60, local copies, waits for them, and re-layouts: 10.6 us -> 10.5 us
  transfers between devices with their start and end apart: 17 -> 17, of which waited for: 10 -> 10; matrix products, arithmetic and copies ran while one was open for 17% -> 16% of each run, Pallas kernels for 0% -> 0%
where the time goes in v7:
time: 243 us; the launch traced here: 242 us
  waiting for transfers between devices  94.2 us (39%)
  starting transfers between devices  68.6 us (28%)
  local copies, waits for them, and re-layouts  30 us (12%)
  other arithmetic  23.9 us (10%)
  matrix products  19.7 us (8%)
  between operations  5.37 us (2%)
    ppermute x17, waiting for transfers between devices, from_partner(): lax.ppermute(array, axis, [(i, i ^ 1 << stride) for i in range(lax.axis_s...  94.2 us
    ppermute x17, starting transfers between devices, from_partner(): lax.ppermute(array, axis, [(i, i ^ 1 << stride) for i in range(lax.axis_s...  68.6 us
    unnamed x60, local copies, waits for them, and re-layouts  10.5 us
    another operation x11, other arithmetic, body(): gathered = jnp.stack([gathered, from_partner(gathered, 'seq', bit)], 0)  6.13 us
  transfers between devices with their start and end apart: 17, of which 10 were waited for; matrix products, arithmetic and copies ran while one was open for 16% of the time, Pallas kernels for 0%

profile of v7, /device:TPU:24, one launch (start us, length us, event | category | flops | bytes accessed | tf_op | source)
XLA Modules:
  0.0 241.7 jit_solution(16452827455907687634)
XLA Ops:
  6.8 9.1 %collective-permute-start = (bf16[2,2,2048]{2,1,0:T(2,128)(2,1)S(1)}, bf16[2,2,2048]{2,1,0:T(2,128)(2,1)S(1)}, u32[]{:S(2)}, u32[]{:S(2)}) collective-permute-start(bf16[2,2,2048]{2,1,0:T(2,128)(2,1)S(1)} %pad_maximum_fusion.12), channel_id=1, source_target_pairs={{0,256},{8,264},{16,272},{24,280},{32,288},{40,296},{48,304},{56,3... | collective-permute-start | bytes 49160 | tf_op jit(solution)/shard_map/ppermute | solution.py:11
  21.0 5.3 %collective-permute-start.1 = (bf16[2,2,2,2048]{3,2,1,0:T(2,128)(2,1)S(1)}, bf16[2,2,2,2048]{3,2,1,0:T(2,128)(2,1)S(1)}, u32[]{:S(2)}, u32[]{:S(2)}) collective-permute-start(bf16[2,2,2,2048]{3,2,1,0:T(2,128)(2,1)S(1)} %pad_maximum_fusion.10), channel_id=1, source_target_pairs={{0,128},{8,136},{16,144},{24,152},{32,160},{40,168},{48,176},{56,1... | collective-permute-start | bytes 98312 | tf_op jit(solution)/shard_map/ppermute | solution.py:11
  26.3 2.2 collective-permute-done.1
  28.6 3.5 %collective-permute-start.2 = (bf16[2,2,2,2,2048]{4,3,2,1,0:T(2,128)(2,1)S(1)}, bf16[2,2,2,2,2048]{4,3,2,1,0:T(2,128)(2,1)S(1)}, u32[]{:S(2)}, u32[]{:S(2)}) collective-permute-start(bf16[2,2,2,2,2048]{4,3,2,1,0:T(2,128)(2,1)S(1)} %pad_maximum_fusion.9), channel_id=1, source_target_pairs={{0,64},{8,72},{16,80},{24,88},{32,96},{40,104},{48,112},{56,120},{... | collective-permute-start | bytes 196616 | tf_op jit(solution)/shard_map/ppermute | solution.py:11
  32.2 2.6 %collective-permute-done.2 = bf16[2,2,2,2,2048]{4,3,2,1,0:T(2,128)(2,1)S(1)} collective-permute-done((bf16[2,2,2,2,2048]{4,3,2,1,0:T(2,128)(2,1)S(1)}, bf16[2,2,2,2,2048]{4,3,2,1,0:T(2,128)(2,1)S(1)}, u32[]{:S(2)}, u32[]{:S(2)}) %collective-permute-start.2) | collective-permute-done | bytes 65568 | tf_op jit(solution)/shard_map/ppermute | solution.py:11
  35.0 4.9 %collective-permute-start.3 = (bf16[2,2,2,2,2,2048]{5,4,3,2,1,0:T(2,128)(2,1)S(1)}, bf16[2,2,2,2,2,2048]{5,4,3,2,1,0:T(2,128)(2,1)S(1)}, u32[]{:S(2)}, u32[]{:S(2)}) collective-permute-start(bf16[2,2,2,2,2,2048]{5,4,3,2,1,0:T(2,128)(2,1)S(1)} %pad_maximum_fusion.8), channel_id=1, source_target_pairs={{0,32},{8,40},{16,48},{24,56},{32,0},{40,8},{48,16},{56,24},{64,96... | collective-permute-start | bytes 393224 | tf_op jit(solution)/shard_map/ppermute | solution.py:11
  40.4 2.9 %collective-permute-done.3 = bf16[2,2,2,2,2,2048]{5,4,3,2,1,0:T(2,128)(2,1)S(1)} collective-permute-done((bf16[2,2,2,2,2,2048]{5,4,3,2,1,0:T(2,128)(2,1)S(1)}, bf16[2,2,2,2,2,2048]{5,4,3,2,1,0:T(2,128)(2,1)S(1)}, u32[]{:S(2)}, u32[]{:S(2)}) %collective-permute-start.3) | collective-permute-done | bytes 131104 | tf_op jit(solution)/shard_map/ppermute | solution.py:11
  43.7 3.4 %collective-permute-start.4 = (bf16[2,2,2,2,2,2,2048]{6,5,4,3,2,1,0:T(2,128)(2,1)S(1)}, bf16[2,2,2,2,2,2,2048]{6,5,4,3,2,1,0:T(2,128)(2,1)S(1)}, u32[]{:S(2)}, u32[]{:S(2)}) collective-permute-start(bf16[2,2,2,2,2,2,2048]{6,5,4,3,2,1,0:T(2,128)(2,1)S(1)} %pad_maximum_fusion.7), channel_id=1, source_target_pairs={{0,16},{8,24},{16,0},{24,8},{32,48},{40,56},{48,32},{56,40},{64,80... | collective-permute-start | bytes 786440 | tf_op jit(solution)/shard_map/ppermute | solution.py:11
  48.8 3.2 %collective-permute-done.4 = bf16[2,2,2,2,2,2,2048]{6,5,4,3,2,1,0:T(2,128)(2,1)S(1)} collective-permute-done((bf16[2,2,2,2,2,2,2048]{6,5,4,3,2,1,0:T(2,128)(2,1)S(1)}, bf16[2,2,2,2,2,2,2048]{6,5,4,3,2,1,0:T(2,128)(2,1)S(1)}, u32[]{:S(2)}, u32[]{:S(2)}) %collective-permute-start.4) | collective-permute-done | bytes 262176 | tf_op jit(solution)/shard_map/ppermute | solution.py:11
  58.5 4.5 %collective-permute-start.7 = (bf16[128,4224]{0,1:T(8,128)(2,1)}, bf16[128,4224]{0,1:T(8,128)(2,1)}, u32[]{:S(2)}, u32[]{:S(2)}) collective-permute-start(bf16[128,4224]{0,1:T(8,128)(2,1)} %pad_maximum_fusion.2), channel_id=1, source_target_pairs={{0,128},{8,136},{16,144},{24,152},{32,160},{40,168},{48,176},{56,1... | collective-permute-start | bytes 3244040 | tf_op jit(solution)/shard_map/ppermute | solution.py:11
  63.0 2.3 collective-permute-start.6
  66.1 2.6 %pad_maximum_fusion.4 = bf16[2,2,2,2,2,2,2,2,2048]{8,7,6,5,4,3,2,1,0:T(2,128)(2,1)S(1)} fusion(bf16[1,2,2,2,2,2,2,2,2048]{8,7,6,5,4,3,2,1,0:T(2,128)(2,1)} %bitcast.15, bf16[1,2,2,2,2,2,2,2,2048]{8,7,6,5,4,3,2,1,0:T(2,128)(2,1)S(1)} %fusion.93), kind=kLoop, calls=%fused_computation.43 | loop fusion | flops 524288 | bytes 2097152 | tf_op jit(solution)/shard_map/stack | solution.py:45
  71.8 39.3 %collective-permute-done.7 = bf16[128,4224]{0,1:T(8,128)(2,1)} collective-permute-done((bf16[128,4224]{0,1:T(8,128)(2,1)}, bf16[128,4224]{0,1:T(8,128)(2,1)}, u32[]{:S(2)}, u32[]{:S(2)}) %collective-permute-start.7) | collective-permute-done | bytes 1081376 | tf_op jit(solution)/shard_map/ppermute | solution.py:11
  123.9 2.7 %fusion.63 = (bf16[384,16,128]{0,2,1:T(8,128)(2,1)}, f32[384,16,128]{0,2,1:T(8,128)}) fusion(bf16[128,16,128]{0,2,1:T(8,128)(2,1)S(1)} %bitcast.150, bf16[16,128,384]{2,1,0:T(8,128)(2,1)S(1)} %fusion.21), kind=kOutput, calls=%fused_computation.127 | convolution fusion | flops 202113024 | bytes 6815744 | tf_op jit(solution)/shard_map/htu,thd->uhd/dot_general | solution.py:125
  130.8 2.6 %copy.76 = f32[128,2048]{1,0:T(8,128)} copy(f32[128,2048]{0,1:T(8,128)} %bitcast.171) | data formatting | bytes 2097152 | tf_op jit(solution)/shard_map/reshape | solution.py:157
  133.4 2.7 %fusion.66 = f32[16,128,128]{1,2,0:T(8,128)} fusion(bf16[16,128,128]{1,2,0:T(8,128)(2,1)} %fusion.11, bf16[128,16,128]{0,2,1:T(8,128)(2,1)} %bitcast.145), kind=kOutput, calls=%fused_computation.130 | convolution fusion | flops 67108864 | bytes 2097152 | tf_op jit(solution)/shard_map/htg,thd->ghd/dot_general | solution.py:150
  136.0 2.6 %copy.75 = f32[128,2048]{1,0:T(8,128)} copy(f32[128,2048]{0,1:T(8,128)} %bitcast.162) | data formatting | bytes 2097152 | tf_op jit(solution)/shard_map/reshape | solution.py:157
  140.1 2.3 collective-permute-start.10
  148.1 2.5 %collective-permute-start.8 = (bf16[128,4096]{0,1:T(8,128)(2,1)}, bf16[128,4096]{0,1:T(8,128)(2,1)}, u32[]{:S(2)}, u32[]{:S(2)}) collective-permute-start(bf16[128,4096]{0,1:T(8,128)(2,1)} %pad_maximum_fusion.5), channel_id=1, source_target_pairs={{0,8},{8,0},{16,24},{24,16},{32,40},{40,32},{48,56},{56,48},{64,72... | collective-permute-start | bytes 3145736 | tf_op jit(solution)/shard_map/ppermute | solution.py:11
  150.9 3.4 %collective-permute-start.11 = (f32[32,4096]{1,0:T(8,128)S(1)}, f32[32,4096]{1,0:T(8,128)S(1)}, u32[]{:S(2)}, u32[]{:S(2)}) collective-permute-start(f32[32,4096]{1,0:T(8,128)S(1)} %slice.168), channel_id=1, source_target_pairs={{0,16},{8,24},{16,0},{24,8},{32,48},{40,56},{48,32},{56,40},{64,80... | collective-permute-start | bytes 1572872 | tf_op jit(solution)/shard_map/ppermute | solution.py:11
  154.8 11.8 %collective-permute-done.11 = f32[32,4096]{1,0:T(8,128)S(1)} collective-permute-done((f32[32,4096]{1,0:T(8,128)S(1)}, f32[32,4096]{1,0:T(8,128)S(1)}, u32[]{:S(2)}, u32[]{:S(2)}) %collective-permute-start.11) | collective-permute-done | bytes 524320 | tf_op jit(solution)/shard_map/ppermute | solution.py:11
  167.4 4.9 %collective-permute-start.12 = (f32[16,4096]{1,0:T(8,128)}, f32[16,4096]{1,0:T(8,128)S(1)}, u32[]{:S(2)}, u32[]{:S(2)}) collective-permute-start(f32[16,4096]{1,0:T(8,128)} %slice.170), channel_id=1, source_target_pairs={{0,32},{8,40},{16,48},{24,56},{32,0},{40,8},{48,16},{56,24},{64,96... | collective-permute-start | bytes 786440 | tf_op jit(solution)/shard_map/ppermute | solution.py:11
  174.0 2.0 copy.79
  176.0 2.0 copy.80
  180.0 4.8 %collective-permute-start.9 = (bf16[128,2048]{0,1:T(8,128)(2,1)}, bf16[128,2048]{0,1:T(8,128)(2,1)S(1)}, u32[]{:S(2)}, u32[]{:S(2)}) collective-permute-start(bf16[128,2048]{0,1:T(8,128)(2,1)} %bitcast.174), channel_id=1, source_target_pairs={{0,128},{8,136},{16,144},{24,152},{32,160},{40,168},{48,176},{56,1... | collective-permute-start | bytes 1572872 | tf_op jit(solution)/shard_map/ppermute | solution.py:11
  185.8 3.1 %collective-permute-start.13 = (f32[8,4096]{1,0:T(8,128)S(1)}, f32[8,4096]{1,0:T(8,128)S(1)}, u32[]{:S(2)}, u32[]{:S(2)}) collective-permute-start(f32[8,4096]{1,0:T(8,128)S(1)} %slice.172), channel_id=1, source_target_pairs={{0,64},{8,72},{16,80},{24,88},{32,96},{40,104},{48,112},{56,120},{... | collective-permute-start | bytes 393224 | tf_op jit(solution)/shard_map/ppermute | solution.py:11
  190.2 14.6 %collective-permute-done.13 = f32[8,4096]{1,0:T(8,128)S(1)} collective-permute-done((f32[8,4096]{1,0:T(8,128)S(1)}, f32[8,4096]{1,0:T(8,128)S(1)}, u32[]{:S(2)}, u32[]{:S(2)}) %collective-permute-start.13) | collective-permute-done | bytes 131104 | tf_op jit(solution)/shard_map/ppermute | solution.py:11
  204.8 6.5 %collective-permute-start.14 = (f32[4,4096]{1,0:T(4,128)S(1)}, f32[4,4096]{1,0:T(4,128)S(1)}, u32[]{:S(2)}, u32[]{:S(2)}) collective-permute-start(f32[4,4096]{1,0:T(4,128)S(1)} %slice.174), channel_id=1, source_target_pairs={{0,128},{8,136},{16,144},{24,152},{32,160},{40,168},{48,176},{56,1... | collective-permute-start | bytes 196616 | tf_op jit(solution)/shard_map/ppermute | solution.py:11
  211.3 7.4 %collective-permute-done.16 = bf16[128,2048]{0,1:T(8,128)(2,1)S(1)} collective-permute-done((bf16[128,2048]{0,1:T(8,128)(2,1)}, bf16[128,2048]{0,1:T(8,128)(2,1)S(1)}, u32[]{:S(2)}, u32[]{:S(2)}) %collective-permute-start.16) | collective-permute-done | bytes 524320 | tf_op jit(solution)/shard_map/ppermute | solution.py:11
  218.6 2.4 fusion.16
  221.0 9.3 %collective-permute-done.14 = f32[4,4096]{1,0:T(4,128)S(1)} collective-permute-done((f32[4,4096]{1,0:T(4,128)S(1)}, f32[4,4096]{1,0:T(4,128)S(1)}, u32[]{:S(2)}, u32[]{:S(2)}) %collective-permute-start.14) | collective-permute-done | bytes 65568 | tf_op jit(solution)/shard_map/ppermute | solution.py:11
  230.3 4.3 %collective-permute-start.15 = (f32[2,4096]{1,0:T(2,128)S(1)}, f32[2,4096]{1,0:T(2,128)S(1)}, u32[]{:S(2)}, u32[]{:S(2)}) collective-permute-start(f32[2,4096]{1,0:T(2,128)S(1)} %slice.176), channel_id=1, source_target_pairs={{0,256},{8,264},{16,272},{24,280},{32,288},{40,296},{48,304},{56,3... | collective-permute-start | bytes 98312 | tf_op jit(solution)/shard_map/ppermute | solution.py:11
  (146 shorter events, 58.8 us)
Async XLA Ops:
  0.6 39.3 %copy-start.20 = (bf16[128,2048]{1,0:T(8,128)(2,1)S(1)}, bf16[128,2048]{1,0:T(8,128)(2,1)}, u32[]{:S(2)}) copy-start(bf16[128,2048]{1,0:T(8,128)(2,1)} %param.7) | copy-start | bytes 1572868
  0.6 19.9 %copy-start.24 = (bf16[128,2048]{1,0:T(8,128)(2,1)S(1)}, bf16[128,2048]{1,0:T(8,128)(2,1)}, u32[]{:S(2)}) copy-start(bf16[128,2048]{1,0:T(8,128)(2,1)} %param.6) | copy-start | bytes 1572868
  6.8 14.1 %collective-permute-start = (bf16[2,2,2048]{2,1,0:T(2,128)(2,1)S(1)}, bf16[2,2,2048]{2,1,0:T(2,128)(2,1)S(1)}, u32[]{:S(2)}, u32[]{:S(2)}) collective-permute-start(bf16[2,2,2048]{2,1,0:T(2,128)(2,1)S(1)} %pad_maximum_fusion.12), channel_id=1, source_target_pairs={{0,256},{8,264},{16,272},{24,280},{32,288},{40,296},{48,304},{56,3... | collective-permute-start | bytes 49160 | tf_op jit(solution)/shard_map/ppermute | solution.py:11
  17.3 22.6 %copy-start.10 = (bf16[128,2048]{0,1:T(8,128)(2,1)}, bf16[128,2048]{0,1:T(8,128)(2,1)S(1)}, u32[]{:S(2)}) copy-start(bf16[128,2048]{0,1:T(8,128)(2,1)S(1)} %copy.41) | copy-start | bytes 1572868
  18.8 21.1 %copy-start.8 = (bf16[128,2048]{0,1:T(8,128)(2,1)}, bf16[128,2048]{0,1:T(8,128)(2,1)S(1)}, u32[]{:S(2)}) copy-start(bf16[128,2048]{0,1:T(8,128)(2,1)S(1)} %copy.40) | copy-start | bytes 1572868
  20.9 91.5 %copy-start = (bf16[128,2048]{0,1:T(8,128)(2,1)}, bf16[128,2048]{0,1:T(8,128)(2,1)S(1)}, u32[]{:S(2)}) copy-start(bf16[128,2048]{0,1:T(8,128)(2,1)S(1)} %copy.99) | copy-start | bytes 1572868
  20.9 36.1 %copy-start.21 = (bf16[128,2048]{1,0:T(8,128)(2,1)S(1)}, bf16[128,2048]{1,0:T(8,128)(2,1)}, u32[]{:S(2)}) copy-start(bf16[128,2048]{1,0:T(8,128)(2,1)} %param.8) | copy-start | bytes 1572868
  21.0 7.5 %collective-permute-start.1 = (bf16[2,2,2,2048]{3,2,1,0:T(2,128)(2,1)S(1)}, bf16[2,2,2,2048]{3,2,1,0:T(2,128)(2,1)S(1)}, u32[]{:S(2)}, u32[]{:S(2)}) collective-permute-start(bf16[2,2,2,2048]{3,2,1,0:T(2,128)(2,1)S(1)} %pad_maximum_fusion.10), channel_id=1, source_target_pairs={{0,128},{8,136},{16,144},{24,152},{32,160},{40,168},{48,176},{56,1... | collective-permute-start | bytes 98312 | tf_op jit(solution)/shard_map/ppermute | solution.py:11
  28.6 6.2 %collective-permute-start.2 = (bf16[2,2,2,2,2048]{4,3,2,1,0:T(2,128)(2,1)S(1)}, bf16[2,2,2,2,2048]{4,3,2,1,0:T(2,128)(2,1)S(1)}, u32[]{:S(2)}, u32[]{:S(2)}) collective-permute-start(bf16[2,2,2,2,2048]{4,3,2,1,0:T(2,128)(2,1)S(1)} %pad_maximum_fusion.9), channel_id=1, source_target_pairs={{0,64},{8,72},{16,80},{24,88},{32,96},{40,104},{48,112},{56,120},{... | collective-permute-start | bytes 196616 | tf_op jit(solution)/shard_map/ppermute | solution.py:11
  35.0 8.4 %collective-permute-start.3 = (bf16[2,2,2,2,2,2048]{5,4,3,2,1,0:T(2,128)(2,1)S(1)}, bf16[2,2,2,2,2,2048]{5,4,3,2,1,0:T(2,128)(2,1)S(1)}, u32[]{:S(2)}, u32[]{:S(2)}) collective-permute-start(bf16[2,2,2,2,2,2048]{5,4,3,2,1,0:T(2,128)(2,1)S(1)} %pad_maximum_fusion.8), channel_id=1, source_target_pairs={{0,32},{8,40},{16,48},{24,56},{32,0},{40,8},{48,16},{56,24},{64,96... | collective-permute-start | bytes 393224 | tf_op jit(solution)/shard_map/ppermute | solution.py:11
  43.7 8.3 %collective-permute-start.4 = (bf16[2,2,2,2,2,2,2048]{6,5,4,3,2,1,0:T(2,128)(2,1)S(1)}, bf16[2,2,2,2,2,2,2048]{6,5,4,3,2,1,0:T(2,128)(2,1)S(1)}, u32[]{:S(2)}, u32[]{:S(2)}) collective-permute-start(bf16[2,2,2,2,2,2,2048]{6,5,4,3,2,1,0:T(2,128)(2,1)S(1)} %pad_maximum_fusion.7), channel_id=1, source_target_pairs={{0,16},{8,24},{16,0},{24,8},{32,48},{40,56},{48,32},{56,40},{64,80... | collective-permute-start | bytes 786440 | tf_op jit(solution)/shard_map/ppermute | solution.py:11
  53.5 12.6 %collective-permute-start.5 = (bf16[2,2,2,2,2,2,2,2048]{7,6,5,4,3,2,1,0:T(2,128)(2,1)}, bf16[2,2,2,2,2,2,2,2048]{7,6,5,4,3,2,1,0:T(2,128)(2,1)}, u32[]{:S(2)}, u32[]{:S(2)}) collective-permute-start(bf16[2,2,2,2,2,2,2,2048]{7,6,5,4,3,2,1,0:T(2,128)(2,1)} %pad_maximum_fusion.6), channel_id=1, source_target_pairs={{0,8},{8,0},{16,24},{24,16},{32,40},{40,32},{48,56},{56,48},{64,72... | collective-permute-start | bytes 1572872 | tf_op jit(solution)/shard_map/ppermute | solution.py:11
  56.8 12.7 %copy-start.2 = (bf16[128,2048]{0,1:T(8,128)(2,1)}, bf16[128,2048]{0,1:T(8,128)(2,1)S(1)}, u32[]{:S(2)}) copy-start(bf16[128,2048]{0,1:T(8,128)(2,1)S(1)} %copy.51) | copy-start | bytes 1572868
  58.5 52.5 %collective-permute-start.7 = (bf16[128,4224]{0,1:T(8,128)(2,1)}, bf16[128,4224]{0,1:T(8,128)(2,1)}, u32[]{:S(2)}, u32[]{:S(2)}) collective-permute-start(bf16[128,4224]{0,1:T(8,128)(2,1)} %pad_maximum_fusion.2), channel_id=1, source_target_pairs={{0,128},{8,136},{16,144},{24,152},{32,160},{40,168},{48,176},{56,1... | collective-permute-start | bytes 3244040 | tf_op jit(solution)/shard_map/ppermute | solution.py:11
  63.0 49.8 %collective-permute-start.6 = (bf16[128,4224]{0,1:T(8,128)(2,1)}, bf16[128,4224]{0,1:T(8,128)(2,1)}, u32[]{:S(2)}, u32[]{:S(2)}) collective-permute-start(bf16[128,4224]{0,1:T(8,128)(2,1)} %pad_maximum_fusion.2), channel_id=1, source_target_pairs={{0,8},{8,0},{16,24},{24,16},{32,40},{40,32},{48,56},{56,48},{64,72... | collective-permute-start | bytes 3244040 | tf_op jit(solution)/shard_map/ppermute | solution.py:11
  71.4 41.0 %copy-start.6 = (bf16[128,16,128]{0,2,1:T(8,128)(2,1)}, bf16[128,16,128]{0,2,1:T(8,128)(2,1)S(1)}, u32[]{:S(2)}) copy-start(bf16[128,16,128]{0,2,1:T(8,128)(2,1)S(1)} %copy.69) | copy-start | bytes 1572868
  112.8 5.7 %copy-start.26 = (s32[128]{0:T(128)S(1)}, s32[128]{0:T(128)}, u32[]{:S(2)}) copy-start(s32[128]{0:T(128)} %param.10) | copy-start | bytes 1540
  140.1 10.6 %collective-permute-start.10 = (f32[64,4096]{1,0:T(8,128)S(1)}, f32[64,4096]{1,0:T(8,128)S(1)}, u32[]{:S(2)}, u32[]{:S(2)}) collective-permute-start(f32[64,4096]{1,0:T(8,128)S(1)} %pad_maximum_fusion.3), channel_id=1, source_target_pairs={{0,8},{8,0},{16,24},{24,16},{32,40},{40,32},{48,56},{56,48},{64,72... | collective-permute-start | bytes 3145736 | tf_op jit(solution)/shard_map/ppermute | solution.py:11
  147.1 7.2 %copy-start.9 = (bf16[128,2048]{0,1:T(8,128)(2,1)S(1)}, bf16[128,2048]{0,1:T(8,128)(2,1)}, u32[]{:S(2)}) copy-start(bf16[128,2048]{0,1:T(8,128)(2,1)} %copy-done.8) | copy-start | bytes 1572868
  147.1 7.2 %copy-start.13 = (bf16[128,2048]{0,1:T(8,128)(2,1)S(1)}, bf16[128,2048]{0,1:T(8,128)(2,1)}, u32[]{:S(2)}) copy-start(bf16[128,2048]{0,1:T(8,128)(2,1)} %copy-done.12) | copy-start | bytes 1572868
  147.1 7.2 %copy-start.15 = (bf16[128,2048]{0,1:T(8,128)(2,1)S(1)}, bf16[128,2048]{0,1:T(8,128)(2,1)}, u32[]{:S(2)}) copy-start(bf16[128,2048]{0,1:T(8,128)(2,1)} %copy-done.14) | copy-start | bytes 1572868
  148.1 6.4 %copy-start.7 = (bf16[128,16,128]{0,2,1:T(8,128)(2,1)S(1)}, bf16[128,16,128]{0,2,1:T(8,128)(2,1)}, u32[]{:S(2)}) copy-start(bf16[128,16,128]{0,2,1:T(8,128)(2,1)} %copy-done.6) | copy-start | bytes 1572868
  148.1 6.4 %copy-start.23 = (bf16[16,128,128]{1,2,0:T(8,128)(2,1)S(1)}, bf16[16,128,128]{1,2,0:T(8,128)(2,1)}, u32[]{:S(2)}) copy-start(bf16[16,128,128]{1,2,0:T(8,128)(2,1)} %fusion.11) | copy-start | bytes 1572868
  148.1 40.8 %collective-permute-start.8 = (bf16[128,4096]{0,1:T(8,128)(2,1)}, bf16[128,4096]{0,1:T(8,128)(2,1)}, u32[]{:S(2)}, u32[]{:S(2)}) collective-permute-start(bf16[128,4096]{0,1:T(8,128)(2,1)} %pad_maximum_fusion.5), channel_id=1, source_target_pairs={{0,8},{8,0},{16,24},{24,16},{32,40},{40,32},{48,56},{56,48},{64,72... | collective-permute-start | bytes 3145736 | tf_op jit(solution)/shard_map/ppermute | solution.py:11
  150.9 15.7 %collective-permute-start.11 = (f32[32,4096]{1,0:T(8,128)S(1)}, f32[32,4096]{1,0:T(8,128)S(1)}, u32[]{:S(2)}, u32[]{:S(2)}) collective-permute-start(f32[32,4096]{1,0:T(8,128)S(1)} %slice.168), channel_id=1, source_target_pairs={{0,16},{8,24},{16,0},{24,8},{32,48},{40,56},{48,32},{56,40},{64,80... | collective-permute-start | bytes 1572872 | tf_op jit(solution)/shard_map/ppermute | solution.py:11
  166.7 7.3 %copy-start.22 = (f32[32,4096]{1,0:T(8,128)}, f32[32,4096]{1,0:T(8,128)S(1)}, u32[]{:S(2)}) copy-start(f32[32,4096]{1,0:T(8,128)S(1)} %slice_add_fusion.4) | copy-start | bytes 1572868
  167.4 17.4 %collective-permute-start.12 = (f32[16,4096]{1,0:T(8,128)}, f32[16,4096]{1,0:T(8,128)S(1)}, u32[]{:S(2)}, u32[]{:S(2)}) collective-permute-start(f32[16,4096]{1,0:T(8,128)} %slice.170), channel_id=1, source_target_pairs={{0,32},{8,40},{16,48},{24,56},{32,0},{40,8},{48,16},{56,24},{64,96... | collective-permute-start | bytes 786440 | tf_op jit(solution)/shard_map/ppermute | solution.py:11
  178.1 40.6 %collective-permute-start.16 = (bf16[128,2048]{0,1:T(8,128)(2,1)}, bf16[128,2048]{0,1:T(8,128)(2,1)S(1)}, u32[]{:S(2)}, u32[]{:S(2)}) collective-permute-start(bf16[128,2048]{0,1:T(8,128)(2,1)} %bitcast.175), channel_id=1, source_target_pairs={{0,128},{8,136},{16,144},{24,152},{32,160},{40,168},{48,176},{56,1... | collective-permute-start | bytes 1572872 | tf_op jit(solution)/shard_map/ppermute | solution.py:11
  180.0 54.7 %collective-permute-start.9 = (bf16[128,2048]{0,1:T(8,128)(2,1)}, bf16[128,2048]{0,1:T(8,128)(2,1)S(1)}, u32[]{:S(2)}, u32[]{:S(2)}) collective-permute-start(bf16[128,2048]{0,1:T(8,128)(2,1)} %bitcast.174), channel_id=1, source_target_pairs={{0,128},{8,136},{16,144},{24,152},{32,160},{40,168},{48,176},{56,1... | collective-permute-start | bytes 1572872 | tf_op jit(solution)/shard_map/ppermute | solution.py:11
  185.8 18.9 %collective-permute-start.13 = (f32[8,4096]{1,0:T(8,128)S(1)}, f32[8,4096]{1,0:T(8,128)S(1)}, u32[]{:S(2)}, u32[]{:S(2)}) collective-permute-start(f32[8,4096]{1,0:T(8,128)S(1)} %slice.172), channel_id=1, source_target_pairs={{0,64},{8,72},{16,80},{24,88},{32,96},{40,104},{48,112},{56,120},{... | collective-permute-start | bytes 393224 | tf_op jit(solution)/shard_map/ppermute | solution.py:11
  204.8 25.5 %collective-permute-start.14 = (f32[4,4096]{1,0:T(4,128)S(1)}, f32[4,4096]{1,0:T(4,128)S(1)}, u32[]{:S(2)}, u32[]{:S(2)}) collective-permute-start(f32[4,4096]{1,0:T(4,128)S(1)} %slice.174), channel_id=1, source_target_pairs={{0,128},{8,136},{16,144},{24,152},{32,160},{40,168},{48,176},{56,1... | collective-permute-start | bytes 196616 | tf_op jit(solution)/shard_map/ppermute | solution.py:11
  230.3 9.7 %collective-permute-start.15 = (f32[2,4096]{1,0:T(2,128)S(1)}, f32[2,4096]{1,0:T(2,128)S(1)}, u32[]{:S(2)}, u32[]{:S(2)}) collective-permute-start(f32[2,4096]{1,0:T(2,128)S(1)} %slice.176), channel_id=1, source_target_pairs={{0,256},{8,264},{16,272},{24,280},{32,288},{40,296},{48,304},{56,3... | collective-permute-start | bytes 98312 | tf_op jit(solution)/shard_map/ppermute | solution.py:11
  (12 other events, 38.2 us)

commit v8 on v6

--- a/solution.py
+++ b/solution.py
@@ -23,7 +23,16 @@
         return array.reshape(array.shape[0], HEADS, head_size)
 
     per_block = global_offsets.shape[0]
-    picked = jnp.stack([keys[global_offsets], values[global_offsets]], 0)
+    chooser = (
+        global_offsets[:, None] == jnp.arange(rows_here, dtype=global_offsets.dtype)[None, :]
+    ).astype(keys.dtype)
+    picked = jnp.stack(
+        [
+            jnp.dot(chooser, array, preferred_element_type=jnp.float32).astype(array.dtype)
+            for array in (keys, values)
+        ],
+        0,
+    )
     gather_bits = list(range(log_shards))[::-1]
     z_steps = min(3, log_shards)
     doc_columns = 128
@@ -150,7 +159,9 @@
     )
     for bit in owner_bits:
         half = owned.shape[0] // 2
-        owned = owned[:half] + from_partner(owned[half:], "seq", bit)
+        sent = owned[half:]
+        sent = sent.astype(jnp.bfloat16)
+        owned = owned[:half] + from_partner(sent, "seq", bit).astype(jnp.float32)
     owned = jnp.concatenate([temper * owned[:, :columns], owned[:, columns:]], 1)
     placement = (jnp.arange(rows_here, dtype=jnp.int32)[:, None] == global_offsets[None, :]).astype(
         jnp.float32

time: 240 us -> 232 us (0.967)
  local copies, waits for them, and re-layouts: 31.3 us -> 24.3 us
  starting transfers between devices: 68.7 us -> 66.2 us
    gather x2 -> x0, local copies, waits for them, and re-layouts: 3.36 us -> none  [body(): picked = jnp.stack([keys[global_offsets], values[global_offsets]], 0)]
    unnamed x62 -> x64, local copies, waits for them, and re-layouts: 10.6 us -> 7.74 us
    dot_general x0 -> x2, matrix products: none -> 2.64 us  [body(): jnp.dot(chooser, array, preferred_element_type=jnp.float32)]
    ppermute x17, starting transfers between devices: 68.7 us -> 66.2 us  [from_partner(): lax.ppermute(array, axis, [(i, i ^ 1 << stride) for i in range(lax.axis_s...]
  transfers between devices with their start and end apart: 17 -> 17, of which waited for: 10 -> 10; matrix products, arithmetic and copies ran while one was open for 17% -> 15% of each run, Pallas kernels for 0% -> 0%
where the time goes in v8:
time: 232 us; the launch traced here: 231 us
  waiting for transfers between devices  91.8 us (40%)
  starting transfers between devices  66.2 us (29%)
  other arithmetic  26 us (11%)
  local copies, waits for them, and re-layouts  24.3 us (10%)
  matrix products  21.4 us (9%)
    ppermute x17, waiting for transfers between devices, from_partner(): lax.ppermute(array, axis, [(i, i ^ 1 << stride) for i in range(lax.axis_s...  91.8 us
    ppermute x17, starting transfers between devices, from_partner(): lax.ppermute(array, axis, [(i, i ^ 1 << stride) for i in range(lax.axis_s...  66.2 us
    unnamed x64, local copies, waits for them, and re-layouts  7.74 us
    another operation x11, other arithmetic, body(): gathered = jnp.stack([gathered, from_partner(gathered, 'seq', bit)], 0)  7.06 us
  transfers between devices with their start and end apart: 17, of which 10 were waited for; matrix products, arithmetic and copies ran while one was open for 15% of the time, Pallas kernels for 0%

profile of v8, /device:TPU:24, one launch (start us, length us, event | category | flops | bytes accessed | tf_op | source)
XLA Modules:
  0.0 231.1 jit_solution(9122946960369549022)
XLA Ops:
  3.3 9.2 %collective-permute-start = (bf16[2,2,2048]{2,1,0:T(2,128)(2,1)S(1)}, bf16[2,2,2048]{2,1,0:T(2,128)(2,1)S(1)}, u32[]{:S(2)}, u32[]{:S(2)}) collective-permute-start(bf16[2,2,2048]{2,1,0:T(2,128)(2,1)S(1)} %pad_maximum_fusion.11), channel_id=1, source_target_pairs={{0,256},{8,264},{16,272},{24,280},{32,288},{40,296},{48,304},{56,3... | collective-permute-start | bytes 49160 | tf_op jit(solution)/shard_map/ppermute | solution.py:11
  16.7 5.2 %collective-permute-start.1 = (bf16[2,2,2,2048]{3,2,1,0:T(2,128)(2,1)S(1)}, bf16[2,2,2,2048]{3,2,1,0:T(2,128)(2,1)S(1)}, u32[]{:S(2)}, u32[]{:S(2)}) collective-permute-start(bf16[2,2,2,2048]{3,2,1,0:T(2,128)(2,1)S(1)} %pad_maximum_fusion.10), channel_id=1, source_target_pairs={{0,128},{8,136},{16,144},{24,152},{32,160},{40,168},{48,176},{56,1... | collective-permute-start | bytes 98312 | tf_op jit(solution)/shard_map/ppermute | solution.py:11
  24.2 3.5 %collective-permute-start.2 = (bf16[2,2,2,2,2048]{4,3,2,1,0:T(2,128)(2,1)S(1)}, bf16[2,2,2,2,2048]{4,3,2,1,0:T(2,128)(2,1)S(1)}, u32[]{:S(2)}, u32[]{:S(2)}) collective-permute-start(bf16[2,2,2,2,2048]{4,3,2,1,0:T(2,128)(2,1)S(1)} %pad_maximum_fusion.9), channel_id=1, source_target_pairs={{0,64},{8,72},{16,80},{24,88},{32,96},{40,104},{48,112},{56,120},{... | collective-permute-start | bytes 196616 | tf_op jit(solution)/shard_map/ppermute | solution.py:11
  27.8 2.6 %collective-permute-done.2 = bf16[2,2,2,2,2048]{4,3,2,1,0:T(2,128)(2,1)S(1)} collective-permute-done((bf16[2,2,2,2,2048]{4,3,2,1,0:T(2,128)(2,1)S(1)}, bf16[2,2,2,2,2048]{4,3,2,1,0:T(2,128)(2,1)S(1)}, u32[]{:S(2)}, u32[]{:S(2)}) %collective-permute-start.2) | collective-permute-done | bytes 65568 | tf_op jit(solution)/shard_map/ppermute | solution.py:11
  30.6 5.1 %collective-permute-start.3 = (bf16[2,2,2,2,2,2048]{5,4,3,2,1,0:T(2,128)(2,1)S(1)}, bf16[2,2,2,2,2,2048]{5,4,3,2,1,0:T(2,128)(2,1)S(1)}, u32[]{:S(2)}, u32[]{:S(2)}) collective-permute-start(bf16[2,2,2,2,2,2048]{5,4,3,2,1,0:T(2,128)(2,1)S(1)} %pad_maximum_fusion.8), channel_id=1, source_target_pairs={{0,32},{8,40},{16,48},{24,56},{32,0},{40,8},{48,16},{56,24},{64,96... | collective-permute-start | bytes 393224 | tf_op jit(solution)/shard_map/ppermute | solution.py:11
  35.9 3.1 %collective-permute-done.3 = bf16[2,2,2,2,2,2048]{5,4,3,2,1,0:T(2,128)(2,1)S(1)} collective-permute-done((bf16[2,2,2,2,2,2048]{5,4,3,2,1,0:T(2,128)(2,1)S(1)}, bf16[2,2,2,2,2,2048]{5,4,3,2,1,0:T(2,128)(2,1)S(1)}, u32[]{:S(2)}, u32[]{:S(2)}) %collective-permute-start.3) | collective-permute-done | bytes 131104 | tf_op jit(solution)/shard_map/ppermute | solution.py:11
  39.4 3.4 %collective-permute-start.4 = (bf16[2,2,2,2,2,2,2048]{6,5,4,3,2,1,0:T(2,128)(2,1)S(1)}, bf16[2,2,2,2,2,2,2048]{6,5,4,3,2,1,0:T(2,128)(2,1)S(1)}, u32[]{:S(2)}, u32[]{:S(2)}) collective-permute-start(bf16[2,2,2,2,2,2,2048]{6,5,4,3,2,1,0:T(2,128)(2,1)S(1)} %pad_maximum_fusion.7), channel_id=1, source_target_pairs={{0,16},{8,24},{16,0},{24,8},{32,48},{40,56},{48,32},{56,40},{64,80... | collective-permute-start | bytes 786440 | tf_op jit(solution)/shard_map/ppermute | solution.py:11
  44.7 3.0 %collective-permute-done.4 = bf16[2,2,2,2,2,2,2048]{6,5,4,3,2,1,0:T(2,128)(2,1)S(1)} collective-permute-done((bf16[2,2,2,2,2,2,2048]{6,5,4,3,2,1,0:T(2,128)(2,1)S(1)}, bf16[2,2,2,2,2,2,2048]{6,5,4,3,2,1,0:T(2,128)(2,1)S(1)}, u32[]{:S(2)}, u32[]{:S(2)}) %collective-permute-start.4) | collective-permute-done | bytes 262176 | tf_op jit(solution)/shard_map/ppermute | solution.py:11
  54.3 4.5 %collective-permute-start.7 = (bf16[128,4224]{0,1:T(8,128)(2,1)}, bf16[128,4224]{0,1:T(8,128)(2,1)}, u32[]{:S(2)}, u32[]{:S(2)}) collective-permute-start(bf16[128,4224]{0,1:T(8,128)(2,1)} %pad_maximum_fusion.2), channel_id=1, source_target_pairs={{0,128},{8,136},{16,144},{24,152},{32,160},{40,168},{48,176},{56,1... | collective-permute-start | bytes 3244040 | tf_op jit(solution)/shard_map/ppermute | solution.py:11
  58.7 2.3 collective-permute-start.6
  61.8 2.6 %pad_maximum_fusion.4 = bf16[2,2,2,2,2,2,2,2,2048]{8,7,6,5,4,3,2,1,0:T(2,128)(2,1)S(1)} fusion(bf16[1,2,2,2,2,2,2,2,2048]{8,7,6,5,4,3,2,1,0:T(2,128)(2,1)} %bitcast.13, bf16[1,2,2,2,2,2,2,2,2048]{8,7,6,5,4,3,2,1,0:T(2,128)(2,1)S(1)} %fusion.104), kind=kLoop, calls=%fused_computation.47 | loop fusion | flops 524288 | bytes 2097152 | tf_op jit(solution)/shard_map/stack | solution.py:46
  67.5 39.3 %collective-permute-done.7 = bf16[128,4224]{0,1:T(8,128)(2,1)} collective-permute-done((bf16[128,4224]{0,1:T(8,128)(2,1)}, bf16[128,4224]{0,1:T(8,128)(2,1)}, u32[]{:S(2)}, u32[]{:S(2)}) %collective-permute-start.7) | collective-permute-done | bytes 1081376 | tf_op jit(solution)/shard_map/ppermute | solution.py:11
  125.7 2.6 %copy.114 = f32[128,2048]{1,0:T(8,128)} copy(f32[128,2048]{0,1:T(8,128)} %bitcast.160) | data formatting | bytes 2097152 | tf_op jit(solution)/shard_map/reshape | solution.py:158
  128.3 2.5 %copy.115 = f32[128,2048]{1,0:T(8,128)} copy(f32[128,2048]{0,1:T(8,128)} %bitcast.169) | data formatting | bytes 2097152 | tf_op jit(solution)/shard_map/reshape | solution.py:158
  132.3 2.3 collective-permute-start.10
  134.6 2.9 %fusion.2 = bf16[16,128,384]{2,1,0:T(8,128)(2,1)S(1)} fusion(f32[16,128,128]{2,1,0:T(8,128)} %convolution_bitcast_fusion.3, f32[16,128,128]{2,1,0:T(8,128)S(1)} %copy-done.20, f32[16,128,128]{2,1,0:T(8,128)S(1)} %copy-done.19, f32[16,128]{1,0:T(8,128)S(1)} %bitcast.182, f32[16,128]{1,0:T(8,128)S(1)} %add.51, f32[16,128]{1,0:T(8,128)S(1)} %max.7, ...), kind=kLoop, calls=%fused_computation.4 | loop fusion | flops 8650752 | bytes 7938048 | tf_op jit(solution)/shard_map/convert_element_type | solution.py:119
  142.2 3.5 %collective-permute-start.11 = (bf16[32,4096]{1,0:T(8,128)(2,1)S(1)}, bf16[32,4096]{1,0:T(8,128)(2,1)S(1)}, u32[]{:S(2)}, u32[]{:S(2)}) collective-permute-start(bf16[32,4096]{1,0:T(8,128)(2,1)S(1)} %slice.209), channel_id=1, source_target_pairs={{0,16},{8,24},{16,0},{24,8},{32,48},{40,56},{48,32},{56,40},{64,80... | collective-permute-start | bytes 786440 | tf_op jit(solution)/shard_map/ppermute | solution.py:11
  146.0 6.9 %collective-permute-done.11 = bf16[32,4096]{1,0:T(8,128)(2,1)S(1)} collective-permute-done((bf16[32,4096]{1,0:T(8,128)(2,1)S(1)}, bf16[32,4096]{1,0:T(8,128)(2,1)S(1)}, u32[]{:S(2)}, u32[]{:S(2)}) %collective-permute-start.11) | collective-permute-done | bytes 262176 | tf_op jit(solution)/shard_map/ppermute | solution.py:11
  153.0 4.9 %collective-permute-start.12 = (bf16[16,4096]{1,0:T(8,128)(2,1)S(1)}, bf16[16,4096]{1,0:T(8,128)(2,1)S(1)}, u32[]{:S(2)}, u32[]{:S(2)}) collective-permute-start(bf16[16,4096]{1,0:T(8,128)(2,1)S(1)} %slice.210), channel_id=1, source_target_pairs={{0,32},{8,40},{16,48},{24,56},{32,0},{40,8},{48,16},{56,24},{64,96... | collective-permute-start | bytes 393224 | tf_op jit(solution)/shard_map/ppermute | solution.py:11
  158.7 2.7 %collective-permute-done.12 = bf16[16,4096]{1,0:T(8,128)(2,1)S(1)} collective-permute-done((bf16[16,4096]{1,0:T(8,128)(2,1)S(1)}, bf16[16,4096]{1,0:T(8,128)(2,1)S(1)}, u32[]{:S(2)}, u32[]{:S(2)}) %collective-permute-start.12) | collective-permute-done | bytes 131104 | tf_op jit(solution)/shard_map/ppermute | solution.py:11
  161.5 2.5 %collective-permute-start.13 = (bf16[8,4096]{1,0:T(8,128)(2,1)S(1)}, bf16[8,4096]{1,0:T(8,128)(2,1)S(1)}, u32[]{:S(2)}, u32[]{:S(2)}) collective-permute-start(bf16[8,4096]{1,0:T(8,128)(2,1)S(1)} %slice.211), channel_id=1, source_target_pairs={{0,64},{8,72},{16,80},{24,88},{32,96},{40,104},{48,112},{56,120},{... | collective-permute-start | bytes 196616 | tf_op jit(solution)/shard_map/ppermute | solution.py:11
  164.2 3.4 %collective-permute-done.13 = bf16[8,4096]{1,0:T(8,128)(2,1)S(1)} collective-permute-done((bf16[8,4096]{1,0:T(8,128)(2,1)S(1)}, bf16[8,4096]{1,0:T(8,128)(2,1)S(1)}, u32[]{:S(2)}, u32[]{:S(2)}) %collective-permute-start.13) | collective-permute-done | bytes 65568 | tf_op jit(solution)/shard_map/ppermute | solution.py:11
  167.7 3.9 %collective-permute-start.14 = (bf16[4,4096]{1,0:T(4,128)(2,1)S(1)}, bf16[4,4096]{1,0:T(4,128)(2,1)S(1)}, u32[]{:S(2)}, u32[]{:S(2)}) collective-permute-start(bf16[4,4096]{1,0:T(4,128)(2,1)S(1)} %slice.212), channel_id=1, source_target_pairs={{0,128},{8,136},{16,144},{24,152},{32,160},{40,168},{48,176},{56,1... | collective-permute-start | bytes 98312 | tf_op jit(solution)/shard_map/ppermute | solution.py:11
  174.7 2.8 %collective-permute-start.16 = (bf16[128,2048]{0,1:T(8,128)(2,1)S(1)}, bf16[128,2048]{0,1:T(8,128)(2,1)S(1)}, u32[]{:S(2)}, u32[]{:S(2)}) collective-permute-start(bf16[128,2048]{0,1:T(8,128)(2,1)S(1)} %bitcast.172), channel_id=1, source_target_pairs={{0,128},{8,136},{16,144},{24,152},{32,160},{40,168},{48,176},{56,1... | collective-permute-start | bytes 1572872 | tf_op jit(solution)/shard_map/ppermute | solution.py:11
  177.6 5.4 %collective-permute-start.15 = (bf16[2,4096]{1,0:T(2,128)(2,1)S(1)}, bf16[2,4096]{1,0:T(2,128)(2,1)S(1)}, u32[]{:S(2)}, u32[]{:S(2)}) collective-permute-start(bf16[2,4096]{1,0:T(2,128)(2,1)S(1)} %slice.213), channel_id=1, source_target_pairs={{0,256},{8,264},{16,272},{24,280},{32,288},{40,296},{48,304},{56,3... | collective-permute-start | bytes 49160 | tf_op jit(solution)/shard_map/ppermute | solution.py:11
  185.0 3.9 %collective-permute-start.9 = (bf16[128,2048]{0,1:T(8,128)(2,1)}, bf16[128,2048]{0,1:T(8,128)(2,1)}, u32[]{:S(2)}, u32[]{:S(2)}) collective-permute-start(bf16[128,2048]{0,1:T(8,128)(2,1)} %bitcast.40), channel_id=1, source_target_pairs={{0,128},{8,136},{16,144},{24,152},{32,160},{40,168},{48,176},{56,1... | collective-permute-start | bytes 1572872 | tf_op jit(solution)/shard_map/ppermute | solution.py:11
  190.8 22.5 %collective-permute-done.16 = bf16[128,2048]{0,1:T(8,128)(2,1)S(1)} collective-permute-done((bf16[128,2048]{0,1:T(8,128)(2,1)S(1)}, bf16[128,2048]{0,1:T(8,128)(2,1)S(1)}, u32[]{:S(2)}, u32[]{:S(2)}) %collective-permute-start.16) | collective-permute-done | bytes 524320 | tf_op jit(solution)/shard_map/ppermute | solution.py:11
  213.3 2.4 %fusion.18 = f32[128,16,128]{0,2,1:T(8,128)} fusion(f32[384,16,128]{0,2,1:T(8,128)} %get-tuple-element.52, bf16[128,16,128]{0,2,1:T(8,128)(2,1)S(1)} %bitcast.173, bf16[128,16,128]{0,2,1:T(8,128)(2,1)S(1)} %bitcast.166), kind=kLoop, calls=%fused_computation.40 | loop fusion | flops 1048576 | bytes 3145728 | tf_op jit(solution)/shard_map/add | solution.py:143
  217.3 6.1 %collective-permute-done.9 = bf16[128,2048]{0,1:T(8,128)(2,1)} collective-permute-done((bf16[128,2048]{0,1:T(8,128)(2,1)}, bf16[128,2048]{0,1:T(8,128)(2,1)}, u32[]{:S(2)}, u32[]{:S(2)}) %collective-permute-start.9) | collective-permute-done | bytes 524320 | tf_op jit(solution)/shard_map/ppermute | solution.py:11
  223.4 2.7 %fusion.21 = f32[128,16,128]{0,2,1:T(8,128)} fusion(f32[384,16,128]{0,2,1:T(8,128)} %get-tuple-element.54, bf16[128,16,128]{0,2,1:T(8,128)(2,1)} %bitcast.56, bf16[128,16,128]{0,2,1:T(8,128)(2,1)} %bitcast.165), kind=kLoop, calls=%fused_computation.46 | loop fusion | flops 1048576 | bytes 3145728 | tf_op jit(solution)/shard_map/add | solution.py:142
  226.1 2.6 %copy.116 = f32[128,2048]{1,0:T(8,128)} copy(f32[128,2048]{0,1:T(8,128)} %bitcast.158) | data formatting | bytes 2097152 | tf_op jit(solution)/shard_map/reshape | solution.py:172
  228.6 2.4 %fusion.17 = (bf16[128,2048]{1,0:T(8,128)(2,1)}, bf16[128,2048]{1,0:T(8,128)(2,1)}) fusion(f32[128,2048]{1,0:T(8,128)S(1)} %copy.117, f32[128,4096]{1,0:T(8,128)S(1)} %fusion.35, f32[128,2048]{1,0:T(8,128)} %copy.116), kind=kLoop, calls=%fused_computation.38 | loop fusion | flops 1048576 | bytes 5242880 | tf_op jit(solution)/shard_map/convert_element_type | solution.py:173
  (145 shorter events, 57.0 us)
Async XLA Ops:
  0.6 14.8 %copy-start.28 = (s32[128]{0:T(128)S(1)}, s32[128]{0:T(128)}, u32[]{:S(2)}) copy-start(s32[128]{0:T(128)} %param.10) | copy-start | bytes 1540
  0.6 35.0 %copy-start.24 = (bf16[128,2048]{1,0:T(8,128)(2,1)S(1)}, bf16[128,2048]{1,0:T(8,128)(2,1)}, u32[]{:S(2)}) copy-start(bf16[128,2048]{1,0:T(8,128)(2,1)} %param.6) | copy-start | bytes 1572868
  3.3 39.6 %copy-start.17 = (bf16[128,2048]{1,0:T(8,128)(2,1)S(1)}, bf16[128,2048]{1,0:T(8,128)(2,1)}, u32[]{:S(2)}) copy-start(bf16[128,2048]{1,0:T(8,128)(2,1)} %param.7) | copy-start | bytes 1572868
  3.3 13.3 %collective-permute-start = (bf16[2,2,2048]{2,1,0:T(2,128)(2,1)S(1)}, bf16[2,2,2048]{2,1,0:T(2,128)(2,1)S(1)}, u32[]{:S(2)}, u32[]{:S(2)}) collective-permute-start(bf16[2,2,2048]{2,1,0:T(2,128)(2,1)S(1)} %pad_maximum_fusion.11), channel_id=1, source_target_pairs={{0,256},{8,264},{16,272},{24,280},{32,288},{40,296},{48,304},{56,3... | collective-permute-start | bytes 49160 | tf_op jit(solution)/shard_map/ppermute | solution.py:11
  13.9 29.0 %copy-start.11 = (bf16[128,2048]{0,1:T(8,128)(2,1)}, bf16[128,2048]{0,1:T(8,128)(2,1)S(1)}, u32[]{:S(2)}) copy-start(bf16[128,2048]{0,1:T(8,128)(2,1)S(1)} %copy.80) | copy-start | bytes 1572868
  15.4 27.4 %copy-start.13 = (bf16[128,2048]{0,1:T(8,128)(2,1)}, bf16[128,2048]{0,1:T(8,128)(2,1)S(1)}, u32[]{:S(2)}) copy-start(bf16[128,2048]{0,1:T(8,128)(2,1)S(1)} %copy.79) | copy-start | bytes 1572868
  16.7 7.4 %collective-permute-start.1 = (bf16[2,2,2,2048]{3,2,1,0:T(2,128)(2,1)S(1)}, bf16[2,2,2,2048]{3,2,1,0:T(2,128)(2,1)S(1)}, u32[]{:S(2)}, u32[]{:S(2)}) collective-permute-start(bf16[2,2,2,2048]{3,2,1,0:T(2,128)(2,1)S(1)} %pad_maximum_fusion.10), channel_id=1, source_target_pairs={{0,128},{8,136},{16,144},{24,152},{32,160},{40,168},{48,176},{56,1... | collective-permute-start | bytes 98312 | tf_op jit(solution)/shard_map/ppermute | solution.py:11
  24.2 6.2 %collective-permute-start.2 = (bf16[2,2,2,2,2048]{4,3,2,1,0:T(2,128)(2,1)S(1)}, bf16[2,2,2,2,2048]{4,3,2,1,0:T(2,128)(2,1)S(1)}, u32[]{:S(2)}, u32[]{:S(2)}) collective-permute-start(bf16[2,2,2,2,2048]{4,3,2,1,0:T(2,128)(2,1)S(1)} %pad_maximum_fusion.9), channel_id=1, source_target_pairs={{0,64},{8,72},{16,80},{24,88},{32,96},{40,104},{48,112},{56,120},{... | collective-permute-start | bytes 196616 | tf_op jit(solution)/shard_map/ppermute | solution.py:11
  30.6 22.2 %copy-start.18 = (bf16[128,2048]{1,0:T(8,128)(2,1)S(1)}, bf16[128,2048]{1,0:T(8,128)(2,1)}, u32[]{:S(2)}) copy-start(bf16[128,2048]{1,0:T(8,128)(2,1)} %param.8) | copy-start | bytes 1572868
  30.6 8.5 %collective-permute-start.3 = (bf16[2,2,2,2,2,2048]{5,4,3,2,1,0:T(2,128)(2,1)S(1)}, bf16[2,2,2,2,2,2048]{5,4,3,2,1,0:T(2,128)(2,1)S(1)}, u32[]{:S(2)}, u32[]{:S(2)}) collective-permute-start(bf16[2,2,2,2,2,2048]{5,4,3,2,1,0:T(2,128)(2,1)S(1)} %pad_maximum_fusion.8), channel_id=1, source_target_pairs={{0,32},{8,40},{16,48},{24,56},{32,0},{40,8},{48,16},{56,24},{64,96... | collective-permute-start | bytes 393224 | tf_op jit(solution)/shard_map/ppermute | solution.py:11
  35.9 72.2 %copy-start = (bf16[128,2048]{0,1:T(8,128)(2,1)}, bf16[128,2048]{0,1:T(8,128)(2,1)S(1)}, u32[]{:S(2)}) copy-start(bf16[128,2048]{0,1:T(8,128)(2,1)S(1)} %copy.138) | copy-start | bytes 1572868
  39.4 8.3 %collective-permute-start.4 = (bf16[2,2,2,2,2,2,2048]{6,5,4,3,2,1,0:T(2,128)(2,1)S(1)}, bf16[2,2,2,2,2,2,2048]{6,5,4,3,2,1,0:T(2,128)(2,1)S(1)}, u32[]{:S(2)}, u32[]{:S(2)}) collective-permute-start(bf16[2,2,2,2,2,2,2048]{6,5,4,3,2,1,0:T(2,128)(2,1)S(1)} %pad_maximum_fusion.7), channel_id=1, source_target_pairs={{0,16},{8,24},{16,0},{24,8},{32,48},{40,56},{48,32},{56,40},{64,80... | collective-permute-start | bytes 786440 | tf_op jit(solution)/shard_map/ppermute | solution.py:11
  49.3 12.5 %collective-permute-start.5 = (bf16[2,2,2,2,2,2,2,2048]{7,6,5,4,3,2,1,0:T(2,128)(2,1)}, bf16[2,2,2,2,2,2,2,2048]{7,6,5,4,3,2,1,0:T(2,128)(2,1)}, u32[]{:S(2)}, u32[]{:S(2)}) collective-permute-start(bf16[2,2,2,2,2,2,2,2048]{7,6,5,4,3,2,1,0:T(2,128)(2,1)} %pad_maximum_fusion.6), channel_id=1, source_target_pairs={{0,8},{8,0},{16,24},{24,16},{32,40},{40,32},{48,56},{56,48},{64,72... | collective-permute-start | bytes 1572872 | tf_op jit(solution)/shard_map/ppermute | solution.py:11
  52.5 12.6 %copy-start.3 = (bf16[128,2048]{0,1:T(8,128)(2,1)}, bf16[128,2048]{0,1:T(8,128)(2,1)S(1)}, u32[]{:S(2)}) copy-start(bf16[128,2048]{0,1:T(8,128)(2,1)S(1)} %copy.90) | copy-start | bytes 1572868
  54.3 52.5 %collective-permute-start.7 = (bf16[128,4224]{0,1:T(8,128)(2,1)}, bf16[128,4224]{0,1:T(8,128)(2,1)}, u32[]{:S(2)}, u32[]{:S(2)}) collective-permute-start(bf16[128,4224]{0,1:T(8,128)(2,1)} %pad_maximum_fusion.2), channel_id=1, source_target_pairs={{0,128},{8,136},{16,144},{24,152},{32,160},{40,168},{48,176},{56,1... | collective-permute-start | bytes 3244040 | tf_op jit(solution)/shard_map/ppermute | solution.py:11
  58.7 49.7 %collective-permute-start.6 = (bf16[128,4224]{0,1:T(8,128)(2,1)}, bf16[128,4224]{0,1:T(8,128)(2,1)}, u32[]{:S(2)}, u32[]{:S(2)}) collective-permute-start(bf16[128,4224]{0,1:T(8,128)(2,1)} %pad_maximum_fusion.2), channel_id=1, source_target_pairs={{0,8},{8,0},{16,24},{24,16},{32,40},{40,32},{48,56},{56,48},{64,72... | collective-permute-start | bytes 3244040 | tf_op jit(solution)/shard_map/ppermute | solution.py:11
  67.1 41.0 %copy-start.15 = (bf16[128,16,128]{0,2,1:T(8,128)(2,1)}, bf16[128,16,128]{0,2,1:T(8,128)(2,1)S(1)}, u32[]{:S(2)}) copy-start(bf16[128,16,128]{0,2,1:T(8,128)(2,1)S(1)} %copy.108) | copy-start | bytes 1572868
  116.6 4.3 %copy-start.6 = (bf16[16,128,384]{2,1,0:T(8,128)(2,1)}, bf16[16,128,384]{2,1,0:T(8,128)(2,1)S(1)}, u32[]{:S(2)}) copy-start(bf16[16,128,384]{2,1,0:T(8,128)(2,1)S(1)} %fusion.24) | copy-start | bytes 4718596
  132.2 5.2 %copy-start.5 = (bf16[128,2048]{0,1:T(8,128)(2,1)S(1)}, bf16[128,2048]{0,1:T(8,128)(2,1)}, u32[]{:S(2)}) copy-start(bf16[128,2048]{0,1:T(8,128)(2,1)} %copy-done.3) | copy-start | bytes 1572868
  132.3 5.2 %copy-start.7 = (bf16[16,128,384]{2,1,0:T(8,128)(2,1)S(1)}, bf16[16,128,384]{2,1,0:T(8,128)(2,1)}, u32[]{:S(2)}) copy-start(bf16[16,128,384]{2,1,0:T(8,128)(2,1)} %copy-done.6) | copy-start | bytes 4718596
  132.3 9.7 %collective-permute-start.10 = (bf16[64,4096]{1,0:T(8,128)(2,1)S(1)}, bf16[64,4096]{1,0:T(8,128)(2,1)S(1)}, u32[]{:S(2)}, u32[]{:S(2)}) collective-permute-start(bf16[64,4096]{1,0:T(8,128)(2,1)S(1)} %fusion.20), channel_id=1, source_target_pairs={{0,8},{8,0},{16,24},{24,16},{32,40},{40,32},{48,56},{56,48},{64,72... | collective-permute-start | bytes 1572872 | tf_op jit(solution)/shard_map/ppermute | solution.py:11
  142.0 15.9 %copy-start.10 = (bf16[384,2048]{0,1:T(8,128)(2,1)S(1)}, bf16[384,2048]{0,1:T(8,128)(2,1)}, u32[]{:S(2)}) copy-start(bf16[384,2048]{0,1:T(8,128)(2,1)} %get-tuple-element.56) | copy-start | bytes 4718596
  142.2 10.7 %collective-permute-start.11 = (bf16[32,4096]{1,0:T(8,128)(2,1)S(1)}, bf16[32,4096]{1,0:T(8,128)(2,1)S(1)}, u32[]{:S(2)}, u32[]{:S(2)}) collective-permute-start(bf16[32,4096]{1,0:T(8,128)(2,1)S(1)} %slice.209), channel_id=1, source_target_pairs={{0,16},{8,24},{16,0},{24,8},{32,48},{40,56},{48,32},{56,40},{64,80... | collective-permute-start | bytes 786440 | tf_op jit(solution)/shard_map/ppermute | solution.py:11
  153.0 8.4 %collective-permute-start.12 = (bf16[16,4096]{1,0:T(8,128)(2,1)S(1)}, bf16[16,4096]{1,0:T(8,128)(2,1)S(1)}, u32[]{:S(2)}, u32[]{:S(2)}) collective-permute-start(bf16[16,4096]{1,0:T(8,128)(2,1)S(1)} %slice.210), channel_id=1, source_target_pairs={{0,32},{8,40},{16,48},{24,56},{32,0},{40,8},{48,16},{56,24},{64,96... | collective-permute-start | bytes 393224 | tf_op jit(solution)/shard_map/ppermute | solution.py:11
  158.7 13.9 %copy-start.21 = (bf16[16,128,128]{2,1,0:T(8,128)(2,1)S(1)}, bf16[16,128,128]{2,1,0:T(8,128)(2,1)}, u32[]{:S(2)}) copy-start(bf16[16,128,128]{2,1,0:T(8,128)(2,1)} %get-tuple-element.50) | copy-start | bytes 1572868
  161.5 6.2 %collective-permute-start.13 = (bf16[8,4096]{1,0:T(8,128)(2,1)S(1)}, bf16[8,4096]{1,0:T(8,128)(2,1)S(1)}, u32[]{:S(2)}, u32[]{:S(2)}) collective-permute-start(bf16[8,4096]{1,0:T(8,128)(2,1)S(1)} %slice.211), channel_id=1, source_target_pairs={{0,64},{8,72},{16,80},{24,88},{32,96},{40,104},{48,112},{56,120},{... | collective-permute-start | bytes 196616 | tf_op jit(solution)/shard_map/ppermute | solution.py:11
  167.7 9.9 %collective-permute-start.14 = (bf16[4,4096]{1,0:T(4,128)(2,1)S(1)}, bf16[4,4096]{1,0:T(4,128)(2,1)S(1)}, u32[]{:S(2)}, u32[]{:S(2)}) collective-permute-start(bf16[4,4096]{1,0:T(4,128)(2,1)S(1)} %slice.212), channel_id=1, source_target_pairs={{0,128},{8,136},{16,144},{24,152},{32,160},{40,168},{48,176},{56,1... | collective-permute-start | bytes 98312 | tf_op jit(solution)/shard_map/ppermute | solution.py:11
  171.6 17.4 %copy-start.27 = (s32[2]{0:T(128)S(1)}, s32[2]{0:T(128)}, u32[]{:S(2)}) copy-start(s32[2]{0:T(128)} %param.11) | copy-start | bytes 28
  174.7 38.6 %collective-permute-start.16 = (bf16[128,2048]{0,1:T(8,128)(2,1)S(1)}, bf16[128,2048]{0,1:T(8,128)(2,1)S(1)}, u32[]{:S(2)}, u32[]{:S(2)}) collective-permute-start(bf16[128,2048]{0,1:T(8,128)(2,1)S(1)} %bitcast.172), channel_id=1, source_target_pairs={{0,128},{8,136},{16,144},{24,152},{32,160},{40,168},{48,176},{56,1... | collective-permute-start | bytes 1572872 | tf_op jit(solution)/shard_map/ppermute | solution.py:11
  177.6 11.3 %collective-permute-start.15 = (bf16[2,4096]{1,0:T(2,128)(2,1)S(1)}, bf16[2,4096]{1,0:T(2,128)(2,1)S(1)}, u32[]{:S(2)}, u32[]{:S(2)}) collective-permute-start(bf16[2,4096]{1,0:T(2,128)(2,1)S(1)} %slice.213), channel_id=1, source_target_pairs={{0,256},{8,264},{16,272},{24,280},{32,288},{40,296},{48,304},{56,3... | collective-permute-start | bytes 49160 | tf_op jit(solution)/shard_map/ppermute | solution.py:11
  183.1 6.9 %collective-permute-start.8 = (bf16[128,4096]{0,1:T(8,128)(2,1)S(1)}, bf16[128,4096]{0,1:T(8,128)(2,1)S(1)}, u32[]{:S(2)}, u32[]{:S(2)}) collective-permute-start(bf16[128,4096]{0,1:T(8,128)(2,1)S(1)} %pad_maximum_fusion.5), channel_id=1, source_target_pairs={{0,8},{8,0},{16,24},{24,16},{32,40},{40,32},{48,56},{56,48},{64,72... | collective-permute-start | bytes 3145736 | tf_op jit(solution)/shard_map/ppermute | solution.py:11
  185.0 38.4 %collective-permute-start.9 = (bf16[128,2048]{0,1:T(8,128)(2,1)}, bf16[128,2048]{0,1:T(8,128)(2,1)}, u32[]{:S(2)}, u32[]{:S(2)}) collective-permute-start(bf16[128,2048]{0,1:T(8,128)(2,1)} %bitcast.40), channel_id=1, source_target_pairs={{0,128},{8,136},{16,144},{24,152},{32,160},{40,168},{48,176},{56,1... | collective-permute-start | bytes 1572872 | tf_op jit(solution)/shard_map/ppermute | solution.py:11
  (14 other events, 36.8 us)
